TPU v7x, 128 devices: a whole 4x4x4 slice. The times are simulated.
128 devices in a mesh: sky: 16 (over x, y), gz: 8 (over z, core).
Axes of the slice: x: 4, y: 4, z: 4, core: 2. Of those that a mesh axis runs over, the one named last changes fastest.
Arguments:
- spectra: bfloat16 [4096, 1032], P('sky', 'gz'), may hold values from -6 to 6
- kernel: bfloat16 [4096, 16], P('sky'), may hold values from 0.049804688 to 0.59765625
- owner: int32 [4096, 1], P('sky'), may hold values from 0 to 15; in each aligned block of 256 rows (0 to 255, 256 to 511, ...) at most 20 rows name the same one
- offset: int32 [4096], P('sky'), may hold values from 0 to 4095
Outputs:
- spectrum: float32 [2, 256, 256, 1032], P(None, None, ('sky', 'gz'))
Inputs may be any that keep to these rules, and one draw needn't show every extreme that they name: `owner`: in each aligned block of 256 rows no sky index is named by more than 20 rows, a bound that some block reaches.
All inputs are finite; a program needn't handle non-finite values.
Results may differ from a plain program's by a relative error of at most 0.0063.
Values may be sent and summed in bfloat16 or wider, within the bound.
No kernel may reach another device: no remote copies, remote signals or barrier semaphores. Data moves between devices by JAX's collectives and lax.ppermute only.
A program may use at most 64 MiB of HBM per device.

v0:
```python
import math

import jax
import jax.numpy as jnp
from jax import lax
from jax.sharding import PartitionSpec as P

NX = 256
NY = 256
NW = 1032
KSIDE = 4


def dft_tables(length):
    steps = jnp.arange(length, dtype=jnp.int32)
    phase = steps[:, None] * steps[None, :] % length
    angles = phase.astype(jnp.float32) * (2.0 * math.pi / length)
    factor = 1.0 / math.sqrt(length)
    return (
        (jnp.cos(angles) * factor).astype(jnp.bfloat16),
        (jnp.sin(angles) * factor).astype(jnp.bfloat16),
    )


def twiddles(length, fine_count=16):
    coarse_count = -(-length // fine_count)
    steps = jnp.arange(length, dtype=jnp.int32)
    angle = 2.0 * math.pi / length
    coarse = (jnp.arange(coarse_count, dtype=jnp.int32)[:, None] * fine_count * steps[None, :]) % length
    fine = (jnp.arange(fine_count, dtype=jnp.int32)[:, None] * steps[None, :]) % length
    cos_c = jnp.cos(coarse.astype(jnp.float32) * angle)[:, None, :]
    sin_c = jnp.sin(coarse.astype(jnp.float32) * angle)[:, None, :]
    cos_f = jnp.cos(fine.astype(jnp.float32) * angle)[None, :, :]
    sin_f = jnp.sin(fine.astype(jnp.float32) * angle)[None, :, :]
    rows = coarse_count * fine_count
    cos_t = (cos_c * cos_f - sin_c * sin_f).reshape(rows, length)[:length]
    sin_t = (sin_c * cos_f + cos_c * sin_f).reshape(rows, length)[:length]
    factor = 1.0 / math.sqrt(length)
    return (cos_t * factor).astype(jnp.bfloat16), (sin_t * factor).astype(jnp.bfloat16)


def complex_table(length):
    cos_t, sin_t = dft_tables(length)
    top = jnp.concatenate([cos_t, -sin_t], axis=1)
    bottom = jnp.concatenate([sin_t, cos_t], axis=1)
    return jnp.concatenate([top, bottom], axis=0)


def route_fibres(spectra, kernel, owner, offset, sky_count):
    fibre_count = spectra.shape[0]
    capacity = fibre_count * 5 // (4 * sky_count)
    block = 2 * capacity
    slots_all = sky_count * block
    target = owner[:, 0]
    order = jnp.arange(fibre_count, dtype=jnp.int32)
    same = (target[:, None] == target[None, :]) & (order[None, :] < order[:, None])
    before = jnp.sum(same.astype(jnp.int32), axis=1)
    first_slot = target * block + before
    second_slot = ((target + 1) % sky_count) * block + capacity + before
    slot_ids = jnp.arange(slots_all, dtype=jnp.int32)
    pick = (
        (slot_ids[:, None] == first_slot[None, :]) | (slot_ids[:, None] == second_slot[None, :])
    ).astype(jnp.bfloat16)
    row = (offset // NY).astype(jnp.bfloat16)[:, None]
    col = (offset % NY).astype(jnp.bfloat16)[:, None]
    packed = jnp.concatenate([spectra, kernel, row, col], axis=1)
    send = jnp.dot(pick, packed, preferred_element_type=jnp.float32).astype(jnp.bfloat16)
    send = send.reshape(sky_count, block * packed.shape[1])
    got = lax.all_to_all(send, "sky", split_axis=0, concat_axis=0, tiled=True)
    return got.reshape(slots_all, packed.shape[1]), capacity, block


def grid_tile(got, slab_width, taps, tile_rows, capacity, block):
    slots_all = got.shape[0]
    values = got[:, :slab_width]
    weights = got[:, slab_width : slab_width + taps].astype(jnp.float32)
    slot_ids = jnp.arange(slots_all, dtype=jnp.int32)
    shift = jnp.where(slot_ids % block >= capacity, tile_rows, 0)
    corner_row = got[:, slab_width + taps].astype(jnp.int32) - shift
    corner_col = got[:, slab_width + taps + 1].astype(jnp.int32)
    rows = jnp.arange(tile_rows, dtype=jnp.int32)
    columns = jnp.arange(NY, dtype=jnp.int32)
    spread = jnp.zeros((slots_all, tile_rows, NY), jnp.float32)
    for step_a in range(KSIDE):
        active = rows[None, :] == (corner_row + step_a)[:, None]
        line = jnp.zeros((slots_all, NY), jnp.float32)
        for step_b in range(KSIDE):
            placed = columns[None, :] == ((corner_col + step_b) % NY)[:, None]
            line = line + jnp.where(placed, weights[:, step_a * KSIDE + step_b][:, None], 0.0)
        spread = spread + jnp.where(active[:, :, None], line[:, None, :], 0.0)
    spread_bf = spread.astype(jnp.bfloat16).reshape(slots_all, tile_rows * NY)
    cube_t = lax.dot_general(
        values, spread_bf, (((0,), (0,)), ((), ())), preferred_element_type=jnp.float32
    )
    return cube_t.astype(jnp.bfloat16)


def shards(spectra, kernel, owner, offset):
    sky_count = lax.axis_size("sky")
    gz_count = lax.axis_size("gz")
    devices = sky_count * gz_count
    slab_width = spectra.shape[1]
    taps = kernel.shape[1]
    tile_rows = NX // sky_count
    per_dev = NY // devices

    got, capacity, block = route_fibres(spectra, kernel, owner, offset, sky_count)
    cube_t = grid_tile(got, slab_width, taps, tile_rows, capacity, block)
    cube_w = lax.all_to_all(cube_t, "gz", split_axis=1, concat_axis=0, tiled=True)
    rows_dev = tile_rows // gz_count
    cube_w = cube_w.reshape(NW, rows_dev, NY)

    cos_y, sin_y = dft_tables(NY)
    table_y = jnp.concatenate([cos_y, -sin_y], axis=1)
    cos_w, sin_w = twiddles(NW)
    table_x = complex_table(NX).reshape(2, devices, rows_dev, 2, NX)
    table_y, cos_w, sin_w, table_x = lax.optimization_barrier((table_y, cos_w, sin_w, table_x))

    first = jnp.einsum("wxy,yK->wxK", cube_w, table_y, preferred_element_type=jnp.float32)
    first = first.astype(jnp.bfloat16).reshape(NW, rows_dev, 2, NY)
    by_cos = jnp.einsum("wxrk,wv->rkxv", first, cos_w, preferred_element_type=jnp.float32)
    by_sin = jnp.einsum("wxrk,wv->rkxv", first, sin_w, preferred_element_type=jnp.float32)
    second = jnp.stack([by_cos[0] + by_sin[1], by_cos[1] - by_sin[0]], axis=2)
    second = second.astype(jnp.bfloat16).reshape(devices, per_dev * rows_dev * 2, NW)
    pencils = lax.all_to_all(second, ("sky", "gz"), split_axis=0, concat_axis=0, tiled=True)
    pencils = pencils.reshape(devices, per_dev, rows_dev, 2, NW)
    return jnp.einsum("sqxRv,RsxUu->Uuqv", pencils, table_x, preferred_element_type=jnp.float32)


def solution(mesh):
    in_specs = (P("sky", "gz"), P("sky", None), P("sky", None), P("sky"))
    out_specs = P(None, None, ("sky", "gz"), None)
    return jax.shard_map(shards, mesh=mesh, in_specs=in_specs, out_specs=out_specs, check_vma=False)
```

profile of v0, /device:TPU:1, one launch (start us, length us, event | category | flops | bytes accessed | tf_op | source)
XLA Modules:
  0.0 137.2 jit_solution(3747097964526952714)
XLA Ops:
  0.0 0.9 convert_reduce_fusion
  0.9 0.7 multiply_add_fusion.1
  1.6 0.7 fusion.70
  2.3 1.2 convolution_convert_fusion.2
  3.5 0.2 copy.39
  3.7 0.5 all_to_all.27
  4.2 0.5 broadcast.792
  4.7 1.8 %reduce.49 = bf16[16,5880]{1,0:T(8,128)(2,1)S(1)} reduce(bf16[16,1,5880]{2,1,0:T(2,128)(2,1)S(1)} %all_to_all.27, bf16[]{:T(256)} %broadcast.792), dimensions={1}, to_apply=%all_to_all.27.reduce_sub_computation | reduce | bytes 376322 | tf_op jit(solution)/shard_map/all_to_all | solution.py:69
  6.5 0.9 reshape.849
  7.4 7.6 %all-to-all-start = ((bf16[16,2,2940]{2,1,0:T(2,128)(2,1)}), bf16[16,2,2940]{2,1,0:T(2,128)(2,1)S(1)}, u32[]{:S(2)}, u32[]{:S(2)}) async-start(bf16[16,2,2940]{2,1,0:T(2,128)(2,1)} %reshape.849), calls=%async_computation | async-start | bytes 376832 | tf_op jit(solution)/shard_map/all_to_all | solution.py:69
  15.0 0.3 fusion.61
  15.3 1.3 multiply_convert_fusion
  16.6 1.0 fusion.64
  17.6 1.4 %fusion.24 = (f32[65,1032]{1,0:T(8,128)S(1)}, f32[65,1032]{1,0:T(8,128)S(1)}) fusion(s32[65]{0:T(128)S(1)} %iota_multiply_fusion), kind=kLoop, calls=%fused_computation.72 | loop fusion | flops 603720 | bytes 536900 | tf_op jit(solution)/shard_map/cos | solution.py:31
  19.0 3.1 %multiply_add_fusion = (f32[65,16,1032]{2,1,0:T(8,128)S(1)}, f32[65,16,1032]{2,1,0:T(8,128)}) fusion(f32[16,1032]{1,0:T(8,128)S(1)} %get-tuple-element.48, f32[65,1032]{1,0:T(8,128)S(1)} %get-tuple-element.47, f32[16,1032]{1,0:T(8,128)S(1)} %get-tuple-element.49, f32[65,1032]{1,0:T(8,128)S(1)} %get-tuple-element.46), kind=kLoop, calls=%fused_computation.2 | loop fusion | flops 6439680 | bytes 9254976 | tf_op jit(solution)/shard_map/add | solution.py:37
  22.1 1.9 %fusion = bf16[1032,1032]{1,0:T(8,128)(2,1)} fusion(f32[1040,1032]{1,0:T(8,128)S(1)} %bitcast.63), kind=kLoop, calls=%fused_computation.5 | loop fusion | flops 2130048 | bytes 6390144 | tf_op jit(solution)/shard_map/convert_element_type | solution.py:39
  24.1 0.1 reshape.813
  24.2 0.0 all-to-all-done
  24.2 0.3 reshape.850
  24.5 1.1 reduce
  25.6 0.5 reshape.814
  26.1 0.1 slice_convert_fusion
  26.2 1.1 fusion.38
  27.3 2.7 %slice_reduce_fusion.15 = (f32[640]{0:T(1024)S(1)}, f32[640]{0:T(1024)S(1)}, f32[640]{0:T(1024)S(1)}, f32[640]{0:T(1024)S(1)}, f32[640]{0:T(1024)S(1)}, /*index=...) fusion(f32[640,16]{1,0:T(8,128)S(1)} %slice_convert_fusion), kind=kLoop, calls=%fused_computation.98 | loop fusion | bytes 81920 | tf_op jit(solution)/shard_map/slice | solution.py:89
  30.0 0.2 iota_compare_fusion.7
  30.2 0.2 iota_compare_fusion.9
  30.5 0.7 select_add_fusion.2
  31.2 1.6 %select_add_fusion.3 = (f32[640,256]{1,0:T(8,128)S(1)}, f32[640,256]{1,0:T(8,128)S(1)}, f32[640,256]{1,0:T(8,128)S(1)}) fusion(f32[640]{0:T(1024)S(1)} %get-tuple-element.34, s32[640]{0:T(1024)S(1)} %get-tuple-element.17, f32[640]{0:T(1024)S(1)} %get-tuple-element.35, s32[640]{0:T(1024)S(1)} %get-tuple-element.18, f32[640]{0:T(1024)S(1)} %get-tuple-element.36, ...), kind=kLoop, calls=%fused_computation.40 | loop fusion | flops 4096000 | bytes 2007040 | tf_op jit(solution)/shard_map/add | solution.py:89
  32.9 7.1 %add_convert_fusion = bf16[640,16,256]{2,1,0:T(8,128)(2,1)S(1)} fusion(f32[640,256]{1,0:T(8,128)S(1)} %get-tuple-element.40, f32[640,256]{1,0:T(8,128)S(1)} %get-tuple-element.41, f32[640,256]{1,0:T(8,128)S(1)} %select_add_fusion.2, f32[640,256]{1,0:T(8,128)S(1)} %get-tuple-element.39, pred[640,16]{1,0:T(8,128)(4,1)S(1)} %get-tuple-element.52, ...), kind=kLoop, calls=%fused_computation | loop fusion | flops 20971520 | bytes 7905280 | tf_op jit(solution)/shard_map/convert.4
  39.9 3.5 %copy.69 = bf16[80,8,16,256]{3,1,2,0:T(8,128)(2,1)S(1)} copy(bf16[80,8,16,256]{3,2,1,0:T(8,128)(2,1)S(1)} %bitcast.60) | data formatting | bytes 10485760
  43.4 1.1 convolution_convert_fusion
  44.5 0.4 copy.70
  44.9 0.1 slice.130
  45.0 1.3 copy.41
  46.4 6.3 %all-to-all-start.1 = ((bf16[129,8,512]{2,0,1:T(8,128)(2,1)}), bf16[129,8,512]{2,0,1:T(8,128)(2,1)S(1)}, u32[]{:S(2)}, u32[]{:S(2)}) async-start(bf16[129,8,512]{2,0,1:T(8,128)(2,1)} %copy.41), calls=%async_computation.1 | async-start | bytes 2228224 | tf_op jit(solution)/shard_map/all_to_all | solution.py:109
  52.6 4.2 %fusion.1 = bf16[1032,1032]{1,0:T(8,128)(2,1)} fusion(f32[1040,1032]{1,0:T(8,128)} %bitcast.62), kind=kLoop, calls=%fused_computation.7 | loop fusion | flops 2130048 | bytes 6390144 | tf_op jit(solution)/shard_map/convert_element_type | solution.py:39
  56.8 11.4 %all-to-all-done.1 = bf16[129,8,512]{2,0,1:T(8,128)(2,1)S(1)} async-done(((bf16[129,8,512]{2,0,1:T(8,128)(2,1)}), bf16[129,8,512]{2,0,1:T(8,128)(2,1)S(1)}, u32[]{:S(2)}, u32[]{:S(2)}) %all-to-all-start.1) | async-done | bytes 1056800 | tf_op jit(solution)/shard_map/all_to_all | solution.py:109
  68.3 0.5 reshape.815
  68.8 0.0 copy-start.1
  68.8 0.7 convolution_convert_fusion.1
  69.5 0.9 copy-done.1
  70.5 0.0 copy-start
  70.5 3.0 %convolution_bitcast_fusion.2 = f32[2,256,2,1032]{1,3,0,2:T(8,128)S(1)} fusion(bf16[1032,1032]{1,0:T(8,128)(2,1)S(1)} %copy-done.1, bf16[2,129,2,8,256]{4,3,2,1,0:T(8,128)(2,1)S(1)} %bitcast.68), kind=kOutput, calls=%fused_computation.10 | convolution fusion | flops 2181169152 | bytes 8470656 | tf_op jit(solution)/shard_map/wxrk,wv->rkxv/dot_general | solution.py:121
  73.5 0.0 copy-done
  73.5 3.0 %convolution_bitcast_fusion.1 = f32[2,256,2,1032]{1,3,2,0:T(8,128)S(1)} fusion(bf16[1032,1032]{1,0:T(8,128)(2,1)S(1)} %copy-done, bf16[2,129,2,8,256]{4,3,2,1,0:T(8,128)(2,1)S(1)} %bitcast.69), kind=kOutput, calls=%fused_computation.9 | convolution fusion | flops 2181169152 | bytes 8470656 | tf_op jit(solution)/shard_map/wxrk,wv->rkxv/dot_general | solution.py:122
  76.5 0.4 fusion.13
  76.9 0.4 fusion.14
  77.4 1.5 %pad_maximum_fusion = bf16[256,2,2,1032]{0,3,1,2:T(8,128)(2,1)} fusion(bf16[256,2,1,1032]{0,3,1,2:T(8,128)(2,1)S(1)} %fusion.14, bf16[256,2,1,1032]{0,3,1,2:T(8,128)(2,1)S(1)} %fusion.13), kind=kLoop, calls=%fused_computation.24 | loop fusion | flops 1056768 | bytes 4227072 | tf_op jit(solution)/shard_map/stack | solution.py:123
  78.9 6.3 %copy.50 = bf16[256,2,2,1032]{3,2,1,0:T(2,128)(2,1)S(1)} copy(bf16[256,2,2,1032]{0,3,1,2:T(8,128)(2,1)} %pad_maximum_fusion) | data formatting | bytes 4227072 | tf_op jit(solution)/shard_map/stack | solution.py:123
  85.2 3.0 %convert_element_type.113 = bf16[128,8,1032]{2,1,0:T(8,128)(2,1)} reshape(bf16[256,2,2,1032]{3,2,1,0:T(2,128)(2,1)S(1)} %copy.50) | data formatting | bytes 4227072 | tf_op jit(solution)/shard_map/convert_element_type | solution.py:124
  88.2 41.5 %all_to_all.31 = bf16[128,8,1032]{2,1,0:T(8,128)(2,1)S(1)} all-to-all(bf16[128,8,1032]{2,1,0:T(8,128)(2,1)} %convert_element_type.113), channel_id=1, replica_groups=mesh['sky'=16,'gz'=8] {'sky','gz'}, dimensions={0} | all-to-all | bytes 4227072 | tf_op jit(solution)/shard_map/all_to_all | solution.py:125
  129.7 2.7 %copy.51 = bf16[128,8,1032]{0,2,1:T(8,128)(2,1)} copy(bf16[128,8,1032]{2,1,0:T(8,128)(2,1)S(1)} %all_to_all.31) | data formatting | bytes 4227072 | tf_op jit(solution)/shard_map/all_to_all | solution.py:125
  132.4 4.9 %convolution_bitcast_fusion = f32[2,256,2,1032]{1,3,2,0:T(8,128)} fusion(bf16[128,2,2,2,1032]{0,4,3,2,1:T(8,128)(2,1)} %bitcast.64, bf16[2,128,2,2,256,1]{4,3,2,1,0,5:T(2,128)(2,1)S(1)} %bitcast.70), kind=kOutput, calls=%fused_computation.8 | convolution fusion | flops 1082130432 | bytes 6864896 | tf_op jit(solution)/shard_map/sqxRv,RsxUu->Uuqv/dot_general | solution.py:127
  (5 shorter events, 0.1 us)
Async XLA Ops:
  7.4 16.9 %all-to-all-start = ((bf16[16,2,2940]{2,1,0:T(2,128)(2,1)}), bf16[16,2,2940]{2,1,0:T(2,128)(2,1)S(1)}, u32[]{:S(2)}, u32[]{:S(2)}) async-start(bf16[16,2,2940]{2,1,0:T(2,128)(2,1)} %reshape.849), calls=%async_computation | async-start | bytes 376832 | tf_op jit(solution)/shard_map/all_to_all | solution.py:69
  46.4 21.9 %all-to-all-start.1 = ((bf16[129,8,512]{2,0,1:T(8,128)(2,1)}), bf16[129,8,512]{2,0,1:T(8,128)(2,1)S(1)}, u32[]{:S(2)}, u32[]{:S(2)}) async-start(bf16[129,8,512]{2,0,1:T(8,128)(2,1)} %copy.41), calls=%async_computation.1 | async-start | bytes 2228224 | tf_op jit(solution)/shard_map/all_to_all | solution.py:109
  68.8 1.7 %copy-start.1 = (bf16[1032,1032]{1,0:T(8,128)(2,1)S(1)}, bf16[1032,1032]{1,0:T(8,128)(2,1)}, u32[]{:S(2)}) copy-start(bf16[1032,1032]{1,0:T(8,128)(2,1)} %fusion.1) | copy-start | bytes 6390148
  70.5 3.0 %copy-start = (bf16[1032,1032]{1,0:T(8,128)(2,1)S(1)}, bf16[1032,1032]{1,0:T(8,128)(2,1)}, u32[]{:S(2)}) copy-start(bf16[1032,1032]{1,0:T(8,128)(2,1)} %fusion) | copy-start | bytes 6390148
where the time goes:
time: 138 us; the launch traced here: 137 us
  blocking collectives  41.5 us (30%)
  other arithmetic  32 us (23%)
  local copies, waits for them, and re-layouts  24.3 us (18%)
  matrix products  13.9 us (10%)
  starting transfers between devices  13.8 us (10%)
  waiting for transfers between devices  11.4 us (8%)
    all_to_all x1, blocking collectives, shards(): lax.all_to_all(second, ('sky', 'gz'), split_axis=0, concat_axis=0, tiled=...  41.5 us
    all_to_all x1, waiting for transfers between devices, shards(): lax.all_to_all(cube_t, 'gz', split_axis=1, concat_axis=0, tiled=True)  11.4 us
    all_to_all x1, starting transfers between devices, route_fibres(): got = lax.all_to_all(send, 'sky', split_axis=0, concat_axis=0, tiled=True)  7.57 us
    another operation x1, other arithmetic  7.08 us
    another operation x1, local copies, waits for them, and re-layouts, shards(): second = jnp.stack([by_cos[0] + by_sin[1], by_cos[1] - by_sin[0]], axis=2)  6.27 us
    all_to_all x1, starting transfers between devices, shards(): lax.all_to_all(cube_t, 'gz', split_axis=1, concat_axis=0, tiled=True)  6.26 us
    unnamed x8, local copies, waits for them, and re-layouts  6 us
    dot_general x1, matrix products, shards(): jnp.einsum('sqxRv,RsxUu->Uuqv', pencils, table_x, preferred_element_type=...  4.87 us
  transfers between devices with their start and end apart: 2, of which 1 were waited for; matrix products, arithmetic and copies ran while one was open for 10% of the time, Pallas kernels for 0%

commit v1 on v0

--- a/solution.py
+++ b/solution.py
@@ -111,16 +111,20 @@
     cube_w = cube_w.reshape(NW, rows_dev, NY)
 
     cos_y, sin_y = dft_tables(NY)
-    table_y = jnp.concatenate([cos_y, -sin_y], axis=1)
-    cos_w, sin_w = twiddles(NW)
+    table_y = lax.optimization_barrier(jnp.concatenate([cos_y, -sin_y], axis=1))
+    cos_w, sin_w = lax.optimization_barrier(twiddles(NW))
     table_x = complex_table(NX).reshape(2, devices, rows_dev, 2, NX)
-    table_y, cos_w, sin_w, table_x = lax.optimization_barrier((table_y, cos_w, sin_w, table_x))
+    table_x = lax.optimization_barrier(table_x)
 
-    first = jnp.einsum("wxy,yK->wxK", cube_w, table_y, preferred_element_type=jnp.float32)
-    first = first.astype(jnp.bfloat16).reshape(NW, rows_dev, 2, NY)
-    by_cos = jnp.einsum("wxrk,wv->rkxv", first, cos_w, preferred_element_type=jnp.float32)
-    by_sin = jnp.einsum("wxrk,wv->rkxv", first, sin_w, preferred_element_type=jnp.float32)
-    second = jnp.stack([by_cos[0] + by_sin[1], by_cos[1] - by_sin[0]], axis=2)
+    first = jnp.einsum(
+        "wxy,yrk->kxrw", cube_w, table_y.reshape(NY, 2, NY), preferred_element_type=jnp.float32
+    ).astype(jnp.bfloat16)
+    swapped = jnp.stack([first[:, :, 1], -first[:, :, 0]], axis=2)
+    first_t = first.reshape(NY * rows_dev * 2, NW)
+    swapped = swapped.reshape(NY * rows_dev * 2, NW)
+    second = jnp.dot(first_t, cos_w, preferred_element_type=jnp.float32) + jnp.dot(
+        swapped, sin_w, preferred_element_type=jnp.float32
+    )
     second = second.astype(jnp.bfloat16).reshape(devices, per_dev * rows_dev * 2, NW)
     pencils = lax.all_to_all(second, ("sky", "gz"), split_axis=0, concat_axis=0, tiled=True)
     pencils = pencils.reshape(devices, per_dev, rows_dev, 2, NW)

time: 138 us -> 155 us (1.12)
  blocking collectives: 41.5 us -> 0 us
  waiting for transfers between devices: 11.4 us -> 44.3 us
  local copies, waits for them, and re-layouts: 24.3 us -> 36.9 us
  starting transfers between devices: 13.8 us -> 22.1 us
  matrix products: 13.9 us -> 17.6 us
    all_to_all x1 -> x0, blocking collectives: 41.5 us -> none  [shards(): lax.all_to_all(second, ('sky', 'gz'), split_axis=0, concat_axis=0, tiled=...]
    all_to_all x0 -> x1, waiting for transfers between devices: none -> 32.8 us  [shards(): lax.all_to_all(second, ('sky', 'gz'), split_axis=0, concat_axis=0, tiled=...]
    reshape x0 -> x2, local copies, waits for them, and re-layouts: none -> 9.18 us  [the longest x1 6.17 us: shards(): first_t = first.reshape(NY * rows_dev * 2, NW)]
    all_to_all x0 -> x1, starting transfers between devices: none -> 8.27 us  [shards(): lax.all_to_all(second, ('sky', 'gz'), split_axis=0, concat_axis=0, tiled=...]
    convert_element_type x0 -> x1, local copies, waits for them, and re-layouts: none -> 4.67 us  [shards(): first = jnp.einsum('wxy,yrk->kxrw', cube_w, table_y.reshape(NY, 2, NY), p...]
    dot_general x3, matrix products: 6.78 us -> 10.5 us  [the longest x1 5.54 us: shards(): jnp.dot(first_t, cos_w, preferred_element_type=jnp.float32)]
    convert_element_type x1, other arithmetic: 4.22 us -> 1.9 us  [twiddles(): (cos_t * factor).astype(jnp.bfloat16)]
    convert_element_type x1, other arithmetic: 1.9 us -> 4.22 us  [twiddles(): (sin_t * factor).astype(jnp.bfloat16)]
  transfers between devices with their start and end apart: 2 -> 3, of which waited for: 1 -> 2; matrix products, arithmetic and copies ran while one was open for 10% -> 10% of each run, Pallas kernels for 0% -> 0%
where the time goes in v1:
time: 155 us
  waiting for transfers between devices  44.3 us (29%)
  local copies, waits for them, and re-layouts  36.9 us (24%)
  other arithmetic  33.4 us (22%)
  starting transfers between devices  22.1 us (14%)
  matrix products  17.6 us (11%)
    all_to_all x1, waiting for transfers between devices, shards(): lax.all_to_all(second, ('sky', 'gz'), split_axis=0, concat_axis=0, tiled=...  32.8 us
    all_to_all x1, waiting for transfers between devices, shards(): lax.all_to_all(cube_t, 'gz', split_axis=1, concat_axis=0, tiled=True)  11.4 us
    all_to_all x1, starting transfers between devices, shards(): lax.all_to_all(second, ('sky', 'gz'), split_axis=0, concat_axis=0, tiled=...  8.27 us
    all_to_all x1, starting transfers between devices, route_fibres(): got = lax.all_to_all(send, 'sky', split_axis=0, concat_axis=0, tiled=True)  7.57 us
    another operation x1, other arithmetic  7.08 us
    another operation x1, local copies, waits for them, and re-layouts, shards(): swapped = jnp.stack([first[:, :, 1], -first[:, :, 0]], axis=2)  6.27 us
    all_to_all x1, starting transfers between devices, shards(): lax.all_to_all(cube_t, 'gz', split_axis=1, concat_axis=0, tiled=True)  6.26 us
    reshape x1, local copies, waits for them, and re-layouts, shards(): first_t = first.reshape(NY * rows_dev * 2, NW)  6.17 us
  transfers between devices with their start and end apart: 3, of which 2 were waited for; matrix products, arithmetic and copies ran while one was open for 10% of the time, Pallas kernels for 0%

profile of v1, /device:TPU:1, one launch (start us, length us, event | category | flops | bytes accessed | tf_op | source)
XLA Modules:
  0.0 154.6 jit_solution(17443267335921088584)
XLA Ops:
  0.0 0.9 convert_reduce_fusion
  0.9 0.7 multiply_add_fusion.1
  1.6 0.7 fusion.61
  2.3 1.2 convolution_convert_fusion.2
  3.5 0.2 copy.29
  3.7 0.5 all_to_all.27
  4.2 0.5 broadcast.792
  4.7 1.8 %reduce.49 = bf16[16,5880]{1,0:T(8,128)(2,1)S(1)} reduce(bf16[16,1,5880]{2,1,0:T(2,128)(2,1)S(1)} %all_to_all.27, bf16[]{:T(256)} %broadcast.792), dimensions={1}, to_apply=%all_to_all.27.reduce_sub_computation | reduce | bytes 376322 | tf_op jit(solution)/shard_map/all_to_all | solution.py:69
  6.5 0.9 reshape.819
  7.4 7.6 %all-to-all-start = ((bf16[16,2,2940]{2,1,0:T(2,128)(2,1)}), bf16[16,2,2940]{2,1,0:T(2,128)(2,1)S(1)}, u32[]{:S(2)}, u32[]{:S(2)}) async-start(bf16[16,2,2940]{2,1,0:T(2,128)(2,1)} %reshape.819), calls=%async_computation | async-start | bytes 376832 | tf_op jit(solution)/shard_map/all_to_all | solution.py:69
  15.0 1.7 %multiply_convert_fusion = (bf16[256,256]{0,1:T(8,128)(2,1)}, bf16[256,256]{0,1:T(8,128)(2,1)S(1)}) fusion(), kind=kLoop, calls=%fused_computation.110 | loop fusion | flops 1179648 | bytes 262144 | tf_op jit(solution)/shard_map/convert_element_type | solution.py:21
  16.7 0.3 fusion.52
  17.0 1.4 fusion.16
  18.4 3.1 %multiply_add_fusion = (f32[65,16,1032]{2,1,0:T(8,128)}, f32[65,16,1032]{2,1,0:T(8,128)S(1)}) fusion(f32[16,1032]{1,0:T(8,128)S(1)} %get-tuple-element.50, f32[65,1032]{1,0:T(8,128)S(1)} %get-tuple-element.45, f32[16,1032]{1,0:T(8,128)S(1)} %get-tuple-element.51, f32[65,1032]{1,0:T(8,128)S(1)} %get-tuple-element.44), kind=kLoop, calls=%fused_computation.2 | loop fusion | flops 6439680 | bytes 9254976 | tf_op jit(solution)/shard_map/add | solution.py:37
  21.6 1.9 %fusion.1 = bf16[1032,1032]{1,0:T(8,128)(2,1)} fusion(f32[1040,1032]{1,0:T(8,128)S(1)} %bitcast.38), kind=kLoop, calls=%fused_computation.7 | loop fusion | flops 2130048 | bytes 6390144 | tf_op jit(solution)/shard_map/convert_element_type | solution.py:39
  23.5 1.0 fusion.55
  24.5 0.8 pad_maximum_fusion.1
  25.2 0.0 all-to-all-done
  25.2 0.3 reshape.820
  25.5 1.1 reduce
  26.6 0.5 reshape.783
  27.1 0.1 slice_convert_fusion
  27.2 1.1 fusion.30
  28.3 2.7 %slice_reduce_fusion.15 = (f32[640]{0:T(1024)S(1)}, f32[640]{0:T(1024)S(1)}, f32[640]{0:T(1024)S(1)}, f32[640]{0:T(1024)S(1)}, f32[640]{0:T(1024)S(1)}, /*index=...) fusion(f32[640,16]{1,0:T(8,128)S(1)} %slice_convert_fusion), kind=kLoop, calls=%fused_computation.87 | loop fusion | bytes 81920 | tf_op jit(solution)/shard_map/slice | solution.py:89
  31.0 0.2 iota_compare_fusion.7
  31.2 0.2 iota_compare_fusion.9
  31.5 0.7 select_add_fusion.2
  32.2 1.6 %select_add_fusion.3 = (f32[640,256]{1,0:T(8,128)S(1)}, f32[640,256]{1,0:T(8,128)S(1)}, f32[640,256]{1,0:T(8,128)S(1)}) fusion(f32[640]{0:T(1024)S(1)} %get-tuple-element.30, s32[640]{0:T(1024)S(1)} %get-tuple-element.13, f32[640]{0:T(1024)S(1)} %get-tuple-element.31, s32[640]{0:T(1024)S(1)} %get-tuple-element.14, f32[640]{0:T(1024)S(1)} %get-tuple-element.32, ...), kind=kLoop, calls=%fused_computation.29 | loop fusion | flops 4096000 | bytes 2007040 | tf_op jit(solution)/shard_map/add | solution.py:89
  33.8 7.1 %add_convert_fusion = bf16[640,16,256]{2,1,0:T(8,128)(2,1)S(1)} fusion(f32[640,256]{1,0:T(8,128)S(1)} %get-tuple-element.38, f32[640,256]{1,0:T(8,128)S(1)} %get-tuple-element.39, f32[640,256]{1,0:T(8,128)S(1)} %select_add_fusion.2, f32[640,256]{1,0:T(8,128)S(1)} %get-tuple-element.37, pred[640,16]{1,0:T(8,128)(4,1)S(1)} %get-tuple-element.46, ...), kind=kLoop, calls=%fused_computation | loop fusion | flops 20971520 | bytes 7905280 | tf_op jit(solution)/shard_map/convert
  40.9 3.5 %copy.47 = bf16[80,8,16,256]{3,1,2,0:T(8,128)(2,1)S(1)} copy(bf16[80,8,16,256]{3,2,1,0:T(8,128)(2,1)S(1)} %bitcast.35) | data formatting | bytes 10485760
  44.4 1.1 convolution_convert_fusion
  45.5 0.4 copy.48
  45.9 0.1 slice.120
  46.0 1.3 copy.31
  47.3 6.3 %all-to-all-start.1 = ((bf16[129,8,512]{2,0,1:T(8,128)(2,1)}), bf16[129,8,512]{2,0,1:T(8,128)(2,1)S(1)}, u32[]{:S(2)}, u32[]{:S(2)}) async-start(bf16[129,8,512]{2,0,1:T(8,128)(2,1)} %copy.31), calls=%async_computation.1 | async-start | bytes 2228224 | tf_op jit(solution)/shard_map/all_to_all | solution.py:109
  53.6 4.2 %fusion = bf16[1032,1032]{1,0:T(8,128)(2,1)} fusion(f32[1040,1032]{1,0:T(8,128)} %bitcast.37), kind=kLoop, calls=%fused_computation.5 | loop fusion | flops 2130048 | bytes 6390144 | tf_op jit(solution)/shard_map/convert_element_type | solution.py:39
  57.8 11.4 %all-to-all-done.1 = bf16[129,8,512]{2,0,1:T(8,128)(2,1)S(1)} async-done(((bf16[129,8,512]{2,0,1:T(8,128)(2,1)}), bf16[129,8,512]{2,0,1:T(8,128)(2,1)S(1)}, u32[]{:S(2)}, u32[]{:S(2)}) %all-to-all-start.1) | async-done | bytes 1056800 | tf_op jit(solution)/shard_map/all_to_all | solution.py:109
  69.3 0.5 reshape.784
  69.8 1.7 %fusion.3 = bf16[256,2,2,1032]{0,3,1,2:T(8,128)(2,1)S(1)} fusion(bf16[256,2,256,1]{0,2,3,1:T(8,128)(2,1)} %bitcast.45, bf16[1032,2,256]{2,1,0:T(2,128)(2,1)S(1)} %reshape.784), kind=kOutput, calls=%fused_computation.12 | convolution fusion | flops 542121984 | bytes 3432448 | tf_op jit(solution)/shard_map/wxy,yrk->kxrw/dot_general | solution.py:119
  71.5 4.7 %copy.34 = bf16[256,2,2,1032]{3,2,1,0:T(2,128)(2,1)} copy(bf16[256,2,2,1032]{0,3,1,2:T(8,128)(2,1)S(1)} %fusion.3) | data formatting | bytes 4227072 | tf_op jit(solution)/shard_map/convert_element_type | solution.py:121
  76.2 1.1 fusion.63
  77.3 0.0 copy-start
  77.3 6.2 %reshape.785 = bf16[1024,1032]{1,0:T(8,128)(2,1)} reshape(bf16[256,2,2,1032]{3,2,1,0:T(2,128)(2,1)} %copy.34) | data formatting | bytes 4227072 | tf_op jit(solution)/shard_map/reshape | solution.py:123
  83.4 0.0 copy-done
  83.4 1.5 pad_maximum_fusion
  84.9 6.3 %copy.35 = bf16[256,2,2,1032]{3,2,1,0:T(2,128)(2,1)S(1)} copy(bf16[256,2,2,1032]{0,3,1,2:T(8,128)(2,1)} %pad_maximum_fusion) | data formatting | bytes 4227072 | tf_op jit(solution)/shard_map/stack | solution.py:122
  91.2 3.0 %reshape.786 = bf16[1024,1032]{1,0:T(8,128)(2,1)} reshape(bf16[256,2,2,1032]{3,2,1,0:T(2,128)(2,1)S(1)} %copy.35) | data formatting | bytes 4227072 | tf_op jit(solution)/shard_map/reshape | solution.py:124
  94.2 0.0 copy-start.1
  94.2 0.0 copy-start.2
  94.2 5.5 %fusion.64 = f32[1024,1032]{0,1:T(8,128)S(1)} fusion(bf16[1024,1032]{1,0:T(8,128)(2,1)} %reshape.785, bf16[1032,1032]{1,0:T(8,128)(2,1)} %fusion.1), kind=kOutput, calls=%fused_computation.154 | convolution fusion | flops 2181169152 | bytes 8470656 | tf_op jit(solution)/shard_map/dot_general | solution.py:125
  99.8 0.0 copy-done.1
  99.8 0.0 copy-done.2
  99.8 3.2 %fusion.2 = bf16[1024,1032]{0,1:T(8,128)(2,1)S(1)} fusion(f32[1024,1032]{0,1:T(8,128)S(1)} %fusion.64, bf16[1024,1032]{1,0:T(8,128)(2,1)S(1)} %copy-done.2, bf16[1032,1032]{1,0:T(8,128)(2,1)S(1)} %copy-done.1), kind=kOutput, calls=%fused_computation.10 | convolution fusion | flops 2183282688 | bytes 10584192 | tf_op jit(solution)/shard_map/dot_general | solution.py:125
  103.0 2.5 %copy.36 = bf16[1024,1032]{1,0:T(8,128)(2,1)} copy(bf16[1024,1032]{0,1:T(8,128)(2,1)S(1)} %fusion.2) | data formatting | bytes 4227072 | tf_op jit(solution)/shard_map/convert_element_type | solution.py:128
  105.5 0.0 copy-start.3
  105.5 8.3 %all-to-all-start.2 = ((bf16[128,8,1032]{2,1,0:T(8,128)(2,1)}), bf16[128,8,1032]{2,1,0:T(8,128)(2,1)S(1)}, u32[]{:S(2)}, u32[]{:S(2)}) async-start(bf16[128,8,1032]{2,1,0:T(8,128)(2,1)} %bitcast.39), calls=%async_computation.2 | async-start | bytes 4718592 | tf_op jit(solution)/shard_map/all_to_all | solution.py:129
  113.8 0.0 copy-done.3
  113.8 0.2 copy.28
  114.0 0.1 reshape.781
  114.2 32.8 %all-to-all-done.2 = bf16[128,8,1032]{2,1,0:T(8,128)(2,1)S(1)} async-done(((bf16[128,8,1032]{2,1,0:T(8,128)(2,1)}), bf16[128,8,1032]{2,1,0:T(8,128)(2,1)S(1)}, u32[]{:S(2)}, u32[]{:S(2)}) %all-to-all-start.2) | async-done | bytes 2113568 | tf_op jit(solution)/shard_map/all_to_all | solution.py:129
  147.0 2.7 %copy.37 = bf16[128,8,1032]{0,2,1:T(8,128)(2,1)} copy(bf16[128,8,1032]{2,1,0:T(8,128)(2,1)S(1)} %all-to-all-done.2) | data formatting | bytes 4227072 | tf_op jit(solution)/shard_map/all_to_all | solution.py:129
  149.7 4.9 %convolution_bitcast_fusion = f32[2,256,2,1032]{1,3,2,0:T(8,128)} fusion(bf16[128,2,2,2,1032]{0,4,3,2,1:T(8,128)(2,1)} %bitcast.40, bf16[2,128,2,2,256,1]{4,3,2,1,0,5:T(2,128)(2,1)S(1)} %bitcast.44), kind=kOutput, calls=%fused_computation.9 | convolution fusion | flops 1082130432 | bytes 6864896 | tf_op jit(solution)/shard_map/sqxRv,RsxUu->Uuqv/dot_general | solution.py:131
  (4 shorter events, 0.1 us)
Async XLA Ops:
  7.4 17.8 %all-to-all-start = ((bf16[16,2,2940]{2,1,0:T(2,128)(2,1)}), bf16[16,2,2940]{2,1,0:T(2,128)(2,1)S(1)}, u32[]{:S(2)}, u32[]{:S(2)}) async-start(bf16[16,2,2940]{2,1,0:T(2,128)(2,1)} %reshape.819), calls=%async_computation | async-start | bytes 376832 | tf_op jit(solution)/shard_map/all_to_all | solution.py:69
  47.3 21.9 %all-to-all-start.1 = ((bf16[129,8,512]{2,0,1:T(8,128)(2,1)}), bf16[129,8,512]{2,0,1:T(8,128)(2,1)S(1)}, u32[]{:S(2)}, u32[]{:S(2)}) async-start(bf16[129,8,512]{2,0,1:T(8,128)(2,1)} %copy.31), calls=%async_computation.1 | async-start | bytes 2228224 | tf_op jit(solution)/shard_map/all_to_all | solution.py:109
  77.3 6.2 %copy-start = (bf16[256,2,1,1032]{0,3,1,2:T(8,128)(2,1)S(1)}, bf16[256,2,1,1032]{0,3,1,2:T(8,128)(2,1)}, u32[]{:S(2)}) copy-start(bf16[256,2,1,1032]{0,3,1,2:T(8,128)(2,1)} %get-tuple-element.34) | copy-start | bytes 3170308
  94.2 5.6 %copy-start.1 = (bf16[1032,1032]{1,0:T(8,128)(2,1)S(1)}, bf16[1032,1032]{1,0:T(8,128)(2,1)}, u32[]{:S(2)}) copy-start(bf16[1032,1032]{1,0:T(8,128)(2,1)} %fusion) | copy-start | bytes 6390148
  94.2 5.6 %copy-start.2 = (bf16[1024,1032]{1,0:T(8,128)(2,1)S(1)}, bf16[1024,1032]{1,0:T(8,128)(2,1)}, u32[]{:S(2)}) copy-start(bf16[1024,1032]{1,0:T(8,128)(2,1)} %reshape.786) | copy-start | bytes 6340612
  105.5 8.3 %copy-start.3 = (bf16[256,256]{0,1:T(8,128)(2,1)S(1)}, bf16[256,256]{0,1:T(8,128)(2,1)}, u32[]{:S(2)}) copy-start(bf16[256,256]{0,1:T(8,128)(2,1)} %get-tuple-element.52) | copy-start | bytes 393220
  105.5 41.5 %all-to-all-start.2 = ((bf16[128,8,1032]{2,1,0:T(8,128)(2,1)}), bf16[128,8,1032]{2,1,0:T(8,128)(2,1)S(1)}, u32[]{:S(2)}, u32[]{:S(2)}) async-start(bf16[128,8,1032]{2,1,0:T(8,128)(2,1)} %bitcast.39), calls=%async_computation.2 | async-start | bytes 4718592 | tf_op jit(solution)/shard_map/all_to_all | solution.py:129

commit v2 on v0

--- a/solution.py
+++ b/solution.py
@@ -112,18 +112,24 @@
 
     cos_y, sin_y = dft_tables(NY)
     table_y = jnp.concatenate([cos_y, -sin_y], axis=1)
-    cos_w, sin_w = twiddles(NW)
+    padded_nw = -(-NW // 128) * 128
+    edge = ((0, padded_nw - NW), (0, padded_nw - NW))
+    cos_w, sin_w = [jnp.pad(t, edge) for t in twiddles(NW)]
     table_x = complex_table(NX).reshape(2, devices, rows_dev, 2, NX)
     table_y, cos_w, sin_w, table_x = lax.optimization_barrier((table_y, cos_w, sin_w, table_x))
 
-    first = jnp.einsum("wxy,yK->wxK", cube_w, table_y, preferred_element_type=jnp.float32)
-    first = first.astype(jnp.bfloat16).reshape(NW, rows_dev, 2, NY)
-    by_cos = jnp.einsum("wxrk,wv->rkxv", first, cos_w, preferred_element_type=jnp.float32)
-    by_sin = jnp.einsum("wxrk,wv->rkxv", first, sin_w, preferred_element_type=jnp.float32)
-    second = jnp.stack([by_cos[0] + by_sin[1], by_cos[1] - by_sin[0]], axis=2)
-    second = second.astype(jnp.bfloat16).reshape(devices, per_dev * rows_dev * 2, NW)
+    cube_yw = jnp.pad(jnp.transpose(cube_w, (2, 1, 0)), ((0, 0), (0, 0), (0, padded_nw - NW)))
+    first = jnp.einsum("yxw,yK->xKw", cube_yw, table_y, preferred_element_type=jnp.float32)
+    first = first.astype(jnp.bfloat16).reshape(2 * NY * rows_dev, padded_nw)
+    by_cos = jnp.dot(first, cos_w, preferred_element_type=jnp.float32)
+    by_sin = jnp.dot(first, sin_w, preferred_element_type=jnp.float32)
+    by_cos = by_cos.reshape(rows_dev, 2, NY, padded_nw)
+    by_sin = by_sin.reshape(rows_dev, 2, NY, padded_nw)
+    second = jnp.stack([by_cos[:, 0] + by_sin[:, 1], by_cos[:, 1] - by_sin[:, 0]], axis=2)
+    second = jnp.transpose(second, (1, 0, 2, 3))
+    second = second.astype(jnp.bfloat16).reshape(devices, per_dev * rows_dev * 2, padded_nw)
     pencils = lax.all_to_all(second, ("sky", "gz"), split_axis=0, concat_axis=0, tiled=True)
-    pencils = pencils.reshape(devices, per_dev, rows_dev, 2, NW)
+    pencils = pencils.reshape(devices, per_dev, rows_dev, 2, padded_nw)[..., :NW]
     return jnp.einsum("sqxRv,RsxUu->Uuqv", pencils, table_x, preferred_element_type=jnp.float32)
 
 

time: 138 us -> 137 us (level)
  other arithmetic: 32 us -> 27.2 us
  local copies, waits for them, and re-layouts: 24.3 us -> 27.2 us
    another operation x1 -> x0, local copies, waits for them, and re-layouts: 6.27 us -> none  [shards(): second = jnp.stack([by_cos[0] + by_sin[1], by_cos[1] - by_sin[0]], axis=2)]
    unnamed x8 -> x17, local copies, waits for them, and re-layouts: 6 us -> 10.7 us
    convert_element_type x1, other arithmetic: 4.22 us -> 0.47 us  [twiddles(): (cos_t * factor).astype(jnp.bfloat16)]
    pad x0 -> x2, local copies, waits for them, and re-layouts: none -> 3.44 us  [shards(): cos_w, sin_w = [jnp.pad(t, edge) for t in twiddles(NW)]]
    reshape x0 -> x1, local copies, waits for them, and re-layouts: none -> 2.32 us  [shards(): second.astype(jnp.bfloat16)]
    all_to_all x1, local copies, waits for them, and re-layouts: 2.69 us -> 0.37 us  [shards(): lax.all_to_all(second, ('sky', 'gz'), split_axis=0, concat_axis=0, tiled=...]
    reshape x1 -> x2, local copies, waits for them, and re-layouts: 0.48 us -> 2.04 us  [shards(): cube_w = cube_w.reshape(NW, rows_dev, NY)]
    another operation x2 -> x1, other arithmetic: 8.59 us -> 7.08 us
where the time goes in v2:
time: 137 us; the launch traced here: 136 us
  blocking collectives  41.5 us (30%)
  other arithmetic  27.2 us (20%)
  local copies, waits for them, and re-layouts  27.2 us (20%)
  matrix products  14.9 us (11%)
  starting transfers between devices  13.9 us (10%)
  waiting for transfers between devices  11.1 us (8%)
    all_to_all x1, blocking collectives, shards(): lax.all_to_all(second, ('sky', 'gz'), split_axis=0, concat_axis=0, tiled=...  41.5 us
    all_to_all x1, waiting for transfers between devices, shards(): lax.all_to_all(cube_t, 'gz', split_axis=1, concat_axis=0, tiled=True)  11.1 us
    unnamed x17, local copies, waits for them, and re-layouts  10.7 us
    all_to_all x1, starting transfers between devices, route_fibres(): got = lax.all_to_all(send, 'sky', split_axis=0, concat_axis=0, tiled=True)  7.62 us
    another operation x1, other arithmetic  7.08 us
    all_to_all x1, starting transfers between devices, shards(): lax.all_to_all(cube_t, 'gz', split_axis=1, concat_axis=0, tiled=True)  6.26 us
    dot_general x1, matrix products, shards(): jnp.einsum('sqxRv,RsxUu->Uuqv', pencils, table_x, preferred_element_type=...  4.88 us
    dot_general x1, matrix products, shards(): by_cos = jnp.dot(first, cos_w, preferred_element_type=jnp.float32)  3.5 us
  transfers between devices with their start and end apart: 2, of which 1 were waited for; matrix products, arithmetic and copies ran while one was open for 10% of the time, Pallas kernels for 0%

profile of v2, /device:TPU:1, one launch (start us, length us, event | category | flops | bytes accessed | tf_op | source)
XLA Modules:
  0.0 136.1 jit_solution(2527429251361032913)
XLA Ops:
  0.0 0.9 convert_reduce_fusion
  0.9 0.7 multiply_add_fusion.1
  1.6 0.7 fusion.67
  2.3 1.2 convolution_convert_fusion.2
  3.5 0.2 copy.29
  3.7 0.5 all_to_all.27
  4.2 0.5 broadcast.798
  4.7 1.8 %reduce.49 = bf16[16,5880]{1,0:T(8,128)(2,1)S(1)} reduce(bf16[16,1,5880]{2,1,0:T(2,128)(2,1)S(1)} %all_to_all.27, bf16[]{:T(256)} %broadcast.798), dimensions={1}, to_apply=%all_to_all.27.reduce_sub_computation | reduce | bytes 376322 | tf_op jit(solution)/shard_map/all_to_all | solution.py:69
  6.5 0.9 reshape.853
  7.4 7.6 %all-to-all-start = ((bf16[16,2,2940]{2,1,0:T(2,128)(2,1)}), bf16[16,2,2940]{2,1,0:T(2,128)(2,1)}, u32[]{:S(2)}, u32[]{:S(2)}) async-start(bf16[16,2,2940]{2,1,0:T(2,128)(2,1)} %reshape.853), calls=%async_computation | async-start | bytes 376832 | tf_op jit(solution)/shard_map/all_to_all | solution.py:69
  15.0 0.3 fusion.58
  15.3 1.1 multiply_convert_fusion
  16.5 0.0 copy-start.2
  16.5 1.4 %fusion.21 = (f32[65,1032]{1,0:T(8,128)S(1)}, f32[65,1032]{1,0:T(8,128)S(1)}) fusion(s32[65]{0:T(128)S(1)} %iota_multiply_fusion), kind=kLoop, calls=%fused_computation.67 | loop fusion | flops 603720 | bytes 536900 | tf_op jit(solution)/shard_map/cos | solution.py:31
  17.9 3.1 %multiply_add_fusion = (f32[65,16,1032]{2,1,0:T(8,128)}, f32[65,16,1032]{2,1,0:T(8,128)S(1)}) fusion(f32[16,1032]{1,0:T(8,128)S(1)} %get-tuple-element.52, f32[65,1032]{1,0:T(8,128)S(1)} %get-tuple-element.47, f32[16,1032]{1,0:T(8,128)S(1)} %get-tuple-element.53, f32[65,1032]{1,0:T(8,128)S(1)} %get-tuple-element.46), kind=kLoop, calls=%fused_computation.2 | loop fusion | flops 6439680 | bytes 9254976 | tf_op jit(solution)/shard_map/add | solution.py:37
  21.0 0.5 fusion.1
  21.5 1.0 fusion.61
  22.5 0.0 copy-start.4
  22.5 0.0 copy-done.2
  22.5 0.6 copy-done.4
  23.2 0.1 reshape.817
  23.3 1.7 %pad.11 = bf16[1152,1152]{1,0:T(8,128)(2,1)} pad(bf16[1032,1032]{1,0:T(8,128)(2,1)S(1)} %fusion.1, bf16[]{:T(256)} %constant.149.clone.1), padding=0_120x0_120 | pad | bytes 4784258 | tf_op jit(solution)/shard_map/jit(_pad)/pad | solution.py:117
  25.0 0.0 all-to-all-done
  25.0 1.9 %reshape.854 = bf16[16,1,5880]{2,1,0:T(2,128)(2,1)S(1)} reshape(bf16[16,2,2940]{2,1,0:T(2,128)(2,1)} %all-to-all-done) | data formatting | bytes 376320
  26.9 1.1 reduce
  28.0 0.5 reshape.818
  28.5 1.1 fusion.35
  29.6 0.1 slice_convert_fusion
  29.7 2.7 %slice_reduce_fusion.15 = (f32[640]{0:T(1024)S(1)}, f32[640]{0:T(1024)S(1)}, f32[640]{0:T(1024)S(1)}, f32[640]{0:T(1024)S(1)}, f32[640]{0:T(1024)S(1)}, /*index=...) fusion(f32[640,16]{1,0:T(8,128)S(1)} %slice_convert_fusion), kind=kLoop, calls=%fused_computation.93 | loop fusion | bytes 81920 | tf_op jit(solution)/shard_map/slice | solution.py:89
  32.4 0.2 iota_compare_fusion.9
  32.6 0.2 iota_compare_fusion.7
  32.9 0.7 select_add_fusion.2
  33.6 1.4 %select_add_fusion.3 = (f32[640,256]{1,0:T(8,128)S(1)}, f32[640,256]{1,0:T(8,128)S(1)}, f32[640,256]{1,0:T(8,128)S(1)}) fusion(f32[640]{0:T(1024)S(1)} %get-tuple-element.34, s32[640]{0:T(1024)S(1)} %get-tuple-element.17, f32[640]{0:T(1024)S(1)} %get-tuple-element.35, s32[640]{0:T(1024)S(1)} %get-tuple-element.18, f32[640]{0:T(1024)S(1)} %get-tuple-element.36, ...), kind=kLoop, calls=%fused_computation.35 | loop fusion | flops 4096000 | bytes 2007040 | tf_op jit(solution)/shard_map/add | solution.py:89
  35.1 7.1 %add_convert_fusion = bf16[640,16,256]{2,1,0:T(8,128)(2,1)S(1)} fusion(f32[640,256]{1,0:T(8,128)S(1)} %get-tuple-element.40, f32[640,256]{1,0:T(8,128)S(1)} %get-tuple-element.41, f32[640,256]{1,0:T(8,128)S(1)} %select_add_fusion.2, f32[640,256]{1,0:T(8,128)S(1)} %get-tuple-element.39, pred[640,16]{1,0:T(8,128)(4,1)S(1)} %get-tuple-element.48, ...), kind=kLoop, calls=%fused_computation | loop fusion | flops 20971520 | bytes 7905280 | tf_op jit(solution)/shard_map/convert.4
  42.1 3.5 %copy.51 = bf16[80,8,16,256]{3,1,2,0:T(8,128)(2,1)S(1)} copy(bf16[80,8,16,256]{3,2,1,0:T(8,128)(2,1)S(1)} %bitcast.59) | data formatting | bytes 10485760
  45.6 1.1 convolution_convert_fusion
  46.7 0.4 copy.52
  47.1 0.1 slice.135
  47.2 1.4 %copy.31 = bf16[129,8,512]{2,0,1:T(8,128)(2,1)} copy(bf16[129,8,512]{2,1,0:T(8,128)(2,1)S(1)} %slice.135) | data formatting | bytes 2113536 | tf_op jit(solution)/shard_map/all_to_all | solution.py:109
  48.6 6.3 %all-to-all-start.1 = ((bf16[129,8,512]{2,0,1:T(8,128)(2,1)}), bf16[129,8,512]{2,0,1:T(8,128)(2,1)S(1)}, u32[]{:S(2)}, u32[]{:S(2)}) async-start(bf16[129,8,512]{2,0,1:T(8,128)(2,1)} %copy.31), calls=%async_computation.1 | async-start | bytes 2228224 | tf_op jit(solution)/shard_map/all_to_all | solution.py:109
  54.9 2.8 %fusion = bf16[1032,1032]{1,0:T(8,128)(2,1)S(1)} fusion(f32[1040,1032]{1,0:T(8,128)} %bitcast.61), kind=kLoop, calls=%fused_computation.5 | loop fusion | flops 2130048 | bytes 6390144 | tf_op jit(solution)/shard_map/convert_element_type | solution.py:39
  57.6 0.0 copy-start.3
  57.6 0.0 copy-start.5
  57.7 1.7 %pad.12 = bf16[1152,1152]{1,0:T(8,128)(2,1)} pad(bf16[1032,1032]{1,0:T(8,128)(2,1)S(1)} %fusion, bf16[]{:T(256)} %constant.149.clone.1), padding=0_120x0_120 | pad | bytes 4784258 | tf_op jit(solution)/shard_map/jit(_pad)/pad | solution.py:117
  59.4 0.0 copy-done.3
  59.4 0.0 copy-done.5
  59.4 11.1 %all-to-all-done.1 = bf16[129,8,512]{2,0,1:T(8,128)(2,1)S(1)} async-done(((bf16[129,8,512]{2,0,1:T(8,128)(2,1)}), bf16[129,8,512]{2,0,1:T(8,128)(2,1)S(1)}, u32[]{:S(2)}, u32[]{:S(2)}) %all-to-all-start.1) | async-done | bytes 1056800 | tf_op jit(solution)/shard_map/all_to_all | solution.py:109
  70.5 0.5 reshape.819
  71.0 1.6 %copy.32 = bf16[1032,2,256]{0,2,1:T(8,128)(2,1)S(1)} copy(bf16[1032,2,256]{2,1,0:T(2,128)(2,1)S(1)} %reshape.819) | data formatting | bytes 2113536 | tf_op jit(solution)/shard_map/reshape | solution.py:111
  72.6 0.0 copy-start.1
  72.6 0.8 convolution_convert_fusion.1
  73.4 0.9 copy-done.1
  74.3 3.5 %fusion.2 = f32[2,2,256,1152]{3,2,1,0:T(8,128)S(1)} fusion(bf16[2,2,256,1152]{3,2,1,0:T(8,128)(2,1)S(1)} %bitcast.68, bf16[1152,1152]{1,0:T(8,128)(2,1)S(1)} %copy-done.1), kind=kOutput, calls=%fused_computation.10 | convolution fusion | flops 2717908992 | bytes 9732096 | tf_op jit(solution)/shard_map/dot_general | solution.py:125
  77.8 0.0 copy-done
  77.8 3.5 %fusion.4 = f32[2,2,256,1152]{3,2,1,0:T(8,128)S(1)} fusion(bf16[2,2,256,1152]{3,2,1,0:T(8,128)(2,1)S(1)} %bitcast.69, bf16[1152,1152]{1,0:T(8,128)(2,1)S(1)} %copy-done), kind=kOutput, calls=%fused_computation.12 | convolution fusion | flops 2717908992 | bytes 9732096 | tf_op jit(solution)/shard_map/dot_general | solution.py:124
  81.4 0.3 fusion.11
  81.7 0.2 fusion.10
  81.9 0.2 maximum_bitcast_fusion
  82.2 2.4 %copy.36 = bf16[256,2,2,1152]{3,2,1,0:T(2,128)(2,1)S(1)} copy(bf16[256,2,2,1152]{3,0,1,2:T(8,128)(2,1)S(1)} %maximum_bitcast_fusion) | data formatting | bytes 4718592 | tf_op jit(solution)/shard_map/convert_element_type | solution.py:130
  84.6 2.3 %reshape.820 = bf16[128,8,1152]{2,1,0:T(8,128)(2,1)} reshape(bf16[256,2,2,1152]{3,2,1,0:T(2,128)(2,1)S(1)} %copy.36) | data formatting | bytes 4718592 | tf_op jit(solution)/shard_map/reshape | solution.py:130
  86.9 41.5 %all_to_all.31 = bf16[128,8,1152]{2,1,0:T(8,128)(2,1)S(1)} all-to-all(bf16[128,8,1152]{2,1,0:T(8,128)(2,1)} %reshape.820), channel_id=1, replica_groups=mesh['sky'=16,'gz'=8] {'sky','gz'}, dimensions={0} | all-to-all | bytes 4718592 | tf_op jit(solution)/shard_map/all_to_all | solution.py:131
  128.4 0.4 copy.37
  128.8 2.4 %copy.50 = bf16[128,2,2,2,1032]{0,4,2,3,1:T(8,128)(2,1)} copy(bf16[128,2,2,2,1032]{4,0,3,2,1:T(8,128)(2,1)S(1)} %bitcast.63) | data formatting | bytes 4227072
  131.2 4.9 %convolution_bitcast_fusion = f32[2,256,2,1032]{1,3,2,0:T(8,128)} fusion(bf16[128,2,2,2,1032]{0,4,2,3,1:T(8,128)(2,1)} %copy.50, bf16[2,128,2,2,256,1]{4,3,2,1,0,5:T(2,128)(2,1)S(1)} %bitcast.70), kind=kOutput, calls=%fused_computation.8 | convolution fusion | flops 1082130432 | bytes 6864896 | tf_op jit(solution)/shard_map/sqxRv,RsxUu->Uuqv/dot_general | solution.py:133
  (6 shorter events, 0.1 us)
Async XLA Ops:
  7.4 17.7 %all-to-all-start = ((bf16[16,2,2940]{2,1,0:T(2,128)(2,1)}), bf16[16,2,2940]{2,1,0:T(2,128)(2,1)}, u32[]{:S(2)}, u32[]{:S(2)}) async-start(bf16[16,2,2940]{2,1,0:T(2,128)(2,1)} %reshape.853), calls=%async_computation | async-start | bytes 376832 | tf_op jit(solution)/shard_map/all_to_all | solution.py:69
  16.5 6.0 %copy-start.2 = (bf16[256,256]{1,0:T(8,128)(2,1)}, bf16[256,256]{1,0:T(8,128)(2,1)S(1)}, u32[]{:S(2)}) copy-start(bf16[256,256]{1,0:T(8,128)(2,1)S(1)} %get-tuple-element.55) | copy-start | bytes 393220
  22.5 0.7 copy-start.4
  48.6 21.9 %all-to-all-start.1 = ((bf16[129,8,512]{2,0,1:T(8,128)(2,1)}), bf16[129,8,512]{2,0,1:T(8,128)(2,1)S(1)}, u32[]{:S(2)}, u32[]{:S(2)}) async-start(bf16[129,8,512]{2,0,1:T(8,128)(2,1)} %copy.31), calls=%async_computation.1 | async-start | bytes 2228224 | tf_op jit(solution)/shard_map/all_to_all | solution.py:109
  57.6 1.7 %copy-start.3 = (bf16[256,256]{1,0:T(8,128)(2,1)S(1)}, bf16[256,256]{1,0:T(8,128)(2,1)}, u32[]{:S(2)}) copy-start(bf16[256,256]{1,0:T(8,128)(2,1)} %copy-done.2) | copy-start | bytes 393220
  57.6 1.7 %copy-start.5 = (bf16[256,256]{1,0:T(8,128)(2,1)S(1)}, bf16[256,256]{1,0:T(8,128)(2,1)}, u32[]{:S(2)}) copy-start(bf16[256,256]{1,0:T(8,128)(2,1)} %copy-done.4) | copy-start | bytes 393220
  72.6 1.8 %copy-start.1 = (bf16[1152,1152]{1,0:T(8,128)(2,1)S(1)}, bf16[1152,1152]{1,0:T(8,128)(2,1)}, u32[]{:S(2)}) copy-start(bf16[1152,1152]{1,0:T(8,128)(2,1)} %pad.12) | copy-start | bytes 7962628
  74.3 3.5 %copy-start = (bf16[1152,1152]{1,0:T(8,128)(2,1)S(1)}, bf16[1152,1152]{1,0:T(8,128)(2,1)}, u32[]{:S(2)}) copy-start(bf16[1152,1152]{1,0:T(8,128)(2,1)} %pad.11) | copy-start | bytes 7962628

commit v3 on v2

--- a/solution.py
+++ b/solution.py
@@ -65,7 +65,7 @@
     col = (offset % NY).astype(jnp.bfloat16)[:, None]
     packed = jnp.concatenate([spectra, kernel, row, col], axis=1)
     send = jnp.dot(pick, packed, preferred_element_type=jnp.float32).astype(jnp.bfloat16)
-    send = send.reshape(sky_count, block * packed.shape[1])
+    send = send.reshape(sky_count, block, packed.shape[1])
     got = lax.all_to_all(send, "sky", split_axis=0, concat_axis=0, tiled=True)
     return got.reshape(slots_all, packed.shape[1]), capacity, block
 
@@ -73,25 +73,22 @@
 def grid_tile(got, slab_width, taps, tile_rows, capacity, block):
     slots_all = got.shape[0]
     values = got[:, :slab_width]
-    weights = got[:, slab_width : slab_width + taps].astype(jnp.float32)
     slot_ids = jnp.arange(slots_all, dtype=jnp.int32)
     shift = jnp.where(slot_ids % block >= capacity, tile_rows, 0)
     corner_row = got[:, slab_width + taps].astype(jnp.int32) - shift
     corner_col = got[:, slab_width + taps + 1].astype(jnp.int32)
     rows = jnp.arange(tile_rows, dtype=jnp.int32)
     columns = jnp.arange(NY, dtype=jnp.int32)
-    spread = jnp.zeros((slots_all, tile_rows, NY), jnp.float32)
+    spread = jnp.zeros((tile_rows, slots_all, NY), jnp.bfloat16)
     for step_a in range(KSIDE):
-        active = rows[None, :] == (corner_row + step_a)[:, None]
-        line = jnp.zeros((slots_all, NY), jnp.float32)
+        line = jnp.zeros((slots_all, NY), jnp.bfloat16)
         for step_b in range(KSIDE):
             placed = columns[None, :] == ((corner_col + step_b) % NY)[:, None]
-            line = line + jnp.where(placed, weights[:, step_a * KSIDE + step_b][:, None], 0.0)
-        spread = spread + jnp.where(active[:, :, None], line[:, None, :], 0.0)
-    spread_bf = spread.astype(jnp.bfloat16).reshape(slots_all, tile_rows * NY)
-    cube_t = lax.dot_general(
-        values, spread_bf, (((0,), (0,)), ((), ())), preferred_element_type=jnp.float32
-    )
+            line = jnp.where(placed, got[:, slab_width + step_a * KSIDE + step_b][:, None], line)
+        active = rows[:, None] == (corner_row + step_a)[None, :]
+        spread = jnp.where(active[:, :, None], line[None, :, :], spread)
+    cube_t = jnp.einsum("sw,xsc->wxc", values, spread, preferred_element_type=jnp.float32)
+    cube_t = cube_t.reshape(slab_width, tile_rows * NY)
     return cube_t.astype(jnp.bfloat16)
 
 

time: 137 us -> 124 us (0.905)
  other arithmetic: 27.2 us -> 17.2 us
  local copies, waits for them, and re-layouts: 27.2 us -> 19.3 us
  matrix products: 14.9 us -> 19.8 us
    unnamed x17 -> x7, local copies, waits for them, and re-layouts: 10.7 us -> 3.37 us
    another operation x1 -> x0, other arithmetic: 7.08 us -> none
    dot_general x1, matrix products: 1.06 us -> 5.95 us  [grid_tile(): jnp.einsum('sw,xsc->wxc', values, spread, preferred_element_type=jnp.floa...]
    select_n x0 -> x3, other arithmetic: none -> 3.73 us  [the longest x2 2.85 us: grid_tile(): jnp.where(placed, got[:, slab_width + step_a * KSIDE + step_b][:, None],...]
    all_to_all x2 -> x0, other arithmetic: 2.88 us -> none  [route_fibres(): got = lax.all_to_all(send, 'sky', split_axis=0, concat_axis=0, tiled=True)]
    all_to_all x4 -> x0, local copies, waits for them, and re-layouts: 2.44 us -> none  [the longest x2 1.43 us: shards(): lax.all_to_all(cube_t, 'gz', split_axis=1, concat_axis=0, tiled=True)]
    add x2 -> x1, other arithmetic: 2.16 us -> 0.01 us  [grid_tile(): active = rows[:, None] == (corner_row + step_a)[None, :]]
    convert_element_type x0 -> x3, local copies, waits for them, and re-layouts: none -> 1.91 us  [grid_tile(): return cube_t.astype(jnp.bfloat16)]
  transfers between devices with their start and end apart: 2 -> 2, of which waited for: 1 -> 1; matrix products, arithmetic and copies ran while one was open for 10% -> 12% of each run, Pallas kernels for 0% -> 0%
where the time goes in v3:
time: 124 us; the launch traced here: 123 us
  blocking collectives  41.5 us (33%)
  matrix products  19.8 us (16%)
  local copies, waits for them, and re-layouts  19.3 us (16%)
  other arithmetic  17.2 us (14%)
  starting transfers between devices  13.8 us (11%)
  waiting for transfers between devices  11.2 us (9%)
    all_to_all x1, blocking collectives, shards(): lax.all_to_all(second, ('sky', 'gz'), split_axis=0, concat_axis=0, tiled=...  41.5 us
    all_to_all x1, waiting for transfers between devices, shards(): lax.all_to_all(cube_t, 'gz', split_axis=1, concat_axis=0, tiled=True)  11.2 us
    all_to_all x1, starting transfers between devices, route_fibres(): got = lax.all_to_all(send, 'sky', split_axis=0, concat_axis=0, tiled=True)  7.57 us
    all_to_all x1, starting transfers between devices, shards(): lax.all_to_all(cube_t, 'gz', split_axis=1, concat_axis=0, tiled=True)  6.26 us
    dot_general x1, matrix products, grid_tile(): jnp.einsum('sw,xsc->wxc', values, spread, preferred_element_type=jnp.floa...  5.95 us
    dot_general x1, matrix products, shards(): jnp.einsum('sqxRv,RsxUu->Uuqv', pencils, table_x, preferred_element_type=...  4.87 us
    dot_general x1, matrix products, shards(): by_cos = jnp.dot(first, cos_w, preferred_element_type=jnp.float32)  3.51 us
    dot_general x1, matrix products, shards(): by_sin = jnp.dot(first, sin_w, preferred_element_type=jnp.float32)  3.49 us
  transfers between devices with their start and end apart: 2, of which 1 were waited for; matrix products, arithmetic and copies ran while one was open for 12% of the time, Pallas kernels for 0%

profile of v3, /device:TPU:1, one launch (start us, length us, event | category | flops | bytes accessed | tf_op | source)
XLA Modules:
  0.0 123.0 jit_solution(835717785161052970)
XLA Ops:
  0.0 0.9 convert_reduce_fusion.1
  0.9 0.7 multiply_add_fusion.1
  1.6 0.7 fusion.98
  2.3 1.2 convolution_convert_fusion.1
  3.5 0.9 copy.43
  4.4 7.6 %all-to-all-start = ((bf16[16,40,147]{2,1,0:T(8,128)(2,1)}), bf16[16,40,147]{2,1,0:T(8,128)(2,1)S(1)}, u32[]{:S(2)}, u32[]{:S(2)}) async-start(bf16[16,40,147]{2,1,0:T(8,128)(2,1)} %bitcast.5), calls=%async_computation | async-start | bytes 655360 | tf_op jit(solution)/shard_map/all_to_all | solution.py:69
  12.0 0.3 fusion.85
  12.4 1.1 multiply_convert_fusion
  13.5 1.4 %fusion.54 = (f32[65,1032]{1,0:T(8,128)S(1)}, f32[65,1032]{1,0:T(8,128)S(1)}) fusion(s32[65]{0:T(128)S(1)} %iota_multiply_fusion), kind=kLoop, calls=%fused_computation.91 | loop fusion | flops 603720 | bytes 536900 | tf_op jit(solution)/shard_map/cos | solution.py:31
  14.9 3.1 %multiply_add_fusion = (f32[65,16,1032]{2,1,0:T(8,128)}, f32[65,16,1032]{2,1,0:T(8,128)S(1)}) fusion(f32[16,1032]{1,0:T(8,128)S(1)} %get-tuple-element.53, f32[65,1032]{1,0:T(8,128)S(1)} %get-tuple-element.48, f32[16,1032]{1,0:T(8,128)S(1)} %get-tuple-element.54, f32[65,1032]{1,0:T(8,128)S(1)} %get-tuple-element.47), kind=kLoop, calls=%fused_computation.9 | loop fusion | flops 6439680 | bytes 9254976 | tf_op jit(solution)/shard_map/add | solution.py:37
  18.0 0.5 fusion.10
  18.5 1.0 fusion.88
  19.5 1.0 reshape.827
  20.5 1.7 %pad.11 = bf16[1152,1152]{1,0:T(8,128)(2,1)} pad(bf16[1032,1032]{1,0:T(8,128)(2,1)S(1)} %fusion.10, bf16[]{:T(256)} %constant.150.clone.1), padding=0_120x0_120 | pad | bytes 4784258 | tf_op jit(solution)/shard_map/jit(_pad)/pad | solution.py:114
  22.2 0.0 all-to-all-done
  22.2 0.9 fusion.57
  23.1 1.5 %slice_reduce_fusion.15 = (bf16[640]{0:T(1024)(128)(2,1)S(1)}, bf16[640]{0:T(1024)(128)(2,1)S(1)}, bf16[640]{0:T(1024)(128)(2,1)S(1)}, bf16[640]{0:T(1024)(128)(...) fusion(bf16[640,147]{1,0:T(8,128)(2,1)S(1)} %bitcast.60), kind=kLoop, calls=%fused_computation.133 | loop fusion | bytes 40960 | tf_op jit(solution)/shard_map/slice | solution.py:87
  24.7 0.9 fusion.44
  25.6 2.0 %fusion.45 = (bf16[640,256]{1,0:T(8,128)(2,1)S(1)}, bf16[640,256]{1,0:T(8,128)(2,1)S(1)}, bf16[640,256]{1,0:T(8,128)(2,1)S(1)}) fusion(s32[640]{0:T(1024)S(1)} %get-tuple-element.32, s32[640]{0:T(1024)S(1)} %get-tuple-element.30, s32[640]{0:T(1024)S(1)} %get-tuple-element.31, s32[640]{0:T(1024)S(1)} %get-tuple-element.29, ...), kind=kLoop, calls=%fused_computation.64 | loop fusion | flops 2621440 | bytes 1008640 | tf_op jit(solution)/shard_map/jit(_where)/select_n | solution.py:87
  27.6 6.0 %fusion.24 = bf16[129,16,256]{2,0,1:T(8,128)(2,1)S(1)} fusion(pred[16,640]{1,0:T(8,128)(4,1)S(1)} %get-tuple-element.49, pred[16,640]{1,0:T(8,128)(4,1)S(1)} %get-tuple-element.50, pred[16,640]{1,0:T(8,128)(4,1)S(1)} %get-tuple-element.51, pred[16,640]{1,0:T(8,128)(4,1)S(1)} %get-tuple-element.52, bf16[640,256]{1,0:T(8,128)(2,1)S(1)} %get-tuple-element.37, ...), kind=kOutput, calls=%fused_computation.34 | convolution fusion | flops 687345664 | bytes 2596608 | tf_op jit(solution)/shard_map/sw,xsc->wxc/dot_general | solution.py:90
  33.5 0.2 copy.45
  33.7 0.3 convert_element_type.130
  34.1 1.4 %copy.46 = bf16[129,8,512]{2,0,1:T(8,128)(2,1)} copy(bf16[129,8,512]{2,1,0:T(8,128)(2,1)S(1)} %convert_element_type.130) | data formatting | bytes 2113536 | tf_op jit(solution)/shard_map/convert_element_type | solution.py:92
  35.5 6.3 %all-to-all-start.1 = ((bf16[129,8,512]{2,0,1:T(8,128)(2,1)}), bf16[129,8,512]{2,0,1:T(8,128)(2,1)S(1)}, u32[]{:S(2)}, u32[]{:S(2)}) async-start(bf16[129,8,512]{2,0,1:T(8,128)(2,1)} %copy.46), calls=%async_computation.1 | async-start | bytes 2228224 | tf_op jit(solution)/shard_map/all_to_all | solution.py:106
  41.7 2.8 %fusion.9 = bf16[1032,1032]{1,0:T(8,128)(2,1)S(1)} fusion(f32[1040,1032]{1,0:T(8,128)} %bitcast.62), kind=kLoop, calls=%fused_computation.12 | loop fusion | flops 2130048 | bytes 6390144 | tf_op jit(solution)/shard_map/convert_element_type | solution.py:39
  44.5 1.7 %pad.12 = bf16[1152,1152]{1,0:T(8,128)(2,1)} pad(bf16[1032,1032]{1,0:T(8,128)(2,1)S(1)} %fusion.9, bf16[]{:T(256)} %constant.150.clone.1), padding=0_120x0_120 | pad | bytes 4784258 | tf_op jit(solution)/shard_map/jit(_pad)/pad | solution.py:114
  46.2 11.2 %all-to-all-done.1 = bf16[129,8,512]{2,0,1:T(8,128)(2,1)S(1)} async-done(((bf16[129,8,512]{2,0,1:T(8,128)(2,1)}), bf16[129,8,512]{2,0,1:T(8,128)(2,1)S(1)}, u32[]{:S(2)}, u32[]{:S(2)}) %all-to-all-start.1) | async-done | bytes 1056800 | tf_op jit(solution)/shard_map/all_to_all | solution.py:106
  57.4 0.5 reshape.830
  57.9 1.6 %copy.47 = bf16[1032,2,256]{0,2,1:T(8,128)(2,1)S(1)} copy(bf16[1032,2,256]{2,1,0:T(2,128)(2,1)S(1)} %reshape.830) | data formatting | bytes 2113536 | tf_op jit(solution)/shard_map/reshape | solution.py:108
  59.5 0.0 copy-start.1
  59.5 0.8 convolution_convert_fusion
  60.3 0.9 copy-done.1
  61.2 0.0 copy-start
  61.2 3.5 %fusion.11 = f32[2,2,256,1152]{3,2,1,0:T(8,128)S(1)} fusion(bf16[2,2,256,1152]{3,2,1,0:T(8,128)(2,1)S(1)} %bitcast.67, bf16[1152,1152]{1,0:T(8,128)(2,1)S(1)} %copy-done.1), kind=kOutput, calls=%fused_computation.17 | convolution fusion | flops 2717908992 | bytes 9732096 | tf_op jit(solution)/shard_map/dot_general | solution.py:122
  64.7 0.0 copy-done
  64.7 3.5 %fusion.13 = f32[2,2,256,1152]{3,2,1,0:T(8,128)S(1)} fusion(bf16[2,2,256,1152]{3,2,1,0:T(8,128)(2,1)S(1)} %bitcast.68, bf16[1152,1152]{1,0:T(8,128)(2,1)S(1)} %copy-done), kind=kOutput, calls=%fused_computation.19 | convolution fusion | flops 2717908992 | bytes 9732096 | tf_op jit(solution)/shard_map/dot_general | solution.py:121
  68.2 0.3 fusion.28
  68.6 0.2 fusion.27
  68.8 0.2 maximum_bitcast_fusion
  69.1 2.4 %copy.51 = bf16[256,2,2,1152]{3,2,1,0:T(2,128)(2,1)S(1)} copy(bf16[256,2,2,1152]{3,0,1,2:T(8,128)(2,1)S(1)} %maximum_bitcast_fusion) | data formatting | bytes 4718592 | tf_op jit(solution)/shard_map/convert_element_type | solution.py:127
  71.5 2.3 %reshape.831 = bf16[128,8,1152]{2,1,0:T(8,128)(2,1)} reshape(bf16[256,2,2,1152]{3,2,1,0:T(2,128)(2,1)S(1)} %copy.51) | data formatting | bytes 4718592 | tf_op jit(solution)/shard_map/reshape | solution.py:127
  73.8 41.5 %all_to_all.23 = bf16[128,8,1152]{2,1,0:T(8,128)(2,1)S(1)} all-to-all(bf16[128,8,1152]{2,1,0:T(8,128)(2,1)} %reshape.831), channel_id=1, replica_groups=mesh['sky'=16,'gz'=8] {'sky','gz'}, dimensions={0} | all-to-all | bytes 4718592 | tf_op jit(solution)/shard_map/all_to_all | solution.py:128
  115.3 0.4 copy.52
  115.7 0.0 copy-start.2
  115.7 2.4 %copy.66 = bf16[128,2,2,2,1032]{0,4,2,3,1:T(8,128)(2,1)} copy(bf16[128,2,2,2,1032]{4,0,3,2,1:T(8,128)(2,1)S(1)} %bitcast.64) | data formatting | bytes 4227072
  118.2 0.0 copy-done.2
  118.2 4.9 %convolution_bitcast_fusion = f32[2,256,2,1032]{1,3,2,0:T(8,128)} fusion(bf16[128,2,2,2,1032]{0,4,2,3,1:T(8,128)(2,1)} %copy.66, bf16[2,128,2,2,256,1]{4,3,2,1,0,5:T(2,128)(2,1)S(1)} %bitcast.69), kind=kOutput, calls=%fused_computation.15 | convolution fusion | flops 1082130432 | bytes 6864896 | tf_op jit(solution)/shard_map/sqxRv,RsxUu->Uuqv/dot_general | solution.py:130
  (8 shorter events, 0.1 us)
Async XLA Ops:
  4.4 17.8 %all-to-all-start = ((bf16[16,40,147]{2,1,0:T(8,128)(2,1)}), bf16[16,40,147]{2,1,0:T(8,128)(2,1)S(1)}, u32[]{:S(2)}, u32[]{:S(2)}) async-start(bf16[16,40,147]{2,1,0:T(8,128)(2,1)} %bitcast.5), calls=%async_computation | async-start | bytes 655360 | tf_op jit(solution)/shard_map/all_to_all | solution.py:69
  35.5 21.9 %all-to-all-start.1 = ((bf16[129,8,512]{2,0,1:T(8,128)(2,1)}), bf16[129,8,512]{2,0,1:T(8,128)(2,1)S(1)}, u32[]{:S(2)}, u32[]{:S(2)}) async-start(bf16[129,8,512]{2,0,1:T(8,128)(2,1)} %copy.46), calls=%async_computation.1 | async-start | bytes 2228224 | tf_op jit(solution)/shard_map/all_to_all | solution.py:106
  59.5 1.8 %copy-start.1 = (bf16[1152,1152]{1,0:T(8,128)(2,1)S(1)}, bf16[1152,1152]{1,0:T(8,128)(2,1)}, u32[]{:S(2)}) copy-start(bf16[1152,1152]{1,0:T(8,128)(2,1)} %pad.12) | copy-start | bytes 7962628
  61.2 3.5 %copy-start = (bf16[1152,1152]{1,0:T(8,128)(2,1)S(1)}, bf16[1152,1152]{1,0:T(8,128)(2,1)}, u32[]{:S(2)}) copy-start(bf16[1152,1152]{1,0:T(8,128)(2,1)} %pad.11) | copy-start | bytes 7962628
  115.7 2.5 %copy-start.2 = (bf16[2,128,2,2,256]{4,3,2,1,0:T(2,128)(2,1)S(1)}, bf16[2,128,2,2,256]{4,3,2,1,0:T(2,128)(2,1)}, u32[]{:S(2)}) copy-start(bf16[2,128,2,2,256]{4,3,2,1,0:T(2,128)(2,1)} %reshape.827) | copy-start | bytes 1572868

commit v4 on v3

--- a/solution.py
+++ b/solution.py
@@ -11,8 +11,9 @@
 KSIDE = 4
 
 
-def dft_tables(length):
-    steps = jnp.arange(length, dtype=jnp.int32)
+def dft_tables(length, steps=None):
+    if steps is None:
+        steps = jnp.arange(length, dtype=jnp.int32)
     phase = steps[:, None] * steps[None, :] % length
     angles = phase.astype(jnp.float32) * (2.0 * math.pi / length)
     factor = 1.0 / math.sqrt(length)
@@ -22,9 +23,9 @@
     )
 
 
-def twiddles(length, fine_count=16):
+def twiddles(steps, fine_count=16):
+    length = steps.shape[0]
     coarse_count = -(-length // fine_count)
-    steps = jnp.arange(length, dtype=jnp.int32)
     angle = 2.0 * math.pi / length
     coarse = (jnp.arange(coarse_count, dtype=jnp.int32)[:, None] * fine_count * steps[None, :]) % length
     fine = (jnp.arange(fine_count, dtype=jnp.int32)[:, None] * steps[None, :]) % length
@@ -39,8 +40,8 @@
     return (cos_t * factor).astype(jnp.bfloat16), (sin_t * factor).astype(jnp.bfloat16)
 
 
-def complex_table(length):
-    cos_t, sin_t = dft_tables(length)
+def complex_table(length, steps=None):
+    cos_t, sin_t = dft_tables(length, steps)
     top = jnp.concatenate([cos_t, -sin_t], axis=1)
     bottom = jnp.concatenate([sin_t, cos_t], axis=1)
     return jnp.concatenate([top, bottom], axis=0)
@@ -103,16 +104,20 @@
 
     got, capacity, block = route_fibres(spectra, kernel, owner, offset, sky_count)
     cube_t = grid_tile(got, slab_width, taps, tile_rows, capacity, block)
+    steps_w = jnp.arange(NW, dtype=jnp.int32)
+    steps_y = jnp.arange(NY, dtype=jnp.int32)
+    steps_x = jnp.arange(NX, dtype=jnp.int32)
+    cube_t, steps_w, steps_y, steps_x = lax.optimization_barrier((cube_t, steps_w, steps_y, steps_x))
     cube_w = lax.all_to_all(cube_t, "gz", split_axis=1, concat_axis=0, tiled=True)
     rows_dev = tile_rows // gz_count
     cube_w = cube_w.reshape(NW, rows_dev, NY)
 
-    cos_y, sin_y = dft_tables(NY)
+    cos_y, sin_y = dft_tables(NY, steps_y)
     table_y = jnp.concatenate([cos_y, -sin_y], axis=1)
     padded_nw = -(-NW // 128) * 128
     edge = ((0, padded_nw - NW), (0, padded_nw - NW))
-    cos_w, sin_w = [jnp.pad(t, edge) for t in twiddles(NW)]
-    table_x = complex_table(NX).reshape(2, devices, rows_dev, 2, NX)
+    cos_w, sin_w = [jnp.pad(t, edge) for t in twiddles(steps_w)]
+    table_x = complex_table(NX, steps_x).reshape(2, devices, rows_dev, 2, NX)
     table_y, cos_w, sin_w, table_x = lax.optimization_barrier((table_y, cos_w, sin_w, table_x))
 
     cube_yw = jnp.pad(jnp.transpose(cube_w, (2, 1, 0)), ((0, 0), (0, 0), (0, padded_nw - NW)))

time: 124 us -> 122 us (0.984)
  local copies, waits for them, and re-layouts: 19.3 us -> 22.9 us
  waiting for transfers between devices: 11.2 us -> 7.92 us
  blocking collectives: 41.5 us -> 39.3 us
  starting transfers between devices: 13.8 us -> 15.1 us
    all_to_all x1, waiting for transfers between devices: 11.2 us -> 0.09 us  [shards(): lax.all_to_all(cube_t, 'gz', split_axis=1, concat_axis=0, tiled=True)]
    all_to_all x1, waiting for transfers between devices: 0.01 us -> 7.84 us  [route_fibres(): got = lax.all_to_all(send, 'sky', split_axis=0, concat_axis=0, tiled=True)]
    convert_element_type x1, other arithmetic: 2.78 us -> 0.46 us  [twiddles(): (sin_t * factor).astype(jnp.bfloat16)]
    all_to_all x1, blocking collectives: 41.5 us -> 39.3 us  [shards(): lax.all_to_all(second, ('sky', 'gz'), split_axis=0, concat_axis=0, tiled=...]
    add x1, other arithmetic: 3.14 us -> 1.01 us  [twiddles(): sin_t = (sin_c * cos_f + cos_c * sin_f).reshape(rows, length)[:length]]
    convert_element_type x3 -> x1, local copies, waits for them, and re-layouts: 1.91 us -> 0.21 us  [grid_tile(): return cube_t.astype(jnp.bfloat16)]
    pad x2, local copies, waits for them, and re-layouts: 3.43 us -> 5.09 us  [shards(): cos_w, sin_w = [jnp.pad(t, edge) for t in twiddles(steps_w)]]
    convert_element_type x1, other arithmetic: 0.47 us -> 1.9 us  [twiddles(): (cos_t * factor).astype(jnp.bfloat16)]
  transfers between devices with their start and end apart: 2 -> 2, of which waited for: 1 -> 2; matrix products, arithmetic and copies ran while one was open for 12% -> 13% of each run, Pallas kernels for 0% -> 0%
where the time goes in v4:
time: 122 us
  blocking collectives  39.3 us (32%)
  local copies, waits for them, and re-layouts  22.9 us (19%)
  matrix products  19.8 us (16%)
  other arithmetic  16.3 us (13%)
  starting transfers between devices  15.1 us (12%)
  waiting for transfers between devices  7.92 us (6%)
    all_to_all x1, blocking collectives, shards(): lax.all_to_all(second, ('sky', 'gz'), split_axis=0, concat_axis=0, tiled=...  39.3 us
    all_to_all x1, waiting for transfers between devices, route_fibres(): got = lax.all_to_all(send, 'sky', split_axis=0, concat_axis=0, tiled=True)  7.84 us
    all_to_all x1, starting transfers between devices, shards(): lax.all_to_all(cube_t, 'gz', split_axis=1, concat_axis=0, tiled=True)  7.57 us
    all_to_all x1, starting transfers between devices, route_fibres(): got = lax.all_to_all(send, 'sky', split_axis=0, concat_axis=0, tiled=True)  7.57 us
    dot_general x1, matrix products, grid_tile(): jnp.einsum('sw,xsc->wxc', values, spread, preferred_element_type=jnp.floa...  5.93 us
    pad x2, local copies, waits for them, and re-layouts, shards(): cos_w, sin_w = [jnp.pad(t, edge) for t in twiddles(steps_w)]  5.09 us
    dot_general x1, matrix products, shards(): jnp.einsum('sqxRv,RsxUu->Uuqv', pencils, table_x, preferred_element_type=...  4.88 us
    unnamed x10, local copies, waits for them, and re-layouts  4.34 us
  transfers between devices with their start and end apart: 2, of which 2 were waited for; matrix products, arithmetic and copies ran while one was open for 13% of the time, Pallas kernels for 0%

profile of v4, /device:TPU:1, one launch (start us, length us, event | category | flops | bytes accessed | tf_op | source)
XLA Modules:
  0.0 121.7 jit_solution(17585373757103785097)
XLA Ops:
  0.0 0.9 convert_reduce_fusion.1
  0.9 0.7 multiply_add_fusion.1
  1.6 0.7 fusion.99
  2.3 1.2 convolution_convert_fusion.1
  3.5 0.9 copy.43
  4.4 7.6 %all-to-all-start = ((bf16[16,40,147]{2,1,0:T(8,128)(2,1)}), bf16[16,40,147]{2,1,0:T(8,128)(2,1)S(1)}, u32[]{:S(2)}, u32[]{:S(2)}) async-start(bf16[16,40,147]{2,1,0:T(8,128)(2,1)} %bitcast.1), calls=%async_computation | async-start | bytes 655360 | tf_op jit(solution)/shard_map/all_to_all | solution.py:70
  12.0 7.8 %all-to-all-done = bf16[16,40,147]{2,1,0:T(8,128)(2,1)S(1)} async-done(((bf16[16,40,147]{2,1,0:T(8,128)(2,1)}), bf16[16,40,147]{2,1,0:T(8,128)(2,1)S(1)}, u32[]{:S(2)}, u32[]{:S(2)}) %all-to-all-start) | async-done | bytes 188192 | tf_op jit(solution)/shard_map/all_to_all | solution.py:70
  19.9 0.9 fusion.57
  20.8 1.5 %slice_reduce_fusion.15 = (bf16[640]{0:T(1024)(128)(2,1)S(1)}, bf16[640]{0:T(1024)(128)(2,1)S(1)}, bf16[640]{0:T(1024)(128)(2,1)S(1)}, bf16[640]{0:T(1024)(128)(...) fusion(bf16[640,147]{1,0:T(8,128)(2,1)S(1)} %bitcast.66), kind=kLoop, calls=%fused_computation.142 | loop fusion | bytes 40960 | tf_op jit(solution)/shard_map/slice | solution.py:88
  22.3 0.9 fusion.44
  23.2 1.8 %fusion.45 = (bf16[640,256]{1,0:T(8,128)(2,1)S(1)}, bf16[640,256]{1,0:T(8,128)(2,1)S(1)}, bf16[640,256]{1,0:T(8,128)(2,1)S(1)}) fusion(s32[640]{0:T(1024)S(1)} %get-tuple-element.40, s32[640]{0:T(1024)S(1)} %get-tuple-element.38, s32[640]{0:T(1024)S(1)} %get-tuple-element.39, s32[640]{0:T(1024)S(1)} %get-tuple-element.37, ...), kind=kLoop, calls=%fused_computation.64 | loop fusion | flops 2621440 | bytes 1008640 | tf_op jit(solution)/shard_map/jit(_where)/select_n | solution.py:88
  25.0 5.9 %fusion.24 = bf16[129,16,256]{2,0,1:T(8,128)(2,1)S(1)} fusion(pred[16,640]{1,0:T(8,128)(4,1)S(1)} %get-tuple-element.61, pred[16,640]{1,0:T(8,128)(4,1)S(1)} %get-tuple-element.62, pred[16,640]{1,0:T(8,128)(4,1)S(1)} %get-tuple-element.63, pred[16,640]{1,0:T(8,128)(4,1)S(1)} %get-tuple-element.64, bf16[640,256]{1,0:T(8,128)(2,1)S(1)} %get-tuple-element.45, ...), kind=kOutput, calls=%fused_computation.34 | convolution fusion | flops 687345664 | bytes 2596608 | tf_op jit(solution)/shard_map/sw,xsc->wxc/dot_general | solution.py:91
  31.0 0.2 copy.45
  31.2 0.1 pad.26
  31.3 0.5 copy.67
  31.7 0.4 copy.68
  32.2 0.1 slice.130
  32.3 1.3 %copy.46 = bf16[129,8,512]{2,0,1:T(8,128)(2,1)} copy(bf16[129,8,512]{2,1,0:T(8,128)(2,1)S(1)} %slice.130) | data formatting | bytes 2113536 | tf_op jit(solution)/shard_map/all_to_all | solution.py:111
  33.6 7.6 %all-to-all-start.1 = ((bf16[129,8,512]{2,0,1:T(8,128)(2,1)}), bf16[129,8,512]{2,0,1:T(8,128)(2,1)}, u32[]{:S(2)}, u32[]{:S(2)}) async-start(bf16[129,8,512]{2,0,1:T(8,128)(2,1)} %copy.46), calls=%async_computation.1 | async-start | bytes 2228224 | tf_op jit(solution)/shard_map/all_to_all | solution.py:111
  41.2 0.3 fusion.87
  41.5 1.3 %multiply_convert_fusion = (bf16[256,256]{1,0:T(8,128)(2,1)S(1)}, bf16[256,256]{1,0:T(8,128)(2,1)S(1)}) fusion(s32[256]{0:T(256)S(1)} %iota.151), kind=kLoop, calls=%fused_computation.120 | loop fusion | flops 1179648 | bytes 263168 | tf_op jit(solution)/shard_map/convert_element_type | solution.py:22
  42.8 1.4 %fusion.54 = (f32[65,1032]{1,0:T(8,128)S(1)}, f32[65,1032]{1,0:T(8,128)S(1)}) fusion(s32[1032]{0:T(1024)S(1)} %iota.150, s32[65]{0:T(128)S(1)} %iota_multiply_fusion), kind=kLoop, calls=%fused_computation.98 | loop fusion | flops 603720 | bytes 541028 | tf_op jit(solution)/shard_map/cos | solution.py:32
  44.2 1.0 multiply_add_fusion
  45.2 0.5 fusion.9
  45.7 1.9 %fusion.10 = bf16[1032,1032]{1,0:T(8,128)(2,1)} fusion(f32[1040,1032]{1,0:T(8,128)S(1)} %bitcast.68), kind=kLoop, calls=%fused_computation.14 | loop fusion | flops 2130048 | bytes 6390144 | tf_op jit(solution)/shard_map/convert_element_type | solution.py:40
  47.6 1.1 fusion.89
  48.7 0.9 reshape.858
  49.6 3.4 %pad.11 = bf16[1152,1152]{1,0:T(8,128)(2,1)} pad(bf16[1032,1032]{1,0:T(8,128)(2,1)} %fusion.10, bf16[]{:T(256)} %constant.155.clone.1), padding=0_120x0_120 | pad | bytes 4784258 | tf_op jit(solution)/shard_map/jit(_pad)/pad | solution.py:119
  53.0 1.7 %pad.12 = bf16[1152,1152]{1,0:T(8,128)(2,1)} pad(bf16[1032,1032]{1,0:T(8,128)(2,1)S(1)} %fusion.9, bf16[]{:T(256)} %constant.155.clone.1), padding=0_120x0_120 | pad | bytes 4784258 | tf_op jit(solution)/shard_map/jit(_pad)/pad | solution.py:119
  54.7 1.1 fusion.74
  55.8 1.1 multiply_convert_fusion.3
  56.9 0.1 all-to-all-done.1
  57.0 1.5 %reshape.859 = bf16[1032,2,256]{2,1,0:T(2,128)(2,1)S(1)} reshape(bf16[8,129,512]{2,1,0:T(8,128)(2,1)} %bitcast.8) | data formatting | bytes 2113536 | tf_op jit(solution)/shard_map/reshape | solution.py:113
  58.5 1.8 %copy.47 = bf16[1032,2,256]{0,2,1:T(8,128)(2,1)S(1)} copy(bf16[1032,2,256]{2,1,0:T(2,128)(2,1)S(1)} %reshape.859) | data formatting | bytes 2113536 | tf_op jit(solution)/shard_map/reshape | solution.py:113
  60.3 0.0 copy-start.1
  60.3 0.8 convolution_convert_fusion
  61.1 0.9 copy-done.1
  62.0 0.0 copy-start
  62.0 3.5 %fusion.11 = f32[2,2,256,1152]{3,2,1,0:T(8,128)S(1)} fusion(bf16[2,2,256,1152]{3,2,1,0:T(8,128)(2,1)S(1)} %bitcast.75, bf16[1152,1152]{1,0:T(8,128)(2,1)S(1)} %copy-done.1), kind=kOutput, calls=%fused_computation.17 | convolution fusion | flops 2717908992 | bytes 9732096 | tf_op jit(solution)/shard_map/dot_general | solution.py:127
  65.5 0.0 copy-done
  65.5 3.5 %fusion.13 = f32[2,2,256,1152]{3,2,1,0:T(8,128)S(1)} fusion(bf16[2,2,256,1152]{3,2,1,0:T(8,128)(2,1)S(1)} %bitcast.76, bf16[1152,1152]{1,0:T(8,128)(2,1)S(1)} %copy-done), kind=kOutput, calls=%fused_computation.19 | convolution fusion | flops 2717908992 | bytes 9732096 | tf_op jit(solution)/shard_map/dot_general | solution.py:126
  69.1 0.3 fusion.28
  69.4 0.2 fusion.27
  69.6 0.2 maximum_bitcast_fusion
  69.9 2.4 %copy.51 = bf16[256,2,2,1152]{3,2,1,0:T(2,128)(2,1)S(1)} copy(bf16[256,2,2,1152]{3,0,1,2:T(8,128)(2,1)S(1)} %maximum_bitcast_fusion) | data formatting | bytes 4718592 | tf_op jit(solution)/shard_map/convert_element_type | solution.py:132
  72.3 2.3 %reshape.860 = bf16[128,8,1152]{2,1,0:T(8,128)(2,1)} reshape(bf16[256,2,2,1152]{3,2,1,0:T(2,128)(2,1)S(1)} %copy.51) | data formatting | bytes 4718592 | tf_op jit(solution)/shard_map/reshape | solution.py:132
  74.7 39.3 %all_to_all.26 = bf16[128,8,1152]{2,1,0:T(8,128)(2,1)S(1)} all-to-all(bf16[128,8,1152]{2,1,0:T(8,128)(2,1)} %reshape.860), channel_id=1, replica_groups=mesh['sky'=16,'gz'=8] {'sky','gz'}, dimensions={0} | all-to-all | bytes 4718592 | tf_op jit(solution)/shard_map/all_to_all | solution.py:133
  114.0 0.4 copy.52
  114.3 0.0 copy-start.2
  114.3 2.4 %copy.66 = bf16[128,2,2,2,1032]{0,4,2,3,1:T(8,128)(2,1)} copy(bf16[128,2,2,2,1032]{4,0,3,2,1:T(8,128)(2,1)S(1)} %bitcast.70) | data formatting | bytes 4227072
  116.8 0.0 copy-done.2
  116.8 4.9 %convolution_bitcast_fusion = f32[2,256,2,1032]{1,3,2,0:T(8,128)} fusion(bf16[128,2,2,2,1032]{0,4,2,3,1:T(8,128)(2,1)} %copy.66, bf16[2,128,2,2,256,1]{4,3,2,1,0,5:T(2,128)(2,1)S(1)} %bitcast.77), kind=kOutput, calls=%fused_computation.15 | convolution fusion | flops 1082130432 | bytes 6864896 | tf_op jit(solution)/shard_map/sqxRv,RsxUu->Uuqv/dot_general | solution.py:135
  (10 shorter events, 0.1 us)
Async XLA Ops:
  4.4 15.4 %all-to-all-start = ((bf16[16,40,147]{2,1,0:T(8,128)(2,1)}), bf16[16,40,147]{2,1,0:T(8,128)(2,1)S(1)}, u32[]{:S(2)}, u32[]{:S(2)}) async-start(bf16[16,40,147]{2,1,0:T(8,128)(2,1)} %bitcast.1), calls=%async_computation | async-start | bytes 655360 | tf_op jit(solution)/shard_map/all_to_all | solution.py:70
  33.6 23.3 %all-to-all-start.1 = ((bf16[129,8,512]{2,0,1:T(8,128)(2,1)}), bf16[129,8,512]{2,0,1:T(8,128)(2,1)}, u32[]{:S(2)}, u32[]{:S(2)}) async-start(bf16[129,8,512]{2,0,1:T(8,128)(2,1)} %copy.46), calls=%async_computation.1 | async-start | bytes 2228224 | tf_op jit(solution)/shard_map/all_to_all | solution.py:111
  60.3 1.8 %copy-start.1 = (bf16[1152,1152]{1,0:T(8,128)(2,1)S(1)}, bf16[1152,1152]{1,0:T(8,128)(2,1)}, u32[]{:S(2)}) copy-start(bf16[1152,1152]{1,0:T(8,128)(2,1)} %pad.12) | copy-start | bytes 7962628
  62.0 3.5 %copy-start = (bf16[1152,1152]{1,0:T(8,128)(2,1)S(1)}, bf16[1152,1152]{1,0:T(8,128)(2,1)}, u32[]{:S(2)}) copy-start(bf16[1152,1152]{1,0:T(8,128)(2,1)} %pad.11) | copy-start | bytes 7962628
  114.3 2.5 %copy-start.2 = (bf16[2,128,2,2,256]{4,3,2,1,0:T(2,128)(2,1)S(1)}, bf16[2,128,2,2,256]{4,3,2,1,0:T(2,128)(2,1)}, u32[]{:S(2)}) copy-start(bf16[2,128,2,2,256]{4,3,2,1,0:T(2,128)(2,1)} %reshape.858) | copy-start | bytes 1572868

commit v5 on v4

--- a/solution.py
+++ b/solution.py
@@ -23,9 +23,9 @@
     )
 
 
-def twiddles(steps, fine_count=16):
-    length = steps.shape[0]
-    coarse_count = -(-length // fine_count)
+def twiddles(length, padded, fine_count=16):
+    coarse_count = padded // fine_count
+    steps = jnp.arange(padded, dtype=jnp.int32)
     angle = 2.0 * math.pi / length
     coarse = (jnp.arange(coarse_count, dtype=jnp.int32)[:, None] * fine_count * steps[None, :]) % length
     fine = (jnp.arange(fine_count, dtype=jnp.int32)[:, None] * steps[None, :]) % length
@@ -33,11 +33,13 @@
     sin_c = jnp.sin(coarse.astype(jnp.float32) * angle)[:, None, :]
     cos_f = jnp.cos(fine.astype(jnp.float32) * angle)[None, :, :]
     sin_f = jnp.sin(fine.astype(jnp.float32) * angle)[None, :, :]
-    rows = coarse_count * fine_count
-    cos_t = (cos_c * cos_f - sin_c * sin_f).reshape(rows, length)[:length]
-    sin_t = (sin_c * cos_f + cos_c * sin_f).reshape(rows, length)[:length]
+    cos_t = (cos_c * cos_f - sin_c * sin_f).reshape(padded, padded)
+    sin_t = (sin_c * cos_f + cos_c * sin_f).reshape(padded, padded)
+    inside = (steps[:, None] < length) & (steps[None, :] < length)
     factor = 1.0 / math.sqrt(length)
-    return (cos_t * factor).astype(jnp.bfloat16), (sin_t * factor).astype(jnp.bfloat16)
+    cos_t = jnp.where(inside, cos_t * factor, 0.0).astype(jnp.bfloat16)
+    sin_t = jnp.where(inside, sin_t * factor, 0.0).astype(jnp.bfloat16)
+    return cos_t, sin_t
 
 
 def complex_table(length, steps=None):
@@ -104,10 +106,9 @@
 
     got, capacity, block = route_fibres(spectra, kernel, owner, offset, sky_count)
     cube_t = grid_tile(got, slab_width, taps, tile_rows, capacity, block)
-    steps_w = jnp.arange(NW, dtype=jnp.int32)
     steps_y = jnp.arange(NY, dtype=jnp.int32)
     steps_x = jnp.arange(NX, dtype=jnp.int32)
-    cube_t, steps_w, steps_y, steps_x = lax.optimization_barrier((cube_t, steps_w, steps_y, steps_x))
+    cube_t, steps_y, steps_x = lax.optimization_barrier((cube_t, steps_y, steps_x))
     cube_w = lax.all_to_all(cube_t, "gz", split_axis=1, concat_axis=0, tiled=True)
     rows_dev = tile_rows // gz_count
     cube_w = cube_w.reshape(NW, rows_dev, NY)
@@ -115,8 +116,7 @@
     cos_y, sin_y = dft_tables(NY, steps_y)
     table_y = jnp.concatenate([cos_y, -sin_y], axis=1)
     padded_nw = -(-NW // 128) * 128
-    edge = ((0, padded_nw - NW), (0, padded_nw - NW))
-    cos_w, sin_w = [jnp.pad(t, edge) for t in twiddles(steps_w)]
+    cos_w, sin_w = twiddles(NW, padded_nw)
     table_x = complex_table(NX, steps_x).reshape(2, devices, rows_dev, 2, NX)
     table_y, cos_w, sin_w, table_x = lax.optimization_barrier((table_y, cos_w, sin_w, table_x))
 

time: 122 us -> 121 us (level)
  local copies, waits for them, and re-layouts: 22.9 us -> 15.9 us
  waiting for transfers between devices: 7.92 us -> 11.7 us
  other arithmetic: 16.3 us -> 18.5 us
    all_to_all x1, waiting for transfers between devices: 0.09 us -> 11 us  [shards(): lax.all_to_all(cube_t, 'gz', split_axis=1, concat_axis=0, tiled=True)]
    all_to_all x1, waiting for transfers between devices: 7.84 us -> 0.76 us  [route_fibres(): got = lax.all_to_all(send, 'sky', split_axis=0, concat_axis=0, tiled=True)]
    pad x2 -> x0, local copies, waits for them, and re-layouts: 5.09 us -> none  [shards(): cos_w, sin_w = [jnp.pad(t, edge) for t in twiddles(steps_w)]]
    mul x0 -> x1, other arithmetic: none -> 2.05 us  [twiddles(): sin_t = jnp.where(inside, sin_t * factor, 0.0).astype(jnp.bfloat16)]
    convert_element_type x2 -> x1, other arithmetic: 2.36 us -> 3.27 us  [twiddles(): sin_t = jnp.where(inside, sin_t * factor, 0.0).astype(jnp.bfloat16)]
    unnamed x10 -> x8, local copies, waits for them, and re-layouts: 4.34 us -> 4.34 us
  transfers between devices with their start and end apart: 2 -> 2, of which waited for: 2 -> 2; matrix products, arithmetic and copies ran while one was open for 13% -> 10% of each run, Pallas kernels for 0% -> 0%
where the time goes in v5:
time: 121 us
  blocking collectives  39.5 us (33%)
  matrix products  19.8 us (16%)
  other arithmetic  18.5 us (15%)
  local copies, waits for them, and re-layouts  15.9 us (13%)
  starting transfers between devices  15.1 us (12%)
  waiting for transfers between devices  11.7 us (10%)
    all_to_all x1, blocking collectives, shards(): lax.all_to_all(second, ('sky', 'gz'), split_axis=0, concat_axis=0, tiled=...  39.5 us
    all_to_all x1, waiting for transfers between devices, shards(): lax.all_to_all(cube_t, 'gz', split_axis=1, concat_axis=0, tiled=True)  11 us
    all_to_all x1, starting transfers between devices, shards(): lax.all_to_all(cube_t, 'gz', split_axis=1, concat_axis=0, tiled=True)  7.57 us
    all_to_all x1, starting transfers between devices, route_fibres(): got = lax.all_to_all(send, 'sky', split_axis=0, concat_axis=0, tiled=True)  7.57 us
    dot_general x1, matrix products, grid_tile(): jnp.einsum('sw,xsc->wxc', values, spread, preferred_element_type=jnp.floa...  5.93 us
    dot_general x1, matrix products, shards(): jnp.einsum('sqxRv,RsxUu->Uuqv', pencils, table_x, preferred_element_type=...  4.88 us
    unnamed x8, local copies, waits for them, and re-layouts  4.34 us
    dot_general x1, matrix products, shards(): by_cos = jnp.dot(first, cos_w, preferred_element_type=jnp.float32)  3.51 us
  transfers between devices with their start and end apart: 2, of which 2 were waited for; matrix products, arithmetic and copies ran while one was open for 10% of the time, Pallas kernels for 0%

profile of v5, /device:TPU:1, one launch (start us, length us, event | category | flops | bytes accessed | tf_op | source)
XLA Modules:
  0.0 120.8 jit_solution(15826498675672538375)
XLA Ops:
  0.0 0.9 convert_reduce_fusion.1
  0.9 0.7 multiply_add_fusion
  1.6 0.7 fusion.99
  2.3 1.2 convolution_convert_fusion.1
  3.5 0.9 copy.43
  4.4 7.6 %all-to-all-start = ((bf16[16,40,147]{2,1,0:T(8,128)(2,1)}), bf16[16,40,147]{2,1,0:T(8,128)(2,1)S(1)}, u32[]{:S(2)}, u32[]{:S(2)}) async-start(bf16[16,40,147]{2,1,0:T(8,128)(2,1)} %bitcast.1), calls=%async_computation | async-start | bytes 655360 | tf_op jit(solution)/shard_map/all_to_all | solution.py:72
  12.1 0.3 fusion.86
  12.4 1.4 %fusion.54 = (f32[72,1152]{1,0:T(8,128)S(1)}, f32[72,1152]{1,0:T(8,128)S(1)}) fusion(s32[72]{0:T(128)S(1)} %iota_multiply_fusion), kind=kLoop, calls=%fused_computation.98 | loop fusion | flops 746496 | bytes 663840 | tf_op jit(solution)/shard_map/cos | solution.py:32
  13.8 2.1 %add_multiply_fusion = (bf16[72,16,1152]{2,1,0:T(8,128)(2,1)S(1)}, bf16[72,16,1152]{2,1,0:T(8,128)(2,1)S(1)}) fusion(f32[16,1152]{1,0:T(8,128)S(1)} %get-tuple-element.63, f32[72,1152]{1,0:T(8,128)S(1)} %get-tuple-element.58, f32[16,1152]{1,0:T(8,128)S(1)} %get-tuple-element.64, f32[72,1152]{1,0:T(8,128)S(1)} %get-tuple-element.57), kind=kLoop, calls=%fused_computation.4 | loop fusion | flops 13271040 | bytes 6119424 | tf_op jit(solution)/shard_map/mul | solution.py:41
  15.8 3.3 %fusion.1 = (bf16[1152,1152]{1,0:T(8,128)(2,1)}, bf16[1152,1152]{1,0:T(8,128)(2,1)}) fusion(bf16[72,16,1152]{2,1,0:T(8,128)(2,1)S(1)} %get-tuple-element.40, pred[1152]{0:T(1024)(128)(4,1)S(1)} %iota_compare_fusion.12, bf16[72,16,1152]{2,1,0:T(8,128)(2,1)S(1)} %get-tuple-element.41), kind=kLoop, calls=%fused_computation.3 | loop fusion | flops 3981312 | bytes 10617984 | tf_op jit(solution)/shard_map/convert_element_type | solution.py:41
  19.1 0.8 all-to-all-done
  19.9 0.9 fusion.57
  20.8 1.5 %slice_reduce_fusion.15 = (bf16[640]{0:T(1024)(128)(2,1)S(1)}, bf16[640]{0:T(1024)(128)(2,1)S(1)}, bf16[640]{0:T(1024)(128)(2,1)S(1)}, bf16[640]{0:T(1024)(128)(...) fusion(bf16[640,147]{1,0:T(8,128)(2,1)S(1)} %bitcast.68), kind=kLoop, calls=%fused_computation.142 | loop fusion | bytes 40960 | tf_op jit(solution)/shard_map/slice | solution.py:90
  22.3 0.9 fusion.44
  23.2 2.0 %fusion.45 = (bf16[640,256]{1,0:T(8,128)(2,1)S(1)}, bf16[640,256]{1,0:T(8,128)(2,1)S(1)}, bf16[640,256]{1,0:T(8,128)(2,1)S(1)}) fusion(s32[640]{0:T(1024)S(1)} %get-tuple-element.38, s32[640]{0:T(1024)S(1)} %get-tuple-element.36, s32[640]{0:T(1024)S(1)} %get-tuple-element.37, s32[640]{0:T(1024)S(1)} %get-tuple-element.35, ...), kind=kLoop, calls=%fused_computation.64 | loop fusion | flops 2621440 | bytes 1008640 | tf_op jit(solution)/shard_map/jit(_where)/select_n | solution.py:90
  25.2 5.9 %fusion.24 = bf16[129,16,256]{2,0,1:T(8,128)(2,1)S(1)} fusion(pred[16,640]{1,0:T(8,128)(4,1)S(1)} %get-tuple-element.59, pred[16,640]{1,0:T(8,128)(4,1)S(1)} %get-tuple-element.60, pred[16,640]{1,0:T(8,128)(4,1)S(1)} %get-tuple-element.61, pred[16,640]{1,0:T(8,128)(4,1)S(1)} %get-tuple-element.62, bf16[640,256]{1,0:T(8,128)(2,1)S(1)} %get-tuple-element.43, ...), kind=kOutput, calls=%fused_computation.34 | convolution fusion | flops 687345664 | bytes 2596608 | tf_op jit(solution)/shard_map/sw,xsc->wxc/dot_general | solution.py:93
  31.1 0.2 copy.45
  31.4 0.1 pad.17
  31.4 0.5 copy.67
  31.9 0.4 copy.68
  32.4 0.1 slice.120
  32.4 1.3 %copy.46 = bf16[129,8,512]{2,0,1:T(8,128)(2,1)} copy(bf16[129,8,512]{2,1,0:T(8,128)(2,1)S(1)} %slice.120) | data formatting | bytes 2113536 | tf_op jit(solution)/shard_map/all_to_all | solution.py:112
  33.8 7.6 %all-to-all-start.1 = ((bf16[129,8,512]{2,0,1:T(8,128)(2,1)}), bf16[129,8,512]{2,0,1:T(8,128)(2,1)S(1)}, u32[]{:S(2)}, u32[]{:S(2)}) async-start(bf16[129,8,512]{2,0,1:T(8,128)(2,1)} %copy.46), calls=%async_computation.1 | async-start | bytes 2228224 | tf_op jit(solution)/shard_map/all_to_all | solution.py:112
  41.4 1.3 %multiply_convert_fusion = (bf16[256,256]{1,0:T(8,128)(2,1)S(1)}, bf16[256,256]{1,0:T(8,128)(2,1)S(1)}) fusion(s32[256]{0:T(256)S(1)} %iota.177), kind=kLoop, calls=%fused_computation.120 | loop fusion | flops 1179648 | bytes 263168 | tf_op jit(solution)/shard_map/convert_element_type | solution.py:22
  42.6 1.1 fusion.89
  43.7 0.1 reshape.846
  43.9 1.1 fusion.74
  44.9 1.1 multiply_convert_fusion.3
  46.0 11.0 %all-to-all-done.1 = bf16[129,8,512]{2,0,1:T(8,128)(2,1)S(1)} async-done(((bf16[129,8,512]{2,0,1:T(8,128)(2,1)}), bf16[129,8,512]{2,0,1:T(8,128)(2,1)S(1)}, u32[]{:S(2)}, u32[]{:S(2)}) %all-to-all-start.1) | async-done | bytes 1056800 | tf_op jit(solution)/shard_map/all_to_all | solution.py:112
  57.0 0.5 reshape.847
  57.5 1.8 %copy.47 = bf16[1032,2,256]{0,2,1:T(8,128)(2,1)S(1)} copy(bf16[1032,2,256]{2,1,0:T(2,128)(2,1)S(1)} %reshape.847) | data formatting | bytes 2113536 | tf_op jit(solution)/shard_map/reshape | solution.py:114
  59.3 0.0 copy-start.1
  59.3 0.8 convolution_convert_fusion
  60.1 0.9 copy-done.1
  61.1 0.0 copy-start
  61.1 3.5 %fusion.11 = f32[2,2,256,1152]{3,2,1,0:T(8,128)S(1)} fusion(bf16[2,2,256,1152]{3,2,1,0:T(8,128)(2,1)S(1)} %bitcast.76, bf16[1152,1152]{1,0:T(8,128)(2,1)S(1)} %copy-done.1), kind=kOutput, calls=%fused_computation.17 | convolution fusion | flops 2717908992 | bytes 9732096 | tf_op jit(solution)/shard_map/dot_general | solution.py:127
  64.6 0.0 copy-done
  64.6 3.5 %fusion.13 = f32[2,2,256,1152]{3,2,1,0:T(8,128)S(1)} fusion(bf16[2,2,256,1152]{3,2,1,0:T(8,128)(2,1)S(1)} %bitcast.77, bf16[1152,1152]{1,0:T(8,128)(2,1)S(1)} %copy-done), kind=kOutput, calls=%fused_computation.19 | convolution fusion | flops 2717908992 | bytes 9732096 | tf_op jit(solution)/shard_map/dot_general | solution.py:126
  68.1 0.3 fusion.28
  68.4 0.2 fusion.27
  68.7 0.2 maximum_bitcast_fusion
  68.9 2.4 %copy.51 = bf16[256,2,2,1152]{3,2,1,0:T(2,128)(2,1)S(1)} copy(bf16[256,2,2,1152]{3,0,1,2:T(8,128)(2,1)S(1)} %maximum_bitcast_fusion) | data formatting | bytes 4718592 | tf_op jit(solution)/shard_map/convert_element_type | solution.py:132
  71.3 2.3 %reshape.848 = bf16[128,8,1152]{2,1,0:T(8,128)(2,1)} reshape(bf16[256,2,2,1152]{3,2,1,0:T(2,128)(2,1)S(1)} %copy.51) | data formatting | bytes 4718592 | tf_op jit(solution)/shard_map/reshape | solution.py:132
  73.7 39.5 %all_to_all.26 = bf16[128,8,1152]{2,1,0:T(8,128)(2,1)S(1)} all-to-all(bf16[128,8,1152]{2,1,0:T(8,128)(2,1)} %reshape.848), channel_id=1, replica_groups=mesh['sky'=16,'gz'=8] {'sky','gz'}, dimensions={0} | all-to-all | bytes 4718592 | tf_op jit(solution)/shard_map/all_to_all | solution.py:133
  113.1 0.4 copy.52
  113.5 2.4 %copy.66 = bf16[128,2,2,2,1032]{0,4,2,3,1:T(8,128)(2,1)} copy(bf16[128,2,2,2,1032]{4,0,3,2,1:T(8,128)(2,1)S(1)} %bitcast.70) | data formatting | bytes 4227072
  115.9 4.9 %convolution_bitcast_fusion = f32[2,256,2,1032]{1,3,2,0:T(8,128)} fusion(bf16[128,2,2,2,1032]{0,4,2,3,1:T(8,128)(2,1)} %copy.66, bf16[2,128,2,2,256,1]{4,3,2,1,0,5:T(2,128)(2,1)S(1)} %bitcast.78), kind=kOutput, calls=%fused_computation.15 | convolution fusion | flops 1082130432 | bytes 6864896 | tf_op jit(solution)/shard_map/sqxRv,RsxUu->Uuqv/dot_general | solution.py:135
  (10 shorter events, 0.1 us)
Async XLA Ops:
  4.4 15.4 %all-to-all-start = ((bf16[16,40,147]{2,1,0:T(8,128)(2,1)}), bf16[16,40,147]{2,1,0:T(8,128)(2,1)S(1)}, u32[]{:S(2)}, u32[]{:S(2)}) async-start(bf16[16,40,147]{2,1,0:T(8,128)(2,1)} %bitcast.1), calls=%async_computation | async-start | bytes 655360 | tf_op jit(solution)/shard_map/all_to_all | solution.py:72
  33.8 23.2 %all-to-all-start.1 = ((bf16[129,8,512]{2,0,1:T(8,128)(2,1)}), bf16[129,8,512]{2,0,1:T(8,128)(2,1)S(1)}, u32[]{:S(2)}, u32[]{:S(2)}) async-start(bf16[129,8,512]{2,0,1:T(8,128)(2,1)} %copy.46), calls=%async_computation.1 | async-start | bytes 2228224 | tf_op jit(solution)/shard_map/all_to_all | solution.py:112
  59.3 1.8 %copy-start.1 = (bf16[1152,1152]{1,0:T(8,128)(2,1)S(1)}, bf16[1152,1152]{1,0:T(8,128)(2,1)}, u32[]{:S(2)}) copy-start(bf16[1152,1152]{1,0:T(8,128)(2,1)} %get-tuple-element.18) | copy-start | bytes 7962628
  61.1 3.5 %copy-start = (bf16[1152,1152]{1,0:T(8,128)(2,1)S(1)}, bf16[1152,1152]{1,0:T(8,128)(2,1)}, u32[]{:S(2)}) copy-start(bf16[1152,1152]{1,0:T(8,128)(2,1)} %get-tuple-element.17) | copy-start | bytes 7962628

commit v6 on v5

--- a/solution.py
+++ b/solution.py
@@ -73,26 +73,24 @@
     return got.reshape(slots_all, packed.shape[1]), capacity, block
 
 
-def grid_tile(got, slab_width, taps, tile_rows, capacity, block):
+def grid_rows(got, values, slab_width, row_ids, capacity, block):
     slots_all = got.shape[0]
-    values = got[:, :slab_width]
     slot_ids = jnp.arange(slots_all, dtype=jnp.int32)
-    shift = jnp.where(slot_ids % block >= capacity, tile_rows, 0)
-    corner_row = got[:, slab_width + taps].astype(jnp.int32) - shift
-    corner_col = got[:, slab_width + taps + 1].astype(jnp.int32)
-    rows = jnp.arange(tile_rows, dtype=jnp.int32)
+    shift = jnp.where(slot_ids % block >= capacity, NX // (slots_all // block), 0)
+    corner_row = got[:, slab_width + KSIDE * KSIDE].astype(jnp.int32) - shift
+    corner_col = got[:, slab_width + KSIDE * KSIDE + 1].astype(jnp.int32)
     columns = jnp.arange(NY, dtype=jnp.int32)
-    spread = jnp.zeros((tile_rows, slots_all, NY), jnp.bfloat16)
+    spread = jnp.zeros((NY, row_ids.shape[0], slots_all), jnp.bfloat16)
     for step_a in range(KSIDE):
-        line = jnp.zeros((slots_all, NY), jnp.bfloat16)
+        line = jnp.zeros((NY, slots_all), jnp.bfloat16)
         for step_b in range(KSIDE):
-            placed = columns[None, :] == ((corner_col + step_b) % NY)[:, None]
-            line = jnp.where(placed, got[:, slab_width + step_a * KSIDE + step_b][:, None], line)
-        active = rows[:, None] == (corner_row + step_a)[None, :]
-        spread = jnp.where(active[:, :, None], line[None, :, :], spread)
-    cube_t = jnp.einsum("sw,xsc->wxc", values, spread, preferred_element_type=jnp.float32)
-    cube_t = cube_t.reshape(slab_width, tile_rows * NY)
-    return cube_t.astype(jnp.bfloat16)
+            placed = columns[:, None] == ((corner_col + step_b) % NY)[None, :]
+            tap = got[:, slab_width + step_a * KSIDE + step_b][None, :]
+            line = jnp.where(placed, tap, line)
+        active = row_ids[:, None] == (corner_row + step_a)[None, :]
+        spread = jnp.where(active[None, :, :], line[:, None, :], spread)
+    spread = spread.reshape(NY * row_ids.shape[0], slots_all)
+    return jnp.dot(spread, values, preferred_element_type=jnp.float32).astype(jnp.bfloat16)
 
 
 def shards(spectra, kernel, owner, offset):
@@ -105,22 +103,22 @@
     per_dev = NY // devices
 
     got, capacity, block = route_fibres(spectra, kernel, owner, offset, sky_count)
-    cube_t = grid_tile(got, slab_width, taps, tile_rows, capacity, block)
+    rows_dev = tile_rows // gz_count
+    padded_nw = -(-NW // 128) * 128
+    values = lax.all_gather(got[:, :slab_width], "gz", axis=1, tiled=True)
+    values = jnp.pad(values, ((0, 0), (0, padded_nw - NW)))
+    row_ids = lax.axis_index("gz") * rows_dev + jnp.arange(rows_dev, dtype=jnp.int32)
+    cube_yw = grid_rows(got, values, slab_width, row_ids, capacity, block)
+    cube_yw = cube_yw.reshape(NY, rows_dev, padded_nw)
     steps_y = jnp.arange(NY, dtype=jnp.int32)
     steps_x = jnp.arange(NX, dtype=jnp.int32)
-    cube_t, steps_y, steps_x = lax.optimization_barrier((cube_t, steps_y, steps_x))
-    cube_w = lax.all_to_all(cube_t, "gz", split_axis=1, concat_axis=0, tiled=True)
-    rows_dev = tile_rows // gz_count
-    cube_w = cube_w.reshape(NW, rows_dev, NY)
 
     cos_y, sin_y = dft_tables(NY, steps_y)
     table_y = jnp.concatenate([cos_y, -sin_y], axis=1)
-    padded_nw = -(-NW // 128) * 128
     cos_w, sin_w = twiddles(NW, padded_nw)
     table_x = complex_table(NX, steps_x).reshape(2, devices, rows_dev, 2, NX)
     table_y, cos_w, sin_w, table_x = lax.optimization_barrier((table_y, cos_w, sin_w, table_x))
 
-    cube_yw = jnp.pad(jnp.transpose(cube_w, (2, 1, 0)), ((0, 0), (0, 0), (0, padded_nw - NW)))
     first = jnp.einsum("yxw,yK->xKw", cube_yw, table_y, preferred_element_type=jnp.float32)
     first = first.astype(jnp.bfloat16).reshape(2 * NY * rows_dev, padded_nw)
     by_cos = jnp.dot(first, cos_w, preferred_element_type=jnp.float32)

time: 121 us -> 128 us (1.058)
  between operations: 0.27 us -> 13.6 us
  starting transfers between devices: 15.1 us -> 7.61 us
  waiting for transfers between devices: 11.7 us -> 15.8 us
  matrix products: 19.8 us -> 16.2 us
  blocking collectives: 39.5 us -> 41.1 us
    all_gather x0 -> x1, waiting for transfers between devices: none -> 12.9 us  [shards(): values = lax.all_gather(got[:, :slab_width], 'gz', axis=1, tiled=True)]
    all_to_all x1 -> x0, waiting for transfers between devices: 11 us -> none  [shards(): lax.all_to_all(cube_t, 'gz', split_axis=1, concat_axis=0, tiled=True)]
    all_to_all x1 -> x0, starting transfers between devices: 7.57 us -> none  [shards(): lax.all_to_all(cube_t, 'gz', split_axis=1, concat_axis=0, tiled=True)]
    dot_general x1, matrix products: 5.93 us -> 2.27 us  [grid_rows(): jnp.dot(spread, values, preferred_element_type=jnp.float32)]
    all_to_all x1, waiting for transfers between devices: 0.76 us -> 2.95 us  [route_fibres(): got = lax.all_to_all(send, 'sky', split_axis=0, concat_axis=0, tiled=True)]
    all_to_all x1, blocking collectives: 39.5 us -> 41.1 us  [shards(): lax.all_to_all(second, ('sky', 'gz'), split_axis=0, concat_axis=0, tiled=...]
    unnamed x8, local copies, waits for them, and re-layouts: 4.34 us -> 5.94 us
    reshape x2 -> x1, local copies, waits for them, and re-layouts: 2.27 us -> 0.67 us  [shards(): cube_yw = cube_yw.reshape(NY, rows_dev, padded_nw)]
  transfers between devices with their start and end apart: 2 -> 2, of which waited for: 2 -> 2; matrix products, arithmetic and copies ran while one was open for 10% -> 14% of each run, Pallas kernels for 0% -> 0%
where the time goes in v6:
time: 128 us; the launch traced here: 127 us
  blocking collectives  41.1 us (32%)
  other arithmetic  17.7 us (14%)
  matrix products  16.2 us (13%)
  waiting for transfers between devices  15.8 us (12%)
  local copies, waits for them, and re-layouts  15.4 us (12%)
  between operations  13.6 us (11%)
  starting transfers between devices  7.61 us (6%)
    all_to_all x1, blocking collectives, shards(): lax.all_to_all(second, ('sky', 'gz'), split_axis=0, concat_axis=0, tiled=...  41.1 us
    all_gather x1, waiting for transfers between devices, shards(): values = lax.all_gather(got[:, :slab_width], 'gz', axis=1, tiled=True)  12.9 us
    all_to_all x1, starting transfers between devices, route_fibres(): got = lax.all_to_all(send, 'sky', split_axis=0, concat_axis=0, tiled=True)  7.57 us
    unnamed x8, local copies, waits for them, and re-layouts  5.94 us
    dot_general x1, matrix products, shards(): jnp.einsum('sqxRv,RsxUu->Uuqv', pencils, table_x, preferred_element_type=...  4.88 us
    convert_element_type x1, other arithmetic, twiddles(): sin_t = jnp.where(inside, sin_t * factor, 0.0).astype(jnp.bfloat16)  4.57 us
    dot_general x1, matrix products, shards(): by_cos = jnp.dot(first, cos_w, preferred_element_type=jnp.float32)  3.51 us
    dot_general x1, matrix products, shards(): by_sin = jnp.dot(first, sin_w, preferred_element_type=jnp.float32)  3.51 us
  transfers between devices with their start and end apart: 2, of which 2 were waited for; matrix products, arithmetic and copies ran while one was open for 14% of the time, Pallas kernels for 0%

profile of v6, /device:TPU:1, one launch (start us, length us, event | category | flops | bytes accessed | tf_op | source)
XLA Modules:
  0.0 127.4 jit_solution(12145881123623862706)
XLA Ops:
  6.5 0.9 convert_reduce_fusion.2
  7.5 0.7 multiply_add_fusion
  8.2 0.7 fusion.78
  8.9 1.2 convolution_convert_fusion.2
  10.1 0.9 copy.38
  11.0 7.6 %all-to-all-start = ((bf16[16,40,147]{2,1,0:T(8,128)(2,1)}), bf16[16,40,147]{2,1,0:T(8,128)(2,1)S(1)}, u32[]{:S(2)}, u32[]{:S(2)}) async-start(bf16[16,40,147]{2,1,0:T(8,128)(2,1)} %bitcast.5), calls=%async_computation | async-start | bytes 655360 | tf_op jit(solution)/shard_map/all_to_all | solution.py:72
  18.5 0.0 all-gather.3.cloned.1.call-start
  18.6 0.3 fusion.61
  18.9 1.4 %fusion.38 = (f32[72,1152]{1,0:T(8,128)S(1)}, f32[72,1152]{1,0:T(8,128)S(1)}) fusion(s32[72]{0:T(128)S(1)} %iota_multiply_fusion), kind=kLoop, calls=%fused_computation.65 | loop fusion | flops 746496 | bytes 663840 | tf_op jit(solution)/shard_map/cos | solution.py:32
  20.3 3.1 %add_multiply_fusion = (bf16[72,16,1152]{2,1,0:T(8,128)(2,1)S(1)}, bf16[72,16,1152]{2,1,0:T(8,128)(2,1)}) fusion(f32[16,1152]{1,0:T(8,128)S(1)} %get-tuple-element.60, f32[72,1152]{1,0:T(8,128)S(1)} %get-tuple-element.51, f32[16,1152]{1,0:T(8,128)S(1)} %get-tuple-element.61, f32[72,1152]{1,0:T(8,128)S(1)} %get-tuple-element.50), kind=kLoop, calls=%fused_computation.4 | loop fusion | flops 13271040 | bytes 6119424 | tf_op jit(solution)/shard_map/mul | solution.py:41
  23.4 2.9 %all-to-all-done = bf16[16,40,147]{2,1,0:T(8,128)(2,1)S(1)} async-done(((bf16[16,40,147]{2,1,0:T(8,128)(2,1)}), bf16[16,40,147]{2,1,0:T(8,128)(2,1)S(1)}, u32[]{:S(2)}, u32[]{:S(2)}) %all-to-all-start) | async-done | bytes 188192 | tf_op jit(solution)/shard_map/all_to_all | solution.py:72
  26.4 0.8 copy.39
  27.2 0.0 all-gather.3.cloned.1.call-update
  27.3 4.6 %fusion.1 = (bf16[1152,1152]{1,0:T(8,128)(2,1)}, bf16[1152,1152]{1,0:T(8,128)(2,1)}) fusion(bf16[72,16,1152]{2,1,0:T(8,128)(2,1)S(1)} %get-tuple-element.31, pred[1152]{0:T(1024)(128)(4,1)S(1)} %iota_compare_fusion.8, bf16[72,16,1152]{2,1,0:T(8,128)(2,1)} %get-tuple-element.32), kind=kLoop, calls=%fused_computation.3 | loop fusion | flops 3981312 | bytes 10617984 | tf_op jit(solution)/shard_map/convert_element_type | solution.py:41
  31.8 1.0 fusion.64
  32.8 1.1 multiply_convert_fusion
  34.0 0.1 reshape.915
  34.2 0.3 convert_reduce_fusion
  34.5 1.5 %slice_reduce_fusion.15 = (bf16[640]{0:T(1024)(128)(2,1)S(1)}, bf16[640]{0:T(1024)(128)(2,1)S(1)}, bf16[640]{0:T(1024)(128)(2,1)S(1)}, bf16[640]{0:T(1024)(128)(...) fusion(bf16[640,147]{1,0:T(8,128)(2,1)S(1)} %bitcast.63), kind=kLoop, calls=%fused_computation.100 | loop fusion | bytes 40960 | tf_op jit(solution)/shard_map/slice | solution.py:88
  36.0 0.1 broadcast_compare_fusion
  36.1 0.2 fusion.28
  36.4 0.5 fusion.29
  36.9 1.8 %broadcast_select_fusion.3 = bf16[256,2,640]{2,1,0:T(2,128)(2,1)S(1)} fusion(pred[2,640]{1,0:T(4,128)(4,1)S(1)} %get-tuple-element.55, pred[2,640]{1,0:T(4,128)(4,1)S(1)} %get-tuple-element.53, pred[2,640]{1,0:T(4,128)(4,1)S(1)} %get-tuple-element.54, pred[2,640]{1,0:T(4,128)(4,1)S(1)} %get-tuple-element.52, bf16[256,640]{1,0:T(8,128)(2,1)S(1)} %get-tuple-element.34, ...), kind=kLoop, calls=%fused_computation.25 | loop fusion | flops 1310720 | bytes 1971200 | tf_op jit(solution)/shard_map/jit(_where)/select_n | solution.py:91
  38.7 1.1 select_n.333
  39.8 12.9 %all-gather.3.cloned.1.call-done = bf16[8,129,640]{2,1,0:T(8,128)(2,1)} async-done(((bf16[1,129,640]{2,1,0:T(8,128)(2,1)}), bf16[8,129,640]{2,1,0:T(8,128)(2,1)}) %all-gather.3.cloned.1.call-update) | async-done | bytes 1320976 | tf_op jit(solution)/shard_map/all_gather | solution.py:108
  52.7 1.7 %reshape.924 = bf16[1032,640]{1,0:T(8,128)(2,1)S(1)} reshape(bf16[8,129,640]{2,1,0:T(8,128)(2,1)} %all-gather.3.cloned.1.call-done) | data formatting | bytes 2641920
  54.4 2.3 %convolution_convert_fusion.1 = bf16[512,1152]{1,0:T(8,128)(2,1)S(1)} fusion(bf16[512,640]{1,0:T(8,128)(2,1)} %select_n.333, bf16[640,1032]{0,1:T(8,128)(2,1)S(1)} %bitcast.68), kind=kOutput, calls=%fused_computation.8 | convolution fusion | flops 755564544 | bytes 3155968 | tf_op jit(solution)/shard_map/dot_general | solution.py:93
  56.7 0.7 reshape.918
  57.4 0.0 copy-start.1
  57.4 0.8 convolution_convert_fusion
  58.2 0.9 copy-done.1
  59.1 0.0 copy-start
  59.1 3.5 %fusion.2 = f32[2,2,256,1152]{3,2,1,0:T(8,128)S(1)} fusion(bf16[2,2,256,1152]{3,2,1,0:T(8,128)(2,1)S(1)} %bitcast.65, bf16[1152,1152]{1,0:T(8,128)(2,1)S(1)} %copy-done.1), kind=kOutput, calls=%fused_computation.9 | convolution fusion | flops 2717908992 | bytes 9732096 | tf_op jit(solution)/shard_map/dot_general | solution.py:125
  62.6 0.0 copy-done
  62.6 3.5 %fusion.4 = f32[2,2,256,1152]{3,2,1,0:T(8,128)S(1)} fusion(bf16[2,2,256,1152]{3,2,1,0:T(8,128)(2,1)S(1)} %bitcast.66, bf16[1152,1152]{1,0:T(8,128)(2,1)S(1)} %copy-done), kind=kOutput, calls=%fused_computation.11 | convolution fusion | flops 2717908992 | bytes 9732096 | tf_op jit(solution)/shard_map/dot_general | solution.py:124
  66.1 0.3 fusion.12
  66.5 0.2 fusion.11
  66.7 0.2 maximum_bitcast_fusion
  67.0 2.4 %copy.44 = bf16[256,2,2,1152]{3,2,1,0:T(2,128)(2,1)S(1)} copy(bf16[256,2,2,1152]{3,0,1,2:T(8,128)(2,1)S(1)} %maximum_bitcast_fusion) | data formatting | bytes 4718592 | tf_op jit(solution)/shard_map/convert_element_type | solution.py:130
  69.4 2.3 %reshape.919 = bf16[128,8,1152]{2,1,0:T(8,128)(2,1)} reshape(bf16[256,2,2,1152]{3,2,1,0:T(2,128)(2,1)S(1)} %copy.44) | data formatting | bytes 4718592 | tf_op jit(solution)/shard_map/reshape | solution.py:130
  71.7 41.1 %all_to_all.10 = bf16[128,8,1152]{2,1,0:T(8,128)(2,1)S(1)} all-to-all(bf16[128,8,1152]{2,1,0:T(8,128)(2,1)} %reshape.919), channel_id=1, replica_groups=mesh['sky'=16,'gz'=8] {'sky','gz'}, dimensions={0} | all-to-all | bytes 4718592 | tf_op jit(solution)/shard_map/all_to_all | solution.py:131
  112.9 0.4 copy.45
  113.3 2.4 %copy.58 = bf16[128,2,2,2,1032]{0,4,2,3,1:T(8,128)(2,1)} copy(bf16[128,2,2,2,1032]{4,0,3,2,1:T(8,128)(2,1)S(1)} %bitcast.64) | data formatting | bytes 4227072
  115.7 4.9 %convolution_bitcast_fusion = f32[2,256,2,1032]{1,3,2,0:T(8,128)} fusion(bf16[128,2,2,2,1032]{0,4,2,3,1:T(8,128)(2,1)} %copy.58, bf16[2,128,2,2,256,1]{4,3,2,1,0,5:T(2,128)(2,1)S(1)} %bitcast.67), kind=kOutput, calls=%fused_computation.6 | convolution fusion | flops 1082130432 | bytes 6864896 | tf_op jit(solution)/shard_map/sqxRv,RsxUu->Uuqv/dot_general | solution.py:133
  (9 shorter events, 0.1 us)
Async XLA Ops:
  11.0 15.4 %all-to-all-start = ((bf16[16,40,147]{2,1,0:T(8,128)(2,1)}), bf16[16,40,147]{2,1,0:T(8,128)(2,1)S(1)}, u32[]{:S(2)}, u32[]{:S(2)}) async-start(bf16[16,40,147]{2,1,0:T(8,128)(2,1)} %bitcast.5), calls=%async_computation | async-start | bytes 655360 | tf_op jit(solution)/shard_map/all_to_all | solution.py:72
  18.5 34.1 %all-gather.3.cloned.1.call-start = ((), (), s32[]{:S(2)}) async-start(), calls=%async_computation.2 | async-start | bytes 1566720 | tf_op jit(solution)/shard_map/all_gather | solution.py:108
  57.4 1.8 %copy-start.1 = (bf16[1152,1152]{1,0:T(8,128)(2,1)S(1)}, bf16[1152,1152]{1,0:T(8,128)(2,1)}, u32[]{:S(2)}) copy-start(bf16[1152,1152]{1,0:T(8,128)(2,1)} %get-tuple-element.12) | copy-start | bytes 7962628
  59.1 3.5 %copy-start = (bf16[1152,1152]{1,0:T(8,128)(2,1)S(1)}, bf16[1152,1152]{1,0:T(8,128)(2,1)}, u32[]{:S(2)}) copy-start(bf16[1152,1152]{1,0:T(8,128)(2,1)} %get-tuple-element.11) | copy-start | bytes 7962628
Sparse Core Ops, SparseCore 0:
  27.4 25.2 all-gather.2

commit v7 on v6

--- a/solution.py
+++ b/solution.py
@@ -73,7 +73,7 @@
     return got.reshape(slots_all, packed.shape[1]), capacity, block
 
 
-def grid_rows(got, values, slab_width, row_ids, capacity, block):
+def grid_rows(got, values_t, slab_width, row_ids, capacity, block):
     slots_all = got.shape[0]
     slot_ids = jnp.arange(slots_all, dtype=jnp.int32)
     shift = jnp.where(slot_ids % block >= capacity, NX // (slots_all // block), 0)
@@ -90,7 +90,10 @@
         active = row_ids[:, None] == (corner_row + step_a)[None, :]
         spread = jnp.where(active[None, :, :], line[:, None, :], spread)
     spread = spread.reshape(NY * row_ids.shape[0], slots_all)
-    return jnp.dot(spread, values, preferred_element_type=jnp.float32).astype(jnp.bfloat16)
+    cube = lax.dot_general(
+        spread, values_t, (((1,), (1,)), ((), ())), preferred_element_type=jnp.float32
+    )
+    return cube.astype(jnp.bfloat16)
 
 
 def shards(spectra, kernel, owner, offset):
@@ -105,10 +108,12 @@
     got, capacity, block = route_fibres(spectra, kernel, owner, offset, sky_count)
     rows_dev = tile_rows // gz_count
     padded_nw = -(-NW // 128) * 128
-    values = lax.all_gather(got[:, :slab_width], "gz", axis=1, tiled=True)
-    values = jnp.pad(values, ((0, 0), (0, padded_nw - NW)))
+    values_t = jnp.transpose(got[:, :slab_width])
+    copies = jnp.broadcast_to(values_t[None], (gz_count,) + values_t.shape)
+    values_t = lax.all_to_all(copies, "gz", split_axis=0, concat_axis=0, tiled=True)
+    values_t = jnp.pad(values_t.reshape(NW, -1), ((0, padded_nw - NW), (0, 0)))
     row_ids = lax.axis_index("gz") * rows_dev + jnp.arange(rows_dev, dtype=jnp.int32)
-    cube_yw = grid_rows(got, values, slab_width, row_ids, capacity, block)
+    cube_yw = grid_rows(got, values_t, slab_width, row_ids, capacity, block)
     cube_yw = cube_yw.reshape(NY, rows_dev, padded_nw)
     steps_y = jnp.arange(NY, dtype=jnp.int32)
     steps_x = jnp.arange(NX, dtype=jnp.int32)

time: 128 us -> 117 us (0.914)
  between operations: 13.6 us -> 0.24 us
  starting transfers between devices: 7.61 us -> 13.8 us
  waiting for transfers between devices: 15.8 us -> 13.4 us
  other arithmetic: 17.7 us -> 15.4 us
    all_to_all x0 -> x1, waiting for transfers between devices: none -> 13.4 us  [shards(): lax.all_to_all(copies, 'gz', split_axis=0, concat_axis=0, tiled=True)]
    all_gather x1 -> x0, waiting for transfers between devices: 12.9 us -> none  [shards(): values = lax.all_gather(got[:, :slab_width], 'gz', axis=1, tiled=True)]
    all_to_all x0 -> x1, starting transfers between devices: none -> 6.26 us  [shards(): lax.all_to_all(copies, 'gz', split_axis=0, concat_axis=0, tiled=True)]
    all_to_all x1, waiting for transfers between devices: 2.95 us -> 0.01 us  [route_fibres(): got = lax.all_to_all(send, 'sky', split_axis=0, concat_axis=0, tiled=True)]
    unnamed x8 -> x5, local copies, waits for them, and re-layouts: 5.94 us -> 3.37 us
    reshape x0 -> x1, local copies, waits for them, and re-layouts: none -> 1.48 us  [shards(): values_t = jnp.pad(values_t.reshape(NW, -1), ((0, padded_nw - NW), (0, 0)))]
    convert_element_type x1, other arithmetic: 4.57 us -> 3.27 us  [twiddles(): sin_t = jnp.where(inside, sin_t * factor, 0.0).astype(jnp.bfloat16)]
  transfers between devices with their start and end apart: 2 -> 2, of which waited for: 2 -> 1; matrix products, arithmetic and copies ran while one was open for 14% -> 13% of each run, Pallas kernels for 0% -> 0%
where the time goes in v7:
time: 117 us
  blocking collectives  41.5 us (35%)
  matrix products  16.6 us (14%)
  local copies, waits for them, and re-layouts  15.7 us (13%)
  other arithmetic  15.4 us (13%)
  starting transfers between devices  13.8 us (12%)
  waiting for transfers between devices  13.4 us (11%)
    all_to_all x1, blocking collectives, shards(): lax.all_to_all(second, ('sky', 'gz'), split_axis=0, concat_axis=0, tiled=...  41.5 us
    all_to_all x1, waiting for transfers between devices, shards(): lax.all_to_all(copies, 'gz', split_axis=0, concat_axis=0, tiled=True)  13.4 us
    all_to_all x1, starting transfers between devices, route_fibres(): got = lax.all_to_all(send, 'sky', split_axis=0, concat_axis=0, tiled=True)  7.57 us
    all_to_all x1, starting transfers between devices, shards(): lax.all_to_all(copies, 'gz', split_axis=0, concat_axis=0, tiled=True)  6.26 us
    dot_general x1, matrix products, shards(): jnp.einsum('sqxRv,RsxUu->Uuqv', pencils, table_x, preferred_element_type=...  4.88 us
    dot_general x1, matrix products, shards(): by_cos = jnp.dot(first, cos_w, preferred_element_type=jnp.float32)  3.51 us
    dot_general x1, matrix products, shards(): by_sin = jnp.dot(first, sin_w, preferred_element_type=jnp.float32)  3.51 us
    unnamed x5, local copies, waits for them, and re-layouts  3.37 us
  transfers between devices with their start and end apart: 2, of which 1 were waited for; matrix products, arithmetic and copies ran while one was open for 13% of the time, Pallas kernels for 0%

profile of v7, /device:TPU:1, one launch (start us, length us, event | category | flops | bytes accessed | tf_op | source)
XLA Modules:
  0.0 116.6 jit_solution(4593730185088736318)
XLA Ops:
  0.0 0.9 convert_reduce_fusion.2
  0.9 0.7 multiply_add_fusion
  1.6 0.7 fusion.78
  2.3 1.2 %convolution_convert_fusion.2 = bf16[640,147]{0,1:T(8,128)(2,1)S(1)} fusion(s32[256]{0:T(256)S(1)} %get-tuple-element.47, s32[256]{0:T(256)S(1)} %get-tuple-element.46, bf16[256,1]{0,1:T(2,128)(2,1)S(1)} %broadcast_in_dim.257, bf16[256,1]{0,1:T(2,128)(2,1)S(1)} %broadcast_in_dim.256, bf16[256,16]{0,1:T(8,128)(2,1)} %param.5, bf16[256,129]{0,1:T(8,128)(2,1)} %param.4), kind=kOutput, calls=%fused_computation.29 | convolution fusion | flops 49055616 | bytes 265472 | tf_op jit(solution)/shard_map/dot_general | solution.py:70
  3.5 0.9 copy.28
  4.4 7.6 %all-to-all-start = ((bf16[16,40,147]{2,1,0:T(8,128)(2,1)}), bf16[16,40,147]{2,1,0:T(8,128)(2,1)S(1)}, u32[]{:S(2)}, u32[]{:S(2)}) async-start(bf16[16,40,147]{2,1,0:T(8,128)(2,1)} %bitcast.5), calls=%async_computation | async-start | bytes 655360 | tf_op jit(solution)/shard_map/all_to_all | solution.py:72
  12.1 1.0 fusion.64
  13.1 0.3 fusion.61
  13.4 1.1 multiply_convert_fusion
  14.5 0.1 reshape.919
  14.7 1.4 %fusion.38 = (f32[72,1152]{1,0:T(8,128)S(1)}, f32[72,1152]{1,0:T(8,128)S(1)}) fusion(s32[72]{0:T(128)S(1)} %iota_multiply_fusion), kind=kLoop, calls=%fused_computation.65 | loop fusion | flops 746496 | bytes 663840 | tf_op jit(solution)/shard_map/cos | solution.py:32
  16.1 2.1 %add_multiply_fusion = (bf16[72,16,1152]{2,1,0:T(8,128)(2,1)S(1)}, bf16[72,16,1152]{2,1,0:T(8,128)(2,1)S(1)}) fusion(f32[16,1152]{1,0:T(8,128)S(1)} %get-tuple-element.60, f32[72,1152]{1,0:T(8,128)S(1)} %get-tuple-element.51, f32[16,1152]{1,0:T(8,128)S(1)} %get-tuple-element.61, f32[72,1152]{1,0:T(8,128)S(1)} %get-tuple-element.50), kind=kLoop, calls=%fused_computation.4 | loop fusion | flops 13271040 | bytes 6119424 | tf_op jit(solution)/shard_map/mul | solution.py:41
  18.1 3.3 %fusion.1 = (bf16[1152,1152]{1,0:T(8,128)(2,1)}, bf16[1152,1152]{1,0:T(8,128)(2,1)}) fusion(bf16[72,16,1152]{2,1,0:T(8,128)(2,1)S(1)} %get-tuple-element.31, pred[1152]{0:T(1024)(128)(4,1)S(1)} %iota_compare_fusion.8, bf16[72,16,1152]{2,1,0:T(8,128)(2,1)S(1)} %get-tuple-element.32), kind=kLoop, calls=%fused_computation.3 | loop fusion | flops 3981312 | bytes 10617984 | tf_op jit(solution)/shard_map/convert_element_type | solution.py:41
  21.4 0.0 all-to-all-done
  21.5 0.3 convert_reduce_fusion
  21.8 0.2 copy.29
  22.0 1.2 %broadcast_in_dim.300 = bf16[8,129,640]{2,1,0:T(8,128)(2,1)} broadcast(bf16[129,640]{1,0:T(8,128)(2,1)S(1)} %copy.29), dimensions={1,2} | broadcast | bytes 1486080 | tf_op jit(solution)/shard_map/broadcast_in_dim | solution.py:112
  23.2 6.3 %all-to-all-start.1 = ((bf16[8,129,640]{2,1,0:T(8,128)(2,1)}), bf16[8,129,640]{2,1,0:T(8,128)(2,1)S(1)}, u32[]{:S(2)}, u32[]{:S(2)}) async-start(bf16[8,129,640]{2,1,0:T(8,128)(2,1)} %broadcast_in_dim.300), calls=%async_computation.1 | async-start | bytes 2785280 | tf_op jit(solution)/shard_map/all_to_all | solution.py:113
  29.5 0.1 broadcast_compare_fusion
  29.6 1.5 %slice_reduce_fusion.15 = (bf16[640]{0:T(1024)(128)(2,1)S(1)}, bf16[640]{0:T(1024)(128)(2,1)S(1)}, bf16[640]{0:T(1024)(128)(2,1)S(1)}, bf16[640]{0:T(1024)(128)(...) fusion(bf16[640,147]{1,0:T(8,128)(2,1)S(1)} %bitcast.60), kind=kLoop, calls=%fused_computation.100 | loop fusion | bytes 40960 | tf_op jit(solution)/shard_map/slice | solution.py:88
  31.1 0.2 fusion.28
  31.3 0.5 fusion.29
  31.8 1.8 %broadcast_select_fusion.3 = bf16[256,2,640]{2,1,0:T(2,128)(2,1)S(1)} fusion(pred[2,640]{1,0:T(4,128)(4,1)S(1)} %get-tuple-element.55, pred[2,640]{1,0:T(4,128)(4,1)S(1)} %get-tuple-element.53, pred[2,640]{1,0:T(4,128)(4,1)S(1)} %get-tuple-element.54, pred[2,640]{1,0:T(4,128)(4,1)S(1)} %get-tuple-element.52, bf16[256,640]{1,0:T(8,128)(2,1)S(1)} %get-tuple-element.34, ...), kind=kLoop, calls=%fused_computation.25 | loop fusion | flops 1310720 | bytes 1971200 | tf_op jit(solution)/shard_map/jit(_where)/select_n | solution.py:91
  33.7 1.1 select_n.333
  34.8 13.4 %all-to-all-done.1 = bf16[8,129,640]{2,1,0:T(8,128)(2,1)S(1)} async-done(((bf16[8,129,640]{2,1,0:T(8,128)(2,1)}), bf16[8,129,640]{2,1,0:T(8,128)(2,1)S(1)}, u32[]{:S(2)}, u32[]{:S(2)}) %all-to-all-start.1) | async-done | bytes 1320992 | tf_op jit(solution)/shard_map/all_to_all | solution.py:113
  48.1 1.5 %reshape.922 = bf16[1032,640]{1,0:T(8,128)(2,1)} reshape(bf16[8,129,640]{2,1,0:T(8,128)(2,1)S(1)} %all-to-all-done.1) | data formatting | bytes 2641920 | tf_op jit(solution)/shard_map/reshape | solution.py:114
  49.6 2.7 %convolution_convert_fusion.1 = bf16[512,1152]{1,0:T(8,128)(2,1)S(1)} fusion(bf16[512,640]{1,0:T(8,128)(2,1)} %select_n.333, bf16[1032,640]{1,0:T(8,128)(2,1)} %reshape.922), kind=kOutput, calls=%fused_computation.8 | convolution fusion | flops 755564544 | bytes 3155968 | tf_op jit(solution)/shard_map/dot_general | solution.py:93
  52.3 0.7 reshape.923
  53.0 0.0 copy-start.1
  53.0 0.8 convolution_convert_fusion
  53.9 0.9 copy-done.1
  54.8 0.0 copy-start
  54.8 3.5 %fusion.2 = f32[2,2,256,1152]{3,2,1,0:T(8,128)S(1)} fusion(bf16[2,2,256,1152]{3,2,1,0:T(8,128)(2,1)S(1)} %bitcast.62, bf16[1152,1152]{1,0:T(8,128)(2,1)S(1)} %copy-done.1), kind=kOutput, calls=%fused_computation.9 | convolution fusion | flops 2717908992 | bytes 9732096 | tf_op jit(solution)/shard_map/dot_general | solution.py:130
  58.3 0.0 copy-done
  58.3 3.5 %fusion.4 = f32[2,2,256,1152]{3,2,1,0:T(8,128)S(1)} fusion(bf16[2,2,256,1152]{3,2,1,0:T(8,128)(2,1)S(1)} %bitcast.63, bf16[1152,1152]{1,0:T(8,128)(2,1)S(1)} %copy-done), kind=kOutput, calls=%fused_computation.11 | convolution fusion | flops 2717908992 | bytes 9732096 | tf_op jit(solution)/shard_map/dot_general | solution.py:129
  61.8 0.3 fusion.12
  62.2 0.2 fusion.11
  62.4 0.2 maximum_bitcast_fusion
  62.7 2.4 %copy.34 = bf16[256,2,2,1152]{3,2,1,0:T(2,128)(2,1)S(1)} copy(bf16[256,2,2,1152]{3,0,1,2:T(8,128)(2,1)S(1)} %maximum_bitcast_fusion) | data formatting | bytes 4718592 | tf_op jit(solution)/shard_map/convert_element_type | solution.py:135
  65.1 2.3 %reshape.924 = bf16[128,8,1152]{2,1,0:T(8,128)(2,1)} reshape(bf16[256,2,2,1152]{3,2,1,0:T(2,128)(2,1)S(1)} %copy.34) | data formatting | bytes 4718592 | tf_op jit(solution)/shard_map/reshape | solution.py:135
  67.4 41.5 %all_to_all.15 = bf16[128,8,1152]{2,1,0:T(8,128)(2,1)S(1)} all-to-all(bf16[128,8,1152]{2,1,0:T(8,128)(2,1)} %reshape.924), channel_id=1, replica_groups=mesh['sky'=16,'gz'=8] {'sky','gz'}, dimensions={0} | all-to-all | bytes 4718592 | tf_op jit(solution)/shard_map/all_to_all | solution.py:136
  108.9 0.4 copy.35
  109.3 2.4 %copy.48 = bf16[128,2,2,2,1032]{0,4,2,3,1:T(8,128)(2,1)} copy(bf16[128,2,2,2,1032]{4,0,3,2,1:T(8,128)(2,1)S(1)} %bitcast.61) | data formatting | bytes 4227072
  111.7 4.9 %convolution_bitcast_fusion = f32[2,256,2,1032]{1,3,2,0:T(8,128)} fusion(bf16[128,2,2,2,1032]{0,4,2,3,1:T(8,128)(2,1)} %copy.48, bf16[2,128,2,2,256,1]{4,3,2,1,0,5:T(2,128)(2,1)S(1)} %bitcast.64), kind=kOutput, calls=%fused_computation.6 | convolution fusion | flops 1082130432 | bytes 6864896 | tf_op jit(solution)/shard_map/sqxRv,RsxUu->Uuqv/dot_general | solution.py:138
  (9 shorter events, 0.1 us)
Async XLA Ops:
  4.4 17.0 %all-to-all-start = ((bf16[16,40,147]{2,1,0:T(8,128)(2,1)}), bf16[16,40,147]{2,1,0:T(8,128)(2,1)S(1)}, u32[]{:S(2)}, u32[]{:S(2)}) async-start(bf16[16,40,147]{2,1,0:T(8,128)(2,1)} %bitcast.5), calls=%async_computation | async-start | bytes 655360 | tf_op jit(solution)/shard_map/all_to_all | solution.py:72
  23.2 24.9 %all-to-all-start.1 = ((bf16[8,129,640]{2,1,0:T(8,128)(2,1)}), bf16[8,129,640]{2,1,0:T(8,128)(2,1)S(1)}, u32[]{:S(2)}, u32[]{:S(2)}) async-start(bf16[8,129,640]{2,1,0:T(8,128)(2,1)} %broadcast_in_dim.300), calls=%async_computation.1 | async-start | bytes 2785280 | tf_op jit(solution)/shard_map/all_to_all | solution.py:113
  53.0 1.8 %copy-start.1 = (bf16[1152,1152]{1,0:T(8,128)(2,1)S(1)}, bf16[1152,1152]{1,0:T(8,128)(2,1)}, u32[]{:S(2)}) copy-start(bf16[1152,1152]{1,0:T(8,128)(2,1)} %get-tuple-element.12) | copy-start | bytes 7962628
  54.8 3.5 %copy-start = (bf16[1152,1152]{1,0:T(8,128)(2,1)S(1)}, bf16[1152,1152]{1,0:T(8,128)(2,1)}, u32[]{:S(2)}) copy-start(bf16[1152,1152]{1,0:T(8,128)(2,1)} %get-tuple-element.11) | copy-start | bytes 7962628

commit v8 on v7

--- a/solution.py
+++ b/solution.py
@@ -110,13 +110,14 @@
     padded_nw = -(-NW // 128) * 128
     values_t = jnp.transpose(got[:, :slab_width])
     copies = jnp.broadcast_to(values_t[None], (gz_count,) + values_t.shape)
+    steps_y = jnp.arange(NY, dtype=jnp.int32)
+    steps_x = jnp.arange(NX, dtype=jnp.int32)
+    copies, steps_y, steps_x = lax.optimization_barrier((copies, steps_y, steps_x))
     values_t = lax.all_to_all(copies, "gz", split_axis=0, concat_axis=0, tiled=True)
     values_t = jnp.pad(values_t.reshape(NW, -1), ((0, padded_nw - NW), (0, 0)))
     row_ids = lax.axis_index("gz") * rows_dev + jnp.arange(rows_dev, dtype=jnp.int32)
     cube_yw = grid_rows(got, values_t, slab_width, row_ids, capacity, block)
     cube_yw = cube_yw.reshape(NY, rows_dev, padded_nw)
-    steps_y = jnp.arange(NY, dtype=jnp.int32)
-    steps_x = jnp.arange(NX, dtype=jnp.int32)
 
     cos_y, sin_y = dft_tables(NY, steps_y)
     table_y = jnp.concatenate([cos_y, -sin_y], axis=1)

time: 117 us -> 116 us (level)
  waiting for transfers between devices: 13.4 us -> 10.9 us
  other arithmetic: 15.4 us -> 17.8 us
  blocking collectives: 41.5 us -> 39.5 us
  starting transfers between devices: 13.8 us -> 15.1 us
    all_to_all x1, waiting for transfers between devices: 13.4 us -> 10.2 us  [shards(): lax.all_to_all(copies, 'gz', split_axis=0, concat_axis=0, tiled=True)]
    all_to_all x1, blocking collectives: 41.5 us -> 39.5 us  [shards(): lax.all_to_all(second, ('sky', 'gz'), split_axis=0, concat_axis=0, tiled=...]
    all_to_all x1, starting transfers between devices: 6.26 us -> 7.58 us  [shards(): lax.all_to_all(copies, 'gz', split_axis=0, concat_axis=0, tiled=True)]
    neg x1, other arithmetic: 0.99 us -> 2.17 us  [shards(): table_y = jnp.concatenate([cos_y, -sin_y], axis=1)]
  transfers between devices with their start and end apart: 2 -> 2, of which waited for: 1 -> 2; matrix products, arithmetic and copies ran while one was open for 13% -> 13% of each run, Pallas kernels for 0% -> 0%
where the time goes in v8:
time: 116 us
  blocking collectives  39.5 us (34%)
  other arithmetic  17.8 us (15%)
  matrix products  16.6 us (14%)
  local copies, waits for them, and re-layouts  15.7 us (14%)
  starting transfers between devices  15.1 us (13%)
  waiting for transfers between devices  10.9 us (9%)
    all_to_all x1, blocking collectives, shards(): lax.all_to_all(second, ('sky', 'gz'), split_axis=0, concat_axis=0, tiled=...  39.5 us
    all_to_all x1, waiting for transfers between devices, shards(): lax.all_to_all(copies, 'gz', split_axis=0, concat_axis=0, tiled=True)  10.2 us
    all_to_all x1, starting transfers between devices, shards(): lax.all_to_all(copies, 'gz', split_axis=0, concat_axis=0, tiled=True)  7.58 us
    all_to_all x1, starting transfers between devices, route_fibres(): got = lax.all_to_all(send, 'sky', split_axis=0, concat_axis=0, tiled=True)  7.57 us
    dot_general x1, matrix products, shards(): jnp.einsum('sqxRv,RsxUu->Uuqv', pencils, table_x, preferred_element_type=...  4.88 us
    dot_general x1, matrix products, shards(): by_cos = jnp.dot(first, cos_w, preferred_element_type=jnp.float32)  3.51 us
    dot_general x1, matrix products, shards(): by_sin = jnp.dot(first, sin_w, preferred_element_type=jnp.float32)  3.49 us
    unnamed x5, local copies, waits for them, and re-layouts  3.37 us
  transfers between devices with their start and end apart: 2, of which 2 were waited for; matrix products, arithmetic and copies ran while one was open for 13% of the time, Pallas kernels for 0%

profile of v8, /device:TPU:1, one launch (start us, length us, event | category | flops | bytes accessed | tf_op | source)
XLA Modules:
  0.0 115.8 jit_solution(6961797334764043085)
XLA Ops:
  0.0 0.9 convert_reduce_fusion.2
  0.9 0.7 multiply_add_fusion
  1.6 0.7 fusion.79
  2.3 1.2 %convolution_convert_fusion.2 = bf16[640,147]{0,1:T(8,128)(2,1)S(1)} fusion(s32[256]{0:T(256)S(1)} %get-tuple-element.53, s32[256]{0:T(256)S(1)} %get-tuple-element.52, bf16[256,1]{0,1:T(2,128)(2,1)S(1)} %broadcast_in_dim.256, bf16[256,1]{0,1:T(2,128)(2,1)S(1)} %broadcast_in_dim.255, bf16[256,16]{0,1:T(8,128)(2,1)} %param.5, bf16[256,129]{0,1:T(8,128)(2,1)} %param.4), kind=kOutput, calls=%fused_computation.29 | convolution fusion | flops 49055616 | bytes 265472 | tf_op jit(solution)/shard_map/dot_general | solution.py:70
  3.5 0.9 copy.28
  4.4 7.6 %all-to-all-start = ((bf16[16,40,147]{2,1,0:T(8,128)(2,1)}), bf16[16,40,147]{2,1,0:T(8,128)(2,1)S(1)}, u32[]{:S(2)}, u32[]{:S(2)}) async-start(bf16[16,40,147]{2,1,0:T(8,128)(2,1)} %bitcast.1), calls=%async_computation | async-start | bytes 655360 | tf_op jit(solution)/shard_map/all_to_all | solution.py:72
  12.1 0.3 fusion.62
  12.4 1.4 %fusion.38 = (f32[72,1152]{1,0:T(8,128)S(1)}, f32[72,1152]{1,0:T(8,128)S(1)}) fusion(s32[72]{0:T(128)S(1)} %iota_multiply_fusion), kind=kLoop, calls=%fused_computation.72 | loop fusion | flops 746496 | bytes 663840 | tf_op jit(solution)/shard_map/cos | solution.py:32
  13.8 2.1 %add_multiply_fusion = (bf16[72,16,1152]{2,1,0:T(8,128)(2,1)S(1)}, bf16[72,16,1152]{2,1,0:T(8,128)(2,1)S(1)}) fusion(f32[16,1152]{1,0:T(8,128)S(1)} %get-tuple-element.70, f32[72,1152]{1,0:T(8,128)S(1)} %get-tuple-element.59, f32[16,1152]{1,0:T(8,128)S(1)} %get-tuple-element.71, f32[72,1152]{1,0:T(8,128)S(1)} %get-tuple-element.58), kind=kLoop, calls=%fused_computation.4 | loop fusion | flops 13271040 | bytes 6119424 | tf_op jit(solution)/shard_map/mul | solution.py:41
  15.8 3.3 %fusion.1 = (bf16[1152,1152]{1,0:T(8,128)(2,1)}, bf16[1152,1152]{1,0:T(8,128)(2,1)}) fusion(bf16[72,16,1152]{2,1,0:T(8,128)(2,1)S(1)} %get-tuple-element.37, pred[1152]{0:T(1024)(128)(4,1)S(1)} %iota_compare_fusion.8, bf16[72,16,1152]{2,1,0:T(8,128)(2,1)S(1)} %get-tuple-element.38), kind=kLoop, calls=%fused_computation.3 | loop fusion | flops 3981312 | bytes 10617984 | tf_op jit(solution)/shard_map/convert_element_type | solution.py:41
  19.1 0.8 all-to-all-done
  19.9 0.3 convert_reduce_fusion
  20.2 1.5 %slice_reduce_fusion.15 = (bf16[640]{0:T(1024)(128)(2,1)S(1)}, bf16[640]{0:T(1024)(128)(2,1)S(1)}, bf16[640]{0:T(1024)(128)(2,1)S(1)}, bf16[640]{0:T(1024)(128)(...) fusion(bf16[640,147]{1,0:T(8,128)(2,1)S(1)} %bitcast.59), kind=kLoop, calls=%fused_computation.109 | loop fusion | bytes 40960 | tf_op jit(solution)/shard_map/slice | solution.py:88
  21.8 0.2 copy.29
  21.9 1.2 %broadcast_in_dim.257 = bf16[8,129,640]{2,1,0:T(8,128)(2,1)} broadcast(bf16[129,640]{1,0:T(8,128)(2,1)S(1)} %copy.29), dimensions={1,2} | broadcast | bytes 1486080 | tf_op jit(solution)/shard_map/broadcast_in_dim | solution.py:112
  23.1 7.6 %all-to-all-start.1 = ((bf16[8,129,640]{2,1,0:T(8,128)(2,1)}), bf16[8,129,640]{2,1,0:T(8,128)(2,1)S(1)}, u32[]{:S(2)}, u32[]{:S(2)}) async-start(bf16[8,129,640]{2,1,0:T(8,128)(2,1)} %broadcast_in_dim.257), calls=%async_computation.1 | async-start | bytes 2785280 | tf_op jit(solution)/shard_map/all_to_all | solution.py:116
  30.7 0.1 broadcast_compare_fusion
  30.8 0.2 fusion.28
  31.1 0.5 fusion.29
  31.6 1.8 %broadcast_select_fusion.3 = bf16[256,2,640]{2,1,0:T(2,128)(2,1)S(1)} fusion(pred[2,640]{1,0:T(4,128)(4,1)S(1)} %get-tuple-element.63, pred[2,640]{1,0:T(4,128)(4,1)S(1)} %get-tuple-element.61, pred[2,640]{1,0:T(4,128)(4,1)S(1)} %get-tuple-element.62, pred[2,640]{1,0:T(4,128)(4,1)S(1)} %get-tuple-element.60, bf16[256,640]{1,0:T(8,128)(2,1)S(1)} %get-tuple-element.40, ...), kind=kLoop, calls=%fused_computation.25 | loop fusion | flops 1310720 | bytes 1971200 | tf_op jit(solution)/shard_map/jit(_where)/select_n | solution.py:91
  33.4 1.1 select_n.330
  34.5 1.3 %multiply_convert_fusion = (bf16[256,256]{1,0:T(8,128)(2,1)S(1)}, bf16[256,256]{1,0:T(8,128)(2,1)S(1)}) fusion(s32[256]{0:T(256)S(1)} %iota.144), kind=kLoop, calls=%fused_computation.87 | loop fusion | flops 1179648 | bytes 263168 | tf_op jit(solution)/shard_map/convert_element_type | solution.py:22
  35.8 2.2 %fusion.50 = (bf16[256,256]{1,0:T(8,128)(2,1)S(1)}, bf16[256,256]{1,0:T(8,128)(2,1)S(1)}) fusion(s32[256]{0:T(256)S(1)} %iota.144), kind=kLoop, calls=%fused_computation.110 | loop fusion | flops 2490368 | bytes 263168 | tf_op jit(solution)/shard_map/neg | solution.py:123
  38.0 0.1 reshape.925
  38.1 1.1 multiply_convert_fusion.3
  39.2 10.2 %all-to-all-done.1 = bf16[8,129,640]{2,1,0:T(8,128)(2,1)S(1)} async-done(((bf16[8,129,640]{2,1,0:T(8,128)(2,1)}), bf16[8,129,640]{2,1,0:T(8,128)(2,1)S(1)}, u32[]{:S(2)}, u32[]{:S(2)}) %all-to-all-start.1) | async-done | bytes 1320992 | tf_op jit(solution)/shard_map/all_to_all | solution.py:116
  49.4 1.5 %reshape.926 = bf16[1032,640]{1,0:T(8,128)(2,1)} reshape(bf16[8,129,640]{2,1,0:T(8,128)(2,1)S(1)} %all-to-all-done.1) | data formatting | bytes 2641920 | tf_op jit(solution)/shard_map/reshape | solution.py:117
  50.9 2.7 %convolution_convert_fusion.1 = bf16[512,1152]{1,0:T(8,128)(2,1)S(1)} fusion(bf16[512,640]{1,0:T(8,128)(2,1)} %select_n.330, bf16[1032,640]{1,0:T(8,128)(2,1)} %reshape.926), kind=kOutput, calls=%fused_computation.8 | convolution fusion | flops 755564544 | bytes 3155968 | tf_op jit(solution)/shard_map/dot_general | solution.py:93
  53.6 0.7 reshape.927
  54.3 0.0 copy-start.1
  54.3 0.8 convolution_convert_fusion
  55.1 0.9 copy-done.1
  56.0 0.0 copy-start
  56.0 3.5 %fusion.2 = f32[2,2,256,1152]{3,2,1,0:T(8,128)S(1)} fusion(bf16[2,2,256,1152]{3,2,1,0:T(8,128)(2,1)S(1)} %bitcast.62, bf16[1152,1152]{1,0:T(8,128)(2,1)S(1)} %copy-done.1), kind=kOutput, calls=%fused_computation.9 | convolution fusion | flops 2717908992 | bytes 9732096 | tf_op jit(solution)/shard_map/dot_general | solution.py:131
  59.5 0.0 copy-done
  59.5 3.5 %fusion.4 = f32[2,2,256,1152]{3,2,1,0:T(8,128)S(1)} fusion(bf16[2,2,256,1152]{3,2,1,0:T(8,128)(2,1)S(1)} %bitcast.63, bf16[1152,1152]{1,0:T(8,128)(2,1)S(1)} %copy-done), kind=kOutput, calls=%fused_computation.11 | convolution fusion | flops 2717908992 | bytes 9732096 | tf_op jit(solution)/shard_map/dot_general | solution.py:130
  63.1 0.3 fusion.12
  63.4 0.2 fusion.11
  63.6 0.2 maximum_bitcast_fusion
  63.9 2.4 %copy.34 = bf16[256,2,2,1152]{3,2,1,0:T(2,128)(2,1)S(1)} copy(bf16[256,2,2,1152]{3,0,1,2:T(8,128)(2,1)S(1)} %maximum_bitcast_fusion) | data formatting | bytes 4718592 | tf_op jit(solution)/shard_map/convert_element_type | solution.py:136
  66.3 2.3 %reshape.928 = bf16[128,8,1152]{2,1,0:T(8,128)(2,1)} reshape(bf16[256,2,2,1152]{3,2,1,0:T(2,128)(2,1)S(1)} %copy.34) | data formatting | bytes 4718592 | tf_op jit(solution)/shard_map/reshape | solution.py:136
  68.7 39.5 %all_to_all.15 = bf16[128,8,1152]{2,1,0:T(8,128)(2,1)S(1)} all-to-all(bf16[128,8,1152]{2,1,0:T(8,128)(2,1)} %reshape.928), channel_id=1, replica_groups=mesh['sky'=16,'gz'=8] {'sky','gz'}, dimensions={0} | all-to-all | bytes 4718592 | tf_op jit(solution)/shard_map/all_to_all | solution.py:137
  108.1 0.4 copy.35
  108.5 2.4 %copy.48 = bf16[128,2,2,2,1032]{0,4,2,3,1:T(8,128)(2,1)} copy(bf16[128,2,2,2,1032]{4,0,3,2,1:T(8,128)(2,1)S(1)} %bitcast.61) | data formatting | bytes 4227072
  110.9 4.9 %convolution_bitcast_fusion = f32[2,256,2,1032]{1,3,2,0:T(8,128)} fusion(bf16[128,2,2,2,1032]{0,4,2,3,1:T(8,128)(2,1)} %copy.48, bf16[2,128,2,2,256,1]{4,3,2,1,0,5:T(2,128)(2,1)S(1)} %bitcast.64), kind=kOutput, calls=%fused_computation.6 | convolution fusion | flops 1082130432 | bytes 6864896 | tf_op jit(solution)/shard_map/sqxRv,RsxUu->Uuqv/dot_general | solution.py:139
  (10 shorter events, 0.1 us)
Async XLA Ops:
  4.4 15.4 %all-to-all-start = ((bf16[16,40,147]{2,1,0:T(8,128)(2,1)}), bf16[16,40,147]{2,1,0:T(8,128)(2,1)S(1)}, u32[]{:S(2)}, u32[]{:S(2)}) async-start(bf16[16,40,147]{2,1,0:T(8,128)(2,1)} %bitcast.1), calls=%async_computation | async-start | bytes 655360 | tf_op jit(solution)/shard_map/all_to_all | solution.py:72
  23.1 26.2 %all-to-all-start.1 = ((bf16[8,129,640]{2,1,0:T(8,128)(2,1)}), bf16[8,129,640]{2,1,0:T(8,128)(2,1)S(1)}, u32[]{:S(2)}, u32[]{:S(2)}) async-start(bf16[8,129,640]{2,1,0:T(8,128)(2,1)} %broadcast_in_dim.257), calls=%async_computation.1 | async-start | bytes 2785280 | tf_op jit(solution)/shard_map/all_to_all | solution.py:116
  54.3 1.8 %copy-start.1 = (bf16[1152,1152]{1,0:T(8,128)(2,1)S(1)}, bf16[1152,1152]{1,0:T(8,128)(2,1)}, u32[]{:S(2)}) copy-start(bf16[1152,1152]{1,0:T(8,128)(2,1)} %get-tuple-element.18) | copy-start | bytes 7962628
  56.0 3.5 %copy-start = (bf16[1152,1152]{1,0:T(8,128)(2,1)S(1)}, bf16[1152,1152]{1,0:T(8,128)(2,1)}, u32[]{:S(2)}) copy-start(bf16[1152,1152]{1,0:T(8,128)(2,1)} %get-tuple-element.17) | copy-start | bytes 7962628

commit v9 on v8

--- a/solution.py
+++ b/solution.py
@@ -9,6 +9,12 @@
 NY = 256
 NW = 1032
 KSIDE = 4
+
+
+def passed_along(block, axis, distance):
+    devices = range(lax.axis_size(axis))
+    route = [((i - distance) % len(devices), i) for i in devices]
+    return lax.ppermute(block, axis, route)
 
 
 def dft_tables(length, steps=None):
@@ -109,11 +115,14 @@
     rows_dev = tile_rows // gz_count
     padded_nw = -(-NW // 128) * 128
     values_t = jnp.transpose(got[:, :slab_width])
-    copies = jnp.broadcast_to(values_t[None], (gz_count,) + values_t.shape)
     steps_y = jnp.arange(NY, dtype=jnp.int32)
     steps_x = jnp.arange(NX, dtype=jnp.int32)
-    copies, steps_y, steps_x = lax.optimization_barrier((copies, steps_y, steps_x))
-    values_t = lax.all_to_all(copies, "gz", split_axis=0, concat_axis=0, tiled=True)
+    values_t, steps_y, steps_x = lax.optimization_barrier((values_t, steps_y, steps_x))
+    held = [values_t] + [passed_along(values_t, "gz", d) for d in range(1, gz_count)]
+    held = jnp.stack(held[::-1])
+    start = (-(lax.axis_index("gz") + 1)) % gz_count
+    doubled = jnp.concatenate([held, held], axis=0)
+    values_t = lax.dynamic_slice_in_dim(doubled, start, gz_count, axis=0)
     values_t = jnp.pad(values_t.reshape(NW, -1), ((0, padded_nw - NW), (0, 0)))
     row_ids = lax.axis_index("gz") * rows_dev + jnp.arange(rows_dev, dtype=jnp.int32)
     cube_yw = grid_rows(got, values_t, slab_width, row_ids, capacity, block)

time: 116 us -> 134 us (1.16)
  blocking collectives: 39.5 us -> 46 us
  starting transfers between devices: 15.1 us -> 19.2 us
  local copies, waits for them, and re-layouts: 15.7 us -> 18.8 us
  other arithmetic: 17.8 us -> 20.7 us
  matrix products: 16.6 us -> 18.1 us
    ppermute x0 -> x7, starting transfers between devices: none -> 11.6 us  [passed_along(): return lax.ppermute(block, axis, route)]
    all_to_all x1 -> x0, waiting for transfers between devices: 10.2 us -> none  [shards(): lax.all_to_all(copies, 'gz', split_axis=0, concat_axis=0, tiled=True)]
    ppermute x0 -> x7, waiting for transfers between devices: none -> 9.15 us  [passed_along(): return lax.ppermute(block, axis, route)]
    all_to_all x1 -> x0, starting transfers between devices: 7.58 us -> none  [shards(): lax.all_to_all(copies, 'gz', split_axis=0, concat_axis=0, tiled=True)]
    all_to_all x1, blocking collectives: 39.5 us -> 46 us  [shards(): lax.all_to_all(second, ('sky', 'gz'), split_axis=0, concat_axis=0, tiled=...]
    dynamic_slice x0 -> x2, local copies, waits for them, and re-layouts: none -> 3 us  [shards(): values_t = lax.dynamic_slice_in_dim(doubled, start, gz_count, axis=0)]
    dot_general x1, matrix products: 3.51 us -> 5.4 us  [shards(): by_cos = jnp.dot(first, cos_w, preferred_element_type=jnp.float32)]
    concatenate x1, other arithmetic: 0.02 us -> 1.7 us  [shards(): table_y = jnp.concatenate([cos_y, -sin_y], axis=1)]
  transfers between devices with their start and end apart: 2 -> 8, of which waited for: 2 -> 3; matrix products, arithmetic and copies ran while one was open for 13% -> 16% of each run, Pallas kernels for 0% -> 0%
where the time goes in v9:
time: 134 us; the launch traced here: 133 us
  blocking collectives  46 us (34%)
  other arithmetic  20.7 us (15%)
  starting transfers between devices  19.2 us (14%)
  local copies, waits for them, and re-layouts  18.8 us (14%)
  matrix products  18.1 us (14%)
  waiting for transfers between devices  9.9 us (7%)
    all_to_all x1, blocking collectives, shards(): lax.all_to_all(second, ('sky', 'gz'), split_axis=0, concat_axis=0, tiled=...  46 us
    ppermute x7, starting transfers between devices, passed_along(): return lax.ppermute(block, axis, route)  11.6 us
    ppermute x7, waiting for transfers between devices, passed_along(): return lax.ppermute(block, axis, route)  9.15 us
    all_to_all x1, starting transfers between devices, route_fibres(): got = lax.all_to_all(send, 'sky', split_axis=0, concat_axis=0, tiled=True)  7.57 us
    dot_general x1, matrix products, shards(): by_cos = jnp.dot(first, cos_w, preferred_element_type=jnp.float32)  5.4 us
    dot_general x1, matrix products, shards(): jnp.einsum('sqxRv,RsxUu->Uuqv', pencils, table_x, preferred_element_type=...  4.87 us
    unnamed x20, local copies, waits for them, and re-layouts  4.74 us
    dot_general x1, matrix products, shards(): by_sin = jnp.dot(first, sin_w, preferred_element_type=jnp.float32)  3.5 us
  transfers between devices with their start and end apart: 8, of which 3 were waited for; matrix products, arithmetic and copies ran while one was open for 16% of the time, Pallas kernels for 0%

profile of v9, /device:TPU:1, one launch (start us, length us, event | category | flops | bytes accessed | tf_op | source)
XLA Modules:
  0.0 133.1 jit_solution(14317337472725375922)
XLA Ops:
  0.0 0.9 convert_reduce_fusion.2
  0.9 0.7 multiply_add_fusion
  1.6 0.7 fusion.79
  2.3 1.2 convolution_convert_fusion.2
  3.5 0.9 copy.28
  4.4 7.6 %all-to-all-start = ((bf16[16,40,147]{2,1,0:T(8,128)(2,1)}), bf16[16,40,147]{2,1,0:T(8,128)(2,1)S(1)}, u32[]{:S(2)}, u32[]{:S(2)}) async-start(bf16[16,40,147]{2,1,0:T(8,128)(2,1)} %bitcast.1), calls=%async_computation | async-start | bytes 655360 | tf_op jit(solution)/shard_map/all_to_all | solution.py:78
  12.0 0.3 fusion.62
  12.4 1.4 %fusion.38 = (f32[72,1152]{1,0:T(8,128)S(1)}, f32[72,1152]{1,0:T(8,128)S(1)}) fusion(s32[72]{0:T(128)S(1)} %iota_multiply_fusion), kind=kLoop, calls=%fused_computation.72 | loop fusion | flops 746496 | bytes 663840 | tf_op jit(solution)/shard_map/cos | solution.py:38
  13.8 2.1 %add_multiply_fusion = (bf16[72,16,1152]{2,1,0:T(8,128)(2,1)S(1)}, bf16[72,16,1152]{2,1,0:T(8,128)(2,1)S(1)}) fusion(f32[16,1152]{1,0:T(8,128)S(1)} %get-tuple-element.70, f32[72,1152]{1,0:T(8,128)S(1)} %get-tuple-element.59, f32[16,1152]{1,0:T(8,128)S(1)} %get-tuple-element.71, f32[72,1152]{1,0:T(8,128)S(1)} %get-tuple-element.58), kind=kLoop, calls=%fused_computation.4 | loop fusion | flops 13271040 | bytes 6119424 | tf_op jit(solution)/shard_map/mul | solution.py:47
  15.8 3.3 %fusion.1 = (bf16[1152,1152]{1,0:T(8,128)(2,1)}, bf16[1152,1152]{1,0:T(8,128)(2,1)}) fusion(bf16[72,16,1152]{2,1,0:T(8,128)(2,1)S(1)} %get-tuple-element.37, pred[1152]{0:T(1024)(128)(4,1)S(1)} %iota_compare_fusion.8, bf16[72,16,1152]{2,1,0:T(8,128)(2,1)S(1)} %get-tuple-element.38), kind=kLoop, calls=%fused_computation.3 | loop fusion | flops 3981312 | bytes 10617984 | tf_op jit(solution)/shard_map/convert_element_type | solution.py:47
  19.1 0.8 all-to-all-done
  19.9 2.3 %collective-permute-start = (bf16[129,640]{0,1:T(8,128)(2,1)S(1)}, bf16[129,640]{0,1:T(8,128)(2,1)S(1)}, u32[]{:S(2)}, u32[]{:S(2)}) collective-permute-start(bf16[129,640]{0,1:T(8,128)(2,1)S(1)} %slice_bitcast_fusion.2), channel_id=1, source_target_pairs={{1,0},{2,1},{3,2},{4,3},{5,4},{6,5},{7,6},{0,7},{9,8},{10,9},{11,1... | collective-permute-start | bytes 495368 | tf_op jit(solution)/shard_map/ppermute | solution.py:17
  22.2 3.8 %collective-permute-start.1 = (bf16[129,640]{0,1:T(8,128)(2,1)S(1)}, bf16[129,640]{0,1:T(8,128)(2,1)S(1)}, u32[]{:S(2)}, u32[]{:S(2)}) collective-permute-start(bf16[129,640]{0,1:T(8,128)(2,1)S(1)} %slice_bitcast_fusion.2), channel_id=1, source_target_pairs={{2,0},{3,1},{4,2},{5,3},{6,4},{7,5},{0,6},{1,7},{10,8},{11,9},{12,... | collective-permute-start | bytes 495368 | tf_op jit(solution)/shard_map/ppermute | solution.py:17
  26.0 0.4 collective-permute-start.2
  26.3 1.2 collective-permute-start.3
  27.5 2.0 %collective-permute-start.4 = (bf16[129,640]{0,1:T(8,128)(2,1)S(1)}, bf16[129,640]{0,1:T(8,128)(2,1)}, u32[]{:S(2)}, u32[]{:S(2)}) collective-permute-start(bf16[129,640]{0,1:T(8,128)(2,1)S(1)} %slice_bitcast_fusion.2), channel_id=1, source_target_pairs={{5,0},{6,1},{7,2},{0,3},{1,4},{2,5},{3,6},{4,7},{13,8},{14,9},{15,... | collective-permute-start | bytes 495368 | tf_op jit(solution)/shard_map/ppermute | solution.py:17
  29.5 0.3 convert_reduce_fusion
  29.8 1.5 %slice_reduce_fusion.15 = (bf16[640]{0:T(1024)(128)(2,1)S(1)}, bf16[640]{0:T(1024)(128)(2,1)S(1)}, bf16[640]{0:T(1024)(128)(2,1)S(1)}, bf16[640]{0:T(1024)(128)(...) fusion(bf16[640,147]{1,0:T(8,128)(2,1)S(1)} %bitcast.84), kind=kLoop, calls=%fused_computation.125 | loop fusion | bytes 40960 | tf_op jit(solution)/shard_map/slice | solution.py:94
  31.3 1.3 multiply_convert_fusion
  32.6 2.8 %fusion.50 = (bf16[256,256]{1,0:T(8,128)(2,1)}, bf16[256,256]{1,0:T(8,128)(2,1)S(1)}) fusion(s32[256]{0:T(256)S(1)} %iota.144), kind=kLoop, calls=%fused_computation.126 | loop fusion | flops 2490368 | bytes 263168 | tf_op jit(solution)/shard_map/neg | solution.py:132
  35.4 1.7 %multiply_convert_fusion.3 = bf16[256,256]{1,0:T(8,128)(2,1)} fusion(s32[256]{0:T(256)S(1)} %iota.144), kind=kLoop, calls=%fused_computation.106 | loop fusion | flops 1048576 | bytes 132096 | tf_op jit(solution)/shard_map/convert_element_type | solution.py:27
  37.1 0.1 broadcast_compare_fusion
  37.2 0.2 fusion.28
  37.5 0.5 fusion.29
  38.0 1.8 %broadcast_select_fusion.3 = bf16[256,2,640]{2,1,0:T(2,128)(2,1)S(1)} fusion(pred[2,640]{1,0:T(4,128)(4,1)S(1)} %get-tuple-element.63, pred[2,640]{1,0:T(4,128)(4,1)S(1)} %get-tuple-element.61, pred[2,640]{1,0:T(4,128)(4,1)S(1)} %get-tuple-element.62, pred[2,640]{1,0:T(4,128)(4,1)S(1)} %get-tuple-element.60, bf16[256,640]{1,0:T(8,128)(2,1)S(1)} %get-tuple-element.40, ...), kind=kLoop, calls=%fused_computation.25 | loop fusion | flops 1310720 | bytes 1971200 | tf_op jit(solution)/shard_map/jit(_where)/select_n | solution.py:97
  39.9 1.1 select_n.339
  40.9 0.1 reshape.924
  41.1 1.7 %pad_maximum_fusion = bf16[256,512]{1,0:T(8,128)(2,1)} fusion(bf16[256,256]{1,0:T(8,128)(2,1)} %get-tuple-element.68, bf16[256,256]{1,0:T(8,128)(2,1)} %multiply_convert_fusion.3), kind=kLoop, calls=%fused_computation.101 | loop fusion | flops 524288 | bytes 524288 | tf_op jit(solution)/shard_map/concatenate | solution.py:132
  42.8 0.0 collective-permute-done
  42.8 0.7 collective-permute-start.5
  43.5 0.0 collective-permute-done.1
  43.5 1.3 collective-permute-start.6
  44.9 8.0 %collective-permute-done.2 = bf16[129,640]{0,1:T(8,128)(2,1)S(1)} collective-permute-done((bf16[129,640]{0,1:T(8,128)(2,1)S(1)}, bf16[129,640]{0,1:T(8,128)(2,1)S(1)}, u32[]{:S(2)}, u32[]{:S(2)}) %collective-permute-start.2) | collective-permute-done | bytes 165152 | tf_op jit(solution)/shard_map/ppermute | solution.py:17
  52.9 0.0 collective-permute-done.3
  52.9 0.0 collective-permute-done.4
  52.9 1.0 bitcast_dynamic-update-slice_fusion.6
  53.9 0.0 collective-permute-done.5
  54.0 1.2 collective-permute-done.6
  55.3 1.0 bitcast_dynamic-update-slice_fusion.7
  56.4 0.2 constant_dynamic-slice_fusion
  56.6 2.8 %copy.29 = bf16[8,129,640]{2,1,0:T(8,128)(2,1)} copy(bf16[8,129,640]{1,2,0:T(8,128)(2,1)S(1)} %constant_dynamic-slice_fusion) | data formatting | bytes 2641920 | tf_op jit(solution)/shard_map/dynamic_slice | solution.py:125
  59.4 0.0 copy-start.1
  59.4 1.8 %reshape.925 = bf16[1032,640]{1,0:T(8,128)(2,1)S(1)} reshape(bf16[8,129,640]{2,1,0:T(8,128)(2,1)} %copy.29) | data formatting | bytes 2641920 | tf_op jit(solution)/shard_map/reshape | solution.py:126
  61.2 2.3 %convolution_convert_fusion.1 = bf16[512,1152]{1,0:T(8,128)(2,1)S(1)} fusion(bf16[512,640]{1,0:T(8,128)(2,1)} %select_n.339, bf16[1032,640]{1,0:T(8,128)(2,1)S(1)} %reshape.925), kind=kOutput, calls=%fused_computation.8 | convolution fusion | flops 755564544 | bytes 3155968 | tf_op jit(solution)/shard_map/dot_general | solution.py:99
  63.5 0.5 reshape.926
  64.0 0.0 copy-done.1
  64.0 0.8 convolution_convert_fusion
  64.8 0.0 copy-start
  64.8 5.4 %fusion.4 = f32[2,2,256,1152]{3,2,1,0:T(8,128)S(1)} fusion(bf16[2,2,256,1152]{3,2,1,0:T(8,128)(2,1)S(1)} %bitcast.86, bf16[1152,1152]{1,0:T(8,128)(2,1)} %get-tuple-element.17), kind=kOutput, calls=%fused_computation.11 | convolution fusion | flops 2717908992 | bytes 9732096 | tf_op jit(solution)/shard_map/dot_general | solution.py:139
  70.2 0.0 copy-done
  70.3 3.5 %fusion.2 = f32[2,2,256,1152]{3,2,1,0:T(8,128)S(1)} fusion(bf16[2,2,256,1152]{3,2,1,0:T(8,128)(2,1)S(1)} %bitcast.87, bf16[1152,1152]{1,0:T(8,128)(2,1)S(1)} %copy-done), kind=kOutput, calls=%fused_computation.9 | convolution fusion | flops 2717908992 | bytes 9732096 | tf_op jit(solution)/shard_map/dot_general | solution.py:140
  73.8 0.2 fusion.11
  74.0 0.3 fusion.12
  74.4 0.2 maximum_bitcast_fusion
  74.6 2.4 %copy.34 = bf16[256,2,2,1152]{3,2,1,0:T(2,128)(2,1)S(1)} copy(bf16[256,2,2,1152]{3,0,1,2:T(8,128)(2,1)S(1)} %maximum_bitcast_fusion) | data formatting | bytes 4718592 | tf_op jit(solution)/shard_map/convert_element_type | solution.py:145
  77.0 2.3 %reshape.927 = bf16[128,8,1152]{2,1,0:T(8,128)(2,1)} reshape(bf16[256,2,2,1152]{3,2,1,0:T(2,128)(2,1)S(1)} %copy.34) | data formatting | bytes 4718592 | tf_op jit(solution)/shard_map/reshape | solution.py:145
  79.4 46.0 %all_to_all.10 = bf16[128,8,1152]{2,1,0:T(8,128)(2,1)S(1)} all-to-all(bf16[128,8,1152]{2,1,0:T(8,128)(2,1)} %reshape.927), channel_id=1, replica_groups=mesh['sky'=16,'gz'=8] {'sky','gz'}, dimensions={0} | all-to-all | bytes 4718592 | tf_op jit(solution)/shard_map/all_to_all | solution.py:146
  125.4 0.4 copy.35
  125.7 2.4 %copy.48 = bf16[128,2,2,2,1032]{0,4,2,3,1:T(8,128)(2,1)} copy(bf16[128,2,2,2,1032]{4,0,3,2,1:T(8,128)(2,1)S(1)} %bitcast.85) | data formatting | bytes 4227072
  128.2 4.9 %convolution_bitcast_fusion = f32[2,256,2,1032]{1,3,2,0:T(8,128)} fusion(bf16[128,2,2,2,1032]{0,4,2,3,1:T(8,128)(2,1)} %copy.48, bf16[2,128,2,2,256,1]{4,3,2,1,0,5:T(2,128)(2,1)S(1)} %bitcast.88), kind=kOutput, calls=%fused_computation.6 | convolution fusion | flops 1082130432 | bytes 6864896 | tf_op jit(solution)/shard_map/sqxRv,RsxUu->Uuqv/dot_general | solution.py:148
  (23 shorter events, 0.4 us)
Async XLA Ops:
  4.4 15.4 %all-to-all-start = ((bf16[16,40,147]{2,1,0:T(8,128)(2,1)}), bf16[16,40,147]{2,1,0:T(8,128)(2,1)S(1)}, u32[]{:S(2)}, u32[]{:S(2)}) async-start(bf16[16,40,147]{2,1,0:T(8,128)(2,1)} %bitcast.1), calls=%async_computation | async-start | bytes 655360 | tf_op jit(solution)/shard_map/all_to_all | solution.py:78
  19.9 22.9 %collective-permute-start = (bf16[129,640]{0,1:T(8,128)(2,1)S(1)}, bf16[129,640]{0,1:T(8,128)(2,1)S(1)}, u32[]{:S(2)}, u32[]{:S(2)}) collective-permute-start(bf16[129,640]{0,1:T(8,128)(2,1)S(1)} %slice_bitcast_fusion.2), channel_id=1, source_target_pairs={{1,0},{2,1},{3,2},{4,3},{5,4},{6,5},{7,6},{0,7},{9,8},{10,9},{11,1... | collective-permute-start | bytes 495368 | tf_op jit(solution)/shard_map/ppermute | solution.py:17
  22.2 21.3 %collective-permute-start.1 = (bf16[129,640]{0,1:T(8,128)(2,1)S(1)}, bf16[129,640]{0,1:T(8,128)(2,1)S(1)}, u32[]{:S(2)}, u32[]{:S(2)}) collective-permute-start(bf16[129,640]{0,1:T(8,128)(2,1)S(1)} %slice_bitcast_fusion.2), channel_id=1, source_target_pairs={{2,0},{3,1},{4,2},{5,3},{6,4},{7,5},{0,6},{1,7},{10,8},{11,9},{12,... | collective-permute-start | bytes 495368 | tf_op jit(solution)/shard_map/ppermute | solution.py:17
  26.0 26.9 %collective-permute-start.2 = (bf16[129,640]{0,1:T(8,128)(2,1)S(1)}, bf16[129,640]{0,1:T(8,128)(2,1)S(1)}, u32[]{:S(2)}, u32[]{:S(2)}) collective-permute-start(bf16[129,640]{0,1:T(8,128)(2,1)S(1)} %slice_bitcast_fusion.2), channel_id=1, source_target_pairs={{3,0},{4,1},{5,2},{6,3},{7,4},{0,5},{1,6},{2,7},{11,8},{12,9},{13,... | collective-permute-start | bytes 495368 | tf_op jit(solution)/shard_map/ppermute | solution.py:17
  26.3 26.6 %collective-permute-start.3 = (bf16[129,640]{0,1:T(8,128)(2,1)S(1)}, bf16[129,640]{0,1:T(8,128)(2,1)S(1)}, u32[]{:S(2)}, u32[]{:S(2)}) collective-permute-start(bf16[129,640]{0,1:T(8,128)(2,1)S(1)} %slice_bitcast_fusion.2), channel_id=1, source_target_pairs={{4,0},{5,1},{6,2},{7,3},{0,4},{1,5},{2,6},{3,7},{12,8},{13,9},{14,... | collective-permute-start | bytes 495368 | tf_op jit(solution)/shard_map/ppermute | solution.py:17
  27.5 25.4 %collective-permute-start.4 = (bf16[129,640]{0,1:T(8,128)(2,1)S(1)}, bf16[129,640]{0,1:T(8,128)(2,1)}, u32[]{:S(2)}, u32[]{:S(2)}) collective-permute-start(bf16[129,640]{0,1:T(8,128)(2,1)S(1)} %slice_bitcast_fusion.2), channel_id=1, source_target_pairs={{5,0},{6,1},{7,2},{0,3},{1,4},{2,5},{3,6},{4,7},{13,8},{14,9},{15,... | collective-permute-start | bytes 495368 | tf_op jit(solution)/shard_map/ppermute | solution.py:17
  42.8 11.2 %collective-permute-start.5 = (bf16[129,640]{0,1:T(8,128)(2,1)S(1)}, bf16[129,640]{0,1:T(8,128)(2,1)S(1)}, u32[]{:S(2)}, u32[]{:S(2)}) collective-permute-start(bf16[129,640]{0,1:T(8,128)(2,1)S(1)} %slice_bitcast_fusion.2), channel_id=1, source_target_pairs={{6,0},{7,1},{0,2},{1,3},{2,4},{3,5},{4,6},{5,7},{14,8},{15,9},{8,1... | collective-permute-start | bytes 495368 | tf_op jit(solution)/shard_map/ppermute | solution.py:17
  43.5 11.6 %collective-permute-start.6 = (bf16[129,640]{0,1:T(8,128)(2,1)S(1)}, bf16[129,640]{0,1:T(8,128)(2,1)S(1)}, u32[]{:S(2)}, u32[]{:S(2)}) collective-permute-start(bf16[129,640]{0,1:T(8,128)(2,1)S(1)} %slice_bitcast_fusion.2), channel_id=1, source_target_pairs={{7,0},{0,1},{1,2},{2,3},{3,4},{4,5},{5,6},{6,7},{15,8},{8,9},{9,10... | collective-permute-start | bytes 495368 | tf_op jit(solution)/shard_map/ppermute | solution.py:17
  59.4 4.6 %copy-start.1 = (bf16[256,512]{1,0:T(8,128)(2,1)S(1)}, bf16[256,512]{1,0:T(8,128)(2,1)}, u32[]{:S(2)}) copy-start(bf16[256,512]{1,0:T(8,128)(2,1)} %pad_maximum_fusion) | copy-start | bytes 786436
  64.8 5.4 %copy-start = (bf16[1152,1152]{1,0:T(8,128)(2,1)S(1)}, bf16[1152,1152]{1,0:T(8,128)(2,1)}, u32[]{:S(2)}) copy-start(bf16[1152,1152]{1,0:T(8,128)(2,1)} %get-tuple-element.18) | copy-start | bytes 7962628
